TPU v7x, 32 devices: a whole 2x2x4 slice. The times are simulated.
32 devices in a mesh: lon: 8 (over z, y), lat: 4 (over x, core).
Axes of the slice: x: 2, y: 2, z: 4, core: 2. Of those that a mesh axis runs over, the one named last changes fastest.
Arguments:
- potential_warmth: float32 [25, 64, 2048], P(None, 'lat', 'lon'), may hold values from -6 to 6
- saltiness_anomaly: float32 [25, 64, 2048], P(None, 'lat', 'lon'), may hold values from -6 to 6
- zonal_speed: float32 [25, 64, 2048], P(None, 'lat', 'lon'), may hold values from -0.625 to 0.625
- meridional_speed: float32 [25, 64, 2048], P(None, 'lat', 'lon'), may hold values from -0.625 to 0.625
- sinking_speed: float32 [25, 64, 2048], P(None, 'lat', 'lon'), may hold values from -0.625 to 0.625
- water_indicator: int32 [64, 2048], P('lat', 'lon'), may hold values from 0 to 1, as said below
- seabed_layer_index: int32 [64, 2048], P('lat', 'lon'), may hold values from 1 to 25
Outputs:
- new_temperature: float32 [25, 64, 2048], P(None, 'lat', 'lon')
- new_salinity: float32 [25, 64, 2048], P(None, 'lat', 'lon')
Inputs may be any that keep to these rules, and one draw needn't show every extreme that they name: `water_indicator`: 1 marks a sea column, 0 a land column. `seabed_layer_index`: levels of a column counted from the top.
All inputs are finite; a program needn't handle non-finite values.
Results may differ from a plain program's by a relative error of at most 0.0003.
Values sent between devices are 32-bit elements; how exact they have to be, the bound alone decides.
No kernel may reach another device: no remote copies, remote signals or barrier semaphores. Data moves between devices by JAX's collectives and lax.ppermute only.
A program may use at most 64 MiB of HBM per device.

v0:
```python
import jax
import jax.numpy as jnp
from jax import lax
from jax.sharding import PartitionSpec as P

DIFFUSIVITY = 0.15
DENSITY_FLOOR = 0.5
SLOPE_LIMIT = 1.0
THERMAL = 0.25
HALINE = 0.75


def extended_2(cells, sides, width, closed):
    for axis, dim in sides:
        count = lax.axis_size(axis)
        ends = count if closed else count - 1
        head = lax.slice_in_dim(cells, 0, width, axis=dim)
        tail = lax.slice_in_dim(cells, cells.shape[dim] - width, cells.shape[dim], axis=dim)
        cells = jnp.concatenate(
            [
                lax.ppermute(tail, axis, [(i, (i + 1) % count) for i in range(ends)]),
                cells,
                lax.ppermute(head, axis, [((i + 1) % count, i) for i in range(ends)]),
            ],
            axis=dim,
        )
    return cells


def tracer_step(extended, sinking_speed):
    layer_total = sinking_speed.shape[0]
    temp_ext = extended[:layer_total]
    salt_ext = extended[layer_total : 2 * layer_total]
    depth_ext = extended[2 * layer_total]
    east_ext = extended[2 * layer_total + 1 : 3 * layer_total + 1]
    north_ext = extended[3 * layer_total + 1 :]
    level_index = jnp.arange(layer_total).astype(depth_ext.dtype)[:, None, None]
    wet_cells = jnp.where(level_index < depth_ext[None], 1.0, 0.0).astype(depth_ext.dtype)
    east_face = wet_cells[:, 1:-1, :-1] * wet_cells[:, 1:-1, 1:]
    north_face = wet_cells[:, :-1, 1:-1] * wet_cells[:, 1:, 1:-1]
    upper_full = wet_cells[1:] * wet_cells[:-1]
    upper_face = upper_full[:, 1:-1, 1:-1]

    def gradients(values):
        grad_east = (values[:, 1:-1, 1:] - values[:, 1:-1, :-1]) * east_face
        grad_north = (values[:, 1:, 1:-1] - values[:, :-1, 1:-1]) * north_face
        grad_down = (values[1:] - values[:-1]) * upper_full
        zero_plane = jnp.zeros_like(grad_down[:1])
        vert_cell = 0.5 * (
            jnp.concatenate([zero_plane, grad_down], 0)
            + jnp.concatenate([grad_down, zero_plane], 0)
        )
        vert_east = 0.5 * (vert_cell[:, 1:-1, :-1] + vert_cell[:, 1:-1, 1:])
        vert_north = 0.5 * (vert_cell[:, :-1, 1:-1] + vert_cell[:, 1:, 1:-1])
        east_cell = 0.5 * (grad_east[:, :, :-1] + grad_east[:, :, 1:])
        north_cell = 0.5 * (grad_north[:, :-1] + grad_north[:, 1:])
        east_upper = 0.5 * (east_cell[:-1] + east_cell[1:])
        north_upper = 0.5 * (north_cell[:-1] + north_cell[1:])
        return (
            grad_east,
            grad_north,
            grad_down[:, 1:-1, 1:-1],
            vert_east,
            vert_north,
            east_upper,
            north_upper,
        )

    density = HALINE * salt_ext - THERMAL * temp_ext
    (
        rho_east,
        rho_north,
        rho_down,
        rho_vert_east,
        rho_vert_north,
        rho_east_upper,
        rho_north_upper,
    ) = gradients(density)
    slope_east = jnp.clip(
        -rho_east / jnp.maximum(rho_vert_east, DENSITY_FLOOR), -SLOPE_LIMIT, SLOPE_LIMIT
    )
    slope_north = jnp.clip(
        -rho_north / jnp.maximum(rho_vert_north, DENSITY_FLOOR), -SLOPE_LIMIT, SLOPE_LIMIT
    )
    slope_x = jnp.clip(
        -rho_east_upper / jnp.maximum(rho_down, DENSITY_FLOOR), -SLOPE_LIMIT, SLOPE_LIMIT
    )
    slope_y = jnp.clip(
        -rho_north_upper / jnp.maximum(rho_down, DENSITY_FLOOR), -SLOPE_LIMIT, SLOPE_LIMIT
    )
    flow_east = 0.5 * (east_ext[:, 1:-1, :-1] + east_ext[:, 1:-1, 1:]) * east_face
    flow_north = 0.5 * (north_ext[:, :-1, 1:-1] + north_ext[:, 1:, 1:-1]) * north_face
    flow_down = 0.5 * (sinking_speed[:-1] + sinking_speed[1:]) * upper_face

    def advance(values):
        grad_east, grad_north, grad_down, vert_east, vert_north, east_upper, north_upper = (
            gradients(values)
        )
        own_cells = values[:, 1:-1, 1:-1]
        flux_east = (
            jnp.maximum(flow_east, 0.0) * values[:, 1:-1, :-1]
            + jnp.minimum(flow_east, 0.0) * values[:, 1:-1, 1:]
            - DIFFUSIVITY * east_face * (grad_east + slope_east * vert_east)
        )
        flux_north = (
            jnp.maximum(flow_north, 0.0) * values[:, :-1, 1:-1]
            + jnp.minimum(flow_north, 0.0) * values[:, 1:, 1:-1]
            - DIFFUSIVITY * north_face * (grad_north + slope_north * vert_north)
        )
        flux_down = (
            jnp.maximum(flow_down, 0.0) * own_cells[:-1]
            + jnp.minimum(flow_down, 0.0) * own_cells[1:]
            - DIFFUSIVITY
            * upper_face
            * (
                slope_x * east_upper
                + slope_y * north_upper
                + (slope_x * slope_x + slope_y * slope_y) * grad_down
            )
        )
        zero_plane = jnp.zeros_like(flux_down[:1])
        divergence = (
            flux_east[:, :, 1:] - flux_east[:, :, :-1] + (flux_north[:, 1:] - flux_north[:, :-1])
        )
        divergence = divergence + (
            jnp.concatenate([flux_down, zero_plane], 0)
            - jnp.concatenate([zero_plane, flux_down], 0)
        )
        return own_cells - divergence

    return (advance(temp_ext), advance(salt_ext))


def framed(centre, west_cols, east_cols, south_rows, north_rows):
    middle = jnp.concatenate([west_cols, centre, east_cols], 2)
    lower_rows = jnp.pad(south_rows, ((0, 0), (0, 0), (1, 1)))
    upper_rows = jnp.pad(north_rows, ((0, 0), (0, 0), (1, 1)))
    return jnp.concatenate([lower_rows, middle, upper_rows], 1)


def on_device(
    potential_warmth,
    saltiness_anomaly,
    zonal_speed,
    meridional_speed,
    sinking_speed,
    water_indicator,
    seabed_layer_index,
):
    layer_total = potential_warmth.shape[0]
    shard_meridional_extent = potential_warmth.shape[1]
    shard_zonal_extent = potential_warmth.shape[2]
    base_planes = 2 * layer_total + 1
    strata_total = (water_indicator * seabed_layer_index).astype(jnp.float32)[None]
    scalar_field_strata = jnp.concatenate([potential_warmth, saltiness_anomaly, strata_total], 0)
    lat_index = lax.axis_index("lat")
    top_row = lat_index == lax.axis_size("lat") - 1
    lon_halo = extended_2(
        jnp.concatenate([scalar_field_strata, zonal_speed], 0), (("lon", 2),), 1, True
    )
    lat_halo = extended_2(
        jnp.concatenate([scalar_field_strata, meridional_speed], 0), (("lat", 1),), 1, False
    )
    col_zeros = jnp.zeros((layer_total, shard_meridional_extent, 1), jnp.float32)
    row_zeros = jnp.zeros((layer_total, 1, shard_zonal_extent), jnp.float32)
    west_cols = jnp.concatenate([lon_halo[:, :, :1], col_zeros], 0)
    east_cols = jnp.concatenate([lon_halo[:, :, -1:], col_zeros], 0)
    south_rows = jnp.concatenate(
        [lat_halo[:base_planes, :1], row_zeros, lat_halo[base_planes:, :1]], 0
    )
    north_rows = jnp.concatenate(
        [lat_halo[:base_planes, -1:], row_zeros, lat_halo[base_planes:, -1:]], 0
    )
    centre = jnp.concatenate([scalar_field_strata, zonal_speed, meridional_speed], 0)
    extended = framed(centre, west_cols, east_cols, south_rows, north_rows)
    own_top = jnp.concatenate([scalar_field_strata, meridional_speed], 0)[:, -1, :]
    lon_count = lax.axis_size("lon")
    flat_top = own_top.reshape(-1)
    entry_count = flat_top.shape[0]
    piece_length = (entry_count + lon_count - 1) // lon_count
    pieces = flat_top.reshape(lon_count, piece_length)
    spread_pieces = lax.all_to_all(pieces, "lon", split_axis=0, concat_axis=0, tiled=True)
    collected = lax.all_to_all(spread_pieces[::-1], "lon", split_axis=0, concat_axis=0, tiled=True)
    facing = collected.reshape(-1).reshape(own_top.shape)
    mirrored = facing[:, ::-1]
    ghost_row = jnp.concatenate(
        [
            mirrored[:base_planes],
            extended[base_planes : base_planes + layer_total, -1, 1:-1],
            -mirrored[base_planes:],
        ],
        0,
    )
    extended = extended.at[:, -1, 1:-1].set(jnp.where(top_row, ghost_row, extended[:, -1, 1:-1]))
    return tracer_step(extended, sinking_speed)


def solution(mesh):
    placed = (
        P(None, "lat", "lon"),
        P(None, "lat", "lon"),
        P(None, "lat", "lon"),
        P(None, "lat", "lon"),
        P(None, "lat", "lon"),
        P("lat", "lon"),
        P("lat", "lon"),
    )
    return jax.shard_map(
        on_device,
        mesh=mesh,
        in_specs=placed,
        out_specs=(P(None, "lat", "lon"), P(None, "lat", "lon")),
        check_vma=False,
    )
```

profile of v0, /device:TPU:2, one launch (start us, length us, event | category | flops | bytes accessed | tf_op | source)
XLA Modules:
  0.0 87.2 jit_solution(4478272802423744062)
XLA Ops:
  0.7 1.3 %copy.18 = f32[25,16,256]{2,0,1:T(8,128)S(1)} copy(f32[25,16,256]{2,1,0:T(8,128)} %param.9) | data formatting | bytes 819200 | tf_op args[0]
  2.0 1.9 %constant_dynamic-update-slice_fusion.3 = f32[101,16,256]{2,1,0:T(8,128)} fusion(f32[25,16,256]{2,1,0:T(8,128)} %param.9), kind=kLoop, calls=%fused_computation.156 | loop fusion | bytes 819200
  3.8 1.2 %copy.20 = f32[25,16,256]{2,0,1:T(8,128)S(1)} copy(f32[25,16,256]{2,1,0:T(8,128)} %param.12) | data formatting | bytes 819200 | tf_op args[3]
  5.1 1.2 %copy.19 = f32[25,16,256]{2,0,1:T(8,128)S(1)} copy(f32[25,16,256]{2,1,0:T(8,128)} %param.10) | data formatting | bytes 819200 | tf_op args[1]
  8.4 2.0 %collective-permute-start = (f32[76,1,256]{2,0,1:T(8,128)S(1)}, f32[76,1,256]{2,0,1:T(8,128)}, u32[]{:S(2)}, u32[]{:S(2)}) collective-permute-start(f32[76,1,256]{2,0,1:T(8,128)S(1)} %get-tuple-element.34), channel_id=1, source_target_pairs={{0,1},{1,2},{2,3},{4,5},{5,6},{6,7},{8,9},{9,10},{10,11},{12,13},{... | collective-permute-start | bytes 233480 | tf_op jit(solution)/shard_map/ppermute | solution.py:21
  11.2 5.8 %all-to-all-start = ((f32[8,1,2432]{2,1,0:T(1,128)}), f32[8,1,2432]{2,1,0:T(1,128)S(1)}, u32[]{:S(2)}, u32[]{:S(2)}) async-start(f32[8,1,2432]{2,1,0:T(1,128)} %all_to_all.19), calls=%async_computation | async-start | bytes 155648 | tf_op jit(solution)/shard_map/all_to_all | solution.py:182
  17.0 3.4 %collective-permute-start.3 = (f32[76,1,256]{2,0,1:T(8,128)}, f32[76,1,256]{2,0,1:T(8,128)}, u32[]{:S(2)}, u32[]{:S(2)}) collective-permute-start(f32[76,1,256]{2,0,1:T(8,128)} %get-tuple-element.35), channel_id=1, source_target_pairs={{1,0},{2,1},{3,2},{5,4},{6,5},{7,6},{9,8},{10,9},{11,10},{13,12},{... | collective-permute-start | bytes 233480 | tf_op jit(solution)/shard_map/ppermute | solution.py:23
  20.4 1.2 %copy.23 = f32[1,16,256]{0,1,2:T(8,128)S(1)} copy(f32[1,16,256]{2,0,1:T(1,128)S(1)} %broadcast_in_dim.16) | data formatting | bytes 32768 | tf_op jit(solution)/shard_map/broadcast_in_dim | solution.py:154
  21.6 2.6 %copy.21 = f32[25,16,256]{0,1,2:T(8,128)} copy(f32[25,16,256]{2,1,0:T(8,128)S(1)} %copy-done.2) | data formatting | bytes 819200 | tf_op args[0]
  24.2 2.6 %copy.22 = f32[25,16,256]{0,1,2:T(8,128)} copy(f32[25,16,256]{2,1,0:T(8,128)S(1)} %copy-done.3) | data formatting | bytes 819200 | tf_op args[1]
  26.7 2.6 %copy.24 = f32[25,16,256]{0,1,2:T(8,128)} copy(f32[25,16,256]{2,1,0:T(8,128)S(1)} %copy-done.4) | data formatting | bytes 819200 | tf_op args[2]
  30.2 1.8 %collective-permute-start.1 = (f32[76,16,1]{0,1,2:T(8,128)S(1)}, f32[76,16,1]{0,1,2:T(8,128)S(1)}, u32[]{:S(2)}, u32[]{:S(2)}) collective-permute-start(f32[76,16,1]{0,1,2:T(8,128)S(1)} %get-tuple-element.30), channel_id=1, source_target_pairs={{0,4},{4,8},{8,12},{12,16},{16,20},{20,24},{24,28},{28,0},{1,5},{5... | collective-permute-start | bytes 14600 | tf_op jit(solution)/shard_map/ppermute | solution.py:21
  32.0 3.0 %collective-permute-start.2 = (f32[76,16,1]{0,1,2:T(8,128)S(1)}, f32[76,16,1]{0,1,2:T(8,128)S(1)}, u32[]{:S(2)}, u32[]{:S(2)}) collective-permute-start(f32[76,16,1]{0,1,2:T(8,128)S(1)} %get-tuple-element.31), channel_id=1, source_target_pairs={{4,0},{8,4},{12,8},{16,12},{20,16},{24,20},{28,24},{0,28},{5,1},{9... | collective-permute-start | bytes 14600 | tf_op jit(solution)/shard_map/ppermute | solution.py:23
  36.8 3.4 %all-to-all-start.1 = ((f32[8,1,2432]{2,1,0:T(1,128)}), f32[8,1,2432]{2,1,0:T(1,128)S(1)}, u32[]{:S(2)}, u32[]{:S(2)}) async-start(f32[8,1,2432]{2,1,0:T(1,128)} %copy.31), calls=%async_computation.1 | async-start | bytes 155648 | tf_op jit(solution)/shard_map/all_to_all | solution.py:183
  45.1 2.0 %all-to-all-done.1 = f32[8,1,2432]{2,1,0:T(1,128)S(1)} async-done(((f32[8,1,2432]{2,1,0:T(1,128)}), f32[8,1,2432]{2,1,0:T(1,128)S(1)}, u32[]{:S(2)}, u32[]{:S(2)}) %all-to-all-start.1) | async-done | bytes 77856 | tf_op jit(solution)/shard_map/all_to_all | solution.py:183
  48.1 4.7 %select_maximum_fusion = f32[101,18,258]{2,1,0:T(8,128)} fusion(f32[101,1,256]{2,1,0:T(1,128)S(1)} %copy.37, f32[76,16,1]{2,1,0:T(8,128)S(1)} %copy.36, f32[76,16,1]{2,1,0:T(8,128)S(1)} %copy.35, f32[101,1,256]{2,1,0:T(1,128)S(1)} %copy.34, f32[101,16,256]{2,1,0:T(8,128)} %constant_dynamic-update-slice_fusion), kind=kLoop, calls=%fused_computation.2 | loop fusion | flops 8911836 | bytes 3747536 | tf_op jit(solution)/shard_map/concatenate | solution.py:138
  52.8 20.2 %scatter.4 = f32[101,18,258]{2,1,0:T(8,128)} dynamic-update-slice(f32[101,18,258]{2,1,0:T(8,128)} %select_maximum_fusion, f32[101,1,256]{2,1,0:T(1,128)S(1)} %copy.32, s32[]{:T(128)} %constant.60.clone.1, s32[]{:T(128)} %constant.61.clone.1, s32[]{:T(128)} %constant.62.clone.1) | dynamic-update-slice | bytes 206852 | tf_op jit(solution)/shard_map/scatter | solution.py:194
  73.0 0.9 %slice_bitcast_fusion = f32[18,258]{1,0:T(8,128)S(1)} fusion(f32[101,18,258]{2,1,0:T(8,128)} %scatter.4), kind=kLoop, calls=%fused_computation.149 | loop fusion | bytes 37152 | tf_op jit(solution)/shard_map/lt | solution.py:38
  73.9 1.8 %fusion.4 = f32[25,18,258]{2,1,0:T(8,128)S(1)} fusion(f32[101,18,258]{2,1,0:T(8,128)} %scatter.4), kind=kLoop, calls=%fused_computation.14 | loop fusion | flops 348300 | bytes 1393200 | tf_op jit(solution)/shard_map/sub | solution.py:69
  76.4 2.1 %fusion.12 = (f32[25,17,256]{2,1,0:T(8,128)S(1)}, f32[25,17,256]{2,1,0:T(8,128)S(1)}, f32[25,17,256]{2,1,0:T(8,128)S(1)}, f32[25,17,256]{2,1,0:T(8,128)S(1)}) fusion(f32[25,18,258]{2,1,0:T(8,128)S(1)} %add_multiply_fusion, f32[101,18,258]{2,1,0:T(8,128)S(1)} %copy-done, f32[25,18,258]{2,1,0:T(8,128)S(1)} %get-tuple-element.42, f32[25,18,258]{2,1,0:T(8,128)S(1)} %fusion.4, ...), kind=kLoop, calls=%fused_computation.32 | loop fusion | flops 2828800 | bytes 6963200 | tf_op jit(solution)/shard_map/sub | solution.py:106
  78.5 1.6 %fusion.17 = (f32[25,16,257]{2,1,0:T(8,128)S(1)}, f32[25,16,257]{2,1,0:T(8,128)S(1)}, f32[25,16,257]{2,1,0:T(8,128)S(1)}, f32[25,16,257]{2,1,0:T(8,128)S(1)}) fusion(f32[25,18,258]{2,1,0:T(8,128)S(1)} %add_multiply_fusion, f32[101,18,258]{2,1,0:T(8,128)S(1)} %copy-done, f32[25,18,258]{2,1,0:T(8,128)S(1)} %get-tuple-element.42, f32[25,18,258]{2,1,0:T(8,128)S(1)} %fusion.4, ...), kind=kLoop, calls=%fused_computation.38 | loop fusion | flops 2672800 | bytes 6579200 | tf_op jit(solution)/shard_map/sub | solution.py:101
  80.4 1.5 %fusion.22 = (f32[25,17,256]{2,1,0:T(8,128)S(1)}, f32[25,17,256]{2,1,0:T(8,128)S(1)}) fusion(f32[25,18,258]{2,1,0:T(8,128)S(1)} %get-tuple-element.41, f32[101,18,258]{2,1,0:T(8,128)S(1)} %copy-done, f32[25,17,256]{2,1,0:T(8,128)S(1)} %get-tuple-element.21, f32[25,18,258]{2,1,0:T(8,128)S(1)} %get-tuple-element.42, f32[25,17,256]{2,1,0:T(8,128)S(1)} %get-tuple-element.20), kind=kLoop, calls=%fused_computation.44 | loop fusion | flops 2502400 | bytes 5222400 | tf_op jit(solution)/shard_map/sub | solution.py:106
  81.9 1.2 %fusion.34 = (f32[25,16,257]{2,1,0:T(8,128)S(1)}, f32[25,16,257]{2,1,0:T(8,128)S(1)}) fusion(f32[25,18,258]{2,1,0:T(8,128)S(1)} %get-tuple-element.41, f32[101,18,258]{2,1,0:T(8,128)S(1)} %copy-done, f32[25,16,257]{2,1,0:T(8,128)S(1)} %get-tuple-element.17, f32[25,18,258]{2,1,0:T(8,128)S(1)} %get-tuple-element.42, f32[25,16,257]{2,1,0:T(8,128)S(1)} %get-tuple-element.16), kind=kLoop, calls=%fused_computation.61 | loop fusion | flops 2364400 | bytes 4934400 | tf_op jit(solution)/shard_map/sub | solution.py:101
  85.7 1.5 %fusion.46 = (f32[25,16,256]{2,1,0:T(8,128)}, f32[25,16,256]{2,1,0:T(8,128)}) fusion(f32[25,17,256]{2,1,0:T(8,128)S(1)} %get-tuple-element.18, f32[25,16,257]{2,1,0:T(8,128)S(1)} %get-tuple-element.14, f32[101,18,258]{2,1,0:T(8,128)S(1)} %copy-done, f32[24,16,256]{2,1,0:T(8,128)S(1)} %fusion.56, f32[24,16,256]{2,1,0:T(8,128)S(1)} %fusion.65, ...), kind=kLoop, calls=%fused_computation.84 | loop fusion | flops 1228800 | bytes 5701632 | tf_op jit(solution)/shard_map/sub | solution.py:129
  (65 shorter events, 14.7 us)
Async XLA Ops:
  0.6 5.7 %copy-start.3 = (f32[25,16,256]{2,1,0:T(8,128)S(1)}, f32[25,16,256]{2,1,0:T(8,128)}, u32[]{:S(2)}) copy-start(f32[25,16,256]{2,1,0:T(8,128)} %param.10) | copy-start | bytes 1228804
  0.6 6.5 %copy-start.7 = (s32[16,256]{1,0:T(8,128)S(1)}, s32[16,256]{1,0:T(8,128)}, u32[]{:S(2)}) copy-start(s32[16,256]{1,0:T(8,128)} %param.15) | copy-start | bytes 49156
  0.7 6.5 %copy-start.6 = (s32[16,256]{1,0:T(8,128)S(1)}, s32[16,256]{1,0:T(8,128)}, u32[]{:S(2)}) copy-start(s32[16,256]{1,0:T(8,128)} %param.14) | copy-start | bytes 49156
  2.0 19.6 %copy-start.2 = (f32[25,16,256]{2,1,0:T(8,128)S(1)}, f32[25,16,256]{2,1,0:T(8,128)}, u32[]{:S(2)}) copy-start(f32[25,16,256]{2,1,0:T(8,128)} %param.9) | copy-start | bytes 1228804
  8.4 18.3 %copy-start.4 = (f32[25,16,256]{2,1,0:T(8,128)S(1)}, f32[25,16,256]{2,1,0:T(8,128)}, u32[]{:S(2)}) copy-start(f32[25,16,256]{2,1,0:T(8,128)} %param.11) | copy-start | bytes 1228804
  8.4 35.1 %collective-permute-start = (f32[76,1,256]{2,0,1:T(8,128)S(1)}, f32[76,1,256]{2,0,1:T(8,128)}, u32[]{:S(2)}, u32[]{:S(2)}) collective-permute-start(f32[76,1,256]{2,0,1:T(8,128)S(1)} %get-tuple-element.34), channel_id=1, source_target_pairs={{0,1},{1,2},{2,3},{4,5},{5,6},{6,7},{8,9},{9,10},{10,11},{12,13},{... | collective-permute-start | bytes 233480 | tf_op jit(solution)/shard_map/ppermute | solution.py:21
  11.2 24.6 %all-to-all-start = ((f32[8,1,2432]{2,1,0:T(1,128)}), f32[8,1,2432]{2,1,0:T(1,128)S(1)}, u32[]{:S(2)}, u32[]{:S(2)}) async-start(f32[8,1,2432]{2,1,0:T(1,128)} %all_to_all.19), calls=%async_computation | async-start | bytes 155648 | tf_op jit(solution)/shard_map/all_to_all | solution.py:182
  17.0 24.9 %collective-permute-start.3 = (f32[76,1,256]{2,0,1:T(8,128)}, f32[76,1,256]{2,0,1:T(8,128)}, u32[]{:S(2)}, u32[]{:S(2)}) collective-permute-start(f32[76,1,256]{2,0,1:T(8,128)} %get-tuple-element.35), channel_id=1, source_target_pairs={{1,0},{2,1},{3,2},{5,4},{6,5},{7,6},{9,8},{10,9},{11,10},{13,12},{... | collective-permute-start | bytes 233480 | tf_op jit(solution)/shard_map/ppermute | solution.py:23
  29.3 10.9 %copy-start.5 = (f32[25,16,256]{2,1,0:T(8,128)S(1)}, f32[25,16,256]{2,1,0:T(8,128)}, u32[]{:S(2)}) copy-start(f32[25,16,256]{2,1,0:T(8,128)} %param.12) | copy-start | bytes 1228804
  30.2 11.2 %collective-permute-start.1 = (f32[76,16,1]{0,1,2:T(8,128)S(1)}, f32[76,16,1]{0,1,2:T(8,128)S(1)}, u32[]{:S(2)}, u32[]{:S(2)}) collective-permute-start(f32[76,16,1]{0,1,2:T(8,128)S(1)} %get-tuple-element.30), channel_id=1, source_target_pairs={{0,4},{4,8},{8,12},{12,16},{16,20},{20,24},{24,28},{28,0},{1,5},{5... | collective-permute-start | bytes 14600 | tf_op jit(solution)/shard_map/ppermute | solution.py:21
  32.0 9.1 %collective-permute-start.2 = (f32[76,16,1]{0,1,2:T(8,128)S(1)}, f32[76,16,1]{0,1,2:T(8,128)S(1)}, u32[]{:S(2)}, u32[]{:S(2)}) collective-permute-start(f32[76,16,1]{0,1,2:T(8,128)S(1)} %get-tuple-element.31), channel_id=1, source_target_pairs={{4,0},{8,4},{12,8},{16,12},{20,16},{24,20},{28,24},{0,28},{5,1},{9... | collective-permute-start | bytes 14600 | tf_op jit(solution)/shard_map/ppermute | solution.py:23
  36.8 10.3 %all-to-all-start.1 = ((f32[8,1,2432]{2,1,0:T(1,128)}), f32[8,1,2432]{2,1,0:T(1,128)S(1)}, u32[]{:S(2)}, u32[]{:S(2)}) async-start(f32[8,1,2432]{2,1,0:T(1,128)} %copy.31), calls=%async_computation.1 | async-start | bytes 155648 | tf_op jit(solution)/shard_map/all_to_all | solution.py:183
  73.0 2.8 %copy-start = (f32[101,18,258]{2,1,0:T(8,128)S(1)}, f32[101,18,258]{2,1,0:T(8,128)}, u32[]{:S(2)}) copy-start(f32[101,18,258]{2,1,0:T(8,128)} %scatter.4) | copy-start | bytes 5628532
  83.1 1.0 %copy-start.1 = (f32[25,16,256]{2,1,0:T(8,128)S(1)}, f32[25,16,256]{2,1,0:T(8,128)}, u32[]{:S(2)}) copy-start(f32[25,16,256]{2,1,0:T(8,128)} %param.13) | copy-start | bytes 1228804
where the time goes:
time: 88.5 us; the launch traced here: 87.2 us
  local copies, waits for them, and re-layouts  45 us (51%)
  other arithmetic  19.8 us (22%)
  starting transfers between devices  19.4 us (22%)
  waiting for transfers between devices  2.06 us (2%)
  between operations  0.96 us (1%)
    scatter x1, local copies, waits for them, and re-layouts, on_device(): extended.at[:, -1, 1:-1]  20.2 us
    unnamed x30, local copies, waits for them, and re-layouts  16.5 us
    ppermute x2, starting transfers between devices, extended_2(): lax.ppermute(head, axis, [((i + 1) % count, i) for i in range(ends)])  6.33 us
    all_to_all x1, starting transfers between devices, on_device(): lax.all_to_all(pieces, 'lon', split_axis=0, concat_axis=0, tiled=True)  5.83 us
    concatenate x1, other arithmetic, framed(): return jnp.concatenate([lower_rows, middle, upper_rows], 1)  4.7 us
    ppermute x2, starting transfers between devices, extended_2(): lax.ppermute(tail, axis, [(i, (i + 1) % count) for i in range(ends)])  3.83 us
    sub x2, other arithmetic, advance(): jnp.maximum(flow_north, 0.0) * values[:, :-1, 1:-1]  3.59 us
    all_to_all x1, starting transfers between devices, on_device(): lax.all_to_all(spread_pieces[::-1], 'lon', split_axis=0, concat_axis=0, t...  3.36 us
  transfers between devices with their start and end apart: 6, of which 1 were waited for; matrix products, arithmetic and copies ran while one was open for 19% of the time, Pallas kernels for 0%

commit v1 on v0

--- a/solution.py
+++ b/solution.py
@@ -148,50 +148,39 @@
     seabed_layer_index,
 ):
     layer_total = potential_warmth.shape[0]
-    shard_meridional_extent = potential_warmth.shape[1]
-    shard_zonal_extent = potential_warmth.shape[2]
     base_planes = 2 * layer_total + 1
     strata_total = (water_indicator * seabed_layer_index).astype(jnp.float32)[None]
     scalar_field_strata = jnp.concatenate([potential_warmth, saltiness_anomaly, strata_total], 0)
-    lat_index = lax.axis_index("lat")
-    top_row = lat_index == lax.axis_size("lat") - 1
-    lon_halo = extended_2(
-        jnp.concatenate([scalar_field_strata, zonal_speed], 0), (("lon", 2),), 1, True
-    )
-    lat_halo = extended_2(
-        jnp.concatenate([scalar_field_strata, meridional_speed], 0), (("lat", 1),), 1, False
-    )
-    col_zeros = jnp.zeros((layer_total, shard_meridional_extent, 1), jnp.float32)
-    row_zeros = jnp.zeros((layer_total, 1, shard_zonal_extent), jnp.float32)
-    west_cols = jnp.concatenate([lon_halo[:, :, :1], col_zeros], 0)
-    east_cols = jnp.concatenate([lon_halo[:, :, -1:], col_zeros], 0)
-    south_rows = jnp.concatenate(
-        [lat_halo[:base_planes, :1], row_zeros, lat_halo[base_planes:, :1]], 0
-    )
-    north_rows = jnp.concatenate(
-        [lat_halo[:base_planes, -1:], row_zeros, lat_halo[base_planes:, -1:]], 0
-    )
+    lon_count = lax.axis_size("lon")
+    lat_count = lax.axis_size("lat")
+    top_row = lax.axis_index("lat") == lat_count - 1
+    lon_fields = jnp.concatenate([scalar_field_strata, zonal_speed], 0)
+    west_cols = lax.ppermute(
+        lon_fields[:, :, -1:], "lon", [(i, (i + 1) % lon_count) for i in range(lon_count)]
+    )
+    east_cols = lax.ppermute(
+        lon_fields[:, :, :1], "lon", [((i + 1) % lon_count, i) for i in range(lon_count)]
+    )
+    lat_fields = jnp.concatenate([scalar_field_strata, meridional_speed], 0)
+    south_rows = lax.ppermute(
+        lat_fields[:, -1:, :], "lat", [(i, i + 1) for i in range(lat_count - 1)]
+    )
+    north_rows = lax.ppermute(
+        lat_fields[:, :1, :], "lat", [(i + 1, i) for i in range(lat_count - 1)]
+    )
+    facing = lax.ppermute(
+        lat_fields[:, -1:, :], "lon", [(i, lon_count - 1 - i) for i in range(lon_count)]
+    )[:, :, ::-1]
+    ghost_row = jnp.concatenate([facing[:base_planes], -facing[base_planes:]], 0)
+    north_rows = jnp.where(top_row, ghost_row, north_rows)
+    col_zeros = jnp.zeros((layer_total,) + west_cols.shape[1:], jnp.float32)
+    row_zeros = jnp.zeros((layer_total,) + south_rows.shape[1:], jnp.float32)
+    west_cols = jnp.concatenate([west_cols, col_zeros], 0)
+    east_cols = jnp.concatenate([east_cols, col_zeros], 0)
+    south_rows = jnp.concatenate([south_rows[:base_planes], row_zeros, south_rows[base_planes:]], 0)
+    north_rows = jnp.concatenate([north_rows[:base_planes], row_zeros, north_rows[base_planes:]], 0)
     centre = jnp.concatenate([scalar_field_strata, zonal_speed, meridional_speed], 0)
     extended = framed(centre, west_cols, east_cols, south_rows, north_rows)
-    own_top = jnp.concatenate([scalar_field_strata, meridional_speed], 0)[:, -1, :]
-    lon_count = lax.axis_size("lon")
-    flat_top = own_top.reshape(-1)
-    entry_count = flat_top.shape[0]
-    piece_length = (entry_count + lon_count - 1) // lon_count
-    pieces = flat_top.reshape(lon_count, piece_length)
-    spread_pieces = lax.all_to_all(pieces, "lon", split_axis=0, concat_axis=0, tiled=True)
-    collected = lax.all_to_all(spread_pieces[::-1], "lon", split_axis=0, concat_axis=0, tiled=True)
-    facing = collected.reshape(-1).reshape(own_top.shape)
-    mirrored = facing[:, ::-1]
-    ghost_row = jnp.concatenate(
-        [
-            mirrored[:base_planes],
-            extended[base_planes : base_planes + layer_total, -1, 1:-1],
-            -mirrored[base_planes:],
-        ],
-        0,
-    )
-    extended = extended.at[:, -1, 1:-1].set(jnp.where(top_row, ghost_row, extended[:, -1, 1:-1]))
     return tracer_step(extended, sinking_speed)
 
 

time: 88.5 us -> 52.4 us (0.59)
  local copies, waits for them, and re-layouts: 45 us -> 19.9 us
  starting transfers between devices: 19.4 us -> 12 us
  other arithmetic: 19.8 us -> 15 us
  waiting for transfers between devices: 2.06 us -> 4.02 us
    scatter x1 -> x0, local copies, waits for them, and re-layouts: 20.2 us -> none  [on_device(): extended.at[:, -1, 1:-1]]
    all_to_all x2 -> x0, starting transfers between devices: 9.19 us -> none  [the longest x1 5.83 us: on_device(): lax.all_to_all(pieces, 'lon', split_axis=0, concat_axis=0, tiled=True)]
    ppermute x4 -> x5, waiting for transfers between devices: 0.01 us -> 4.02 us  [the longest x1 2.55 us: on_device(): lax.ppermute(lon_fields[:, :, -1:], 'lon', [(i, (i + 1) % lon_count) for...]
    concatenate x1, other arithmetic: 4.7 us -> 1.62 us  [framed(): return jnp.concatenate([lower_rows, middle, upper_rows], 1)]
    slice x8, local copies, waits for them, and re-layouts: 3.51 us -> 1.17 us  [the longest x2 0.99 us: on_device(): facing[:base_planes]]
    unnamed x30 -> x33, local copies, waits for them, and re-layouts: 16.5 us -> 14.3 us
    all_to_all x2 -> x0, waiting for transfers between devices: 2.05 us -> none  [the longest x1 2.05 us: on_device(): lax.all_to_all(spread_pieces[::-1], 'lon', split_axis=0, concat_axis=0, t...]
    ppermute x4 -> x5, starting transfers between devices: 10.2 us -> 12 us  [the longest x1 4.62 us: on_device(): lax.ppermute(lat_fields[:, -1:, :], 'lon', [(i, lon_count - 1 - i) for i...]
  transfers between devices with their start and end apart: 6 -> 5, of which waited for: 1 -> 2; matrix products, arithmetic and copies ran while one was open for 19% -> 31% of each run, Pallas kernels for 0% -> 0%
where the time goes in v1:
time: 52.4 us; the launch traced here: 51.9 us
  local copies, waits for them, and re-layouts  19.9 us (38%)
  other arithmetic  15 us (29%)
  starting transfers between devices  12 us (23%)
  waiting for transfers between devices  4.02 us (8%)
  between operations  1.03 us (2%)
    unnamed x33, local copies, waits for them, and re-layouts  14.3 us
    ppermute x1, starting transfers between devices, on_device(): lax.ppermute(lat_fields[:, -1:, :], 'lon', [(i, lon_count - 1 - i) for i...  4.62 us
    ppermute x1, starting transfers between devices, on_device(): lax.ppermute(lat_fields[:, :1, :], 'lat', [(i + 1, i) for i in range(lat_...  3.35 us
    ppermute x1, waiting for transfers between devices, on_device(): lax.ppermute(lon_fields[:, :, -1:], 'lon', [(i, (i + 1) % lon_count) for...  2.55 us
    broadcast_in_dim x2, local copies, waits for them, and re-layouts, on_device(): (water_indicator * seabed_layer_index).astype(jnp.float32)[None]  2.37 us
    sub x2, other arithmetic, advance(): jnp.maximum(flow_north, 0.0) * values[:, :-1, 1:-1]  2.36 us
    sub x2, other arithmetic, advance(): jnp.maximum(flow_east, 0.0) * values[:, 1:-1, :-1]  2.16 us
    sub x2, other arithmetic, advance(): return own_cells - divergence  1.95 us
  transfers between devices with their start and end apart: 5, of which 2 were waited for; matrix products, arithmetic and copies ran while one was open for 31% of the time, Pallas kernels for 0%

profile of v1, /device:TPU:2, one launch (start us, length us, event | category | flops | bytes accessed | tf_op | source)
XLA Modules:
  0.0 51.9 jit_solution(16595469680740688336)
XLA Ops:
  0.7 1.1 %constant_dynamic-update-slice_fusion.4 = f32[101,16,256]{2,1,0:T(8,128)S(1)} fusion(f32[25,16,256]{2,1,0:T(8,128)} %param.7), kind=kLoop, calls=%fused_computation.148 | loop fusion | bytes 819200
  1.8 1.3 %copy.33 = f32[25,16,256]{2,0,1:T(8,128)S(1)} copy(f32[25,16,256]{2,1,0:T(8,128)} %param.7) | data formatting | bytes 819200 | tf_op args[0]
  4.3 1.9 %collective-permute-start.2 = (f32[76,1,256]{2,0,1:T(8,128)}, f32[76,1,256]{2,0,1:T(8,128)S(1)}, u32[]{:S(2)}, u32[]{:S(2)}) collective-permute-start(f32[76,1,256]{2,0,1:T(8,128)} %get-tuple-element.31), channel_id=1, source_target_pairs={{0,1},{1,2},{2,3},{4,5},{5,6},{6,7},{8,9},{9,10},{10,11},{12,13},{... | collective-permute-start | bytes 233480 | tf_op jit(solution)/shard_map/ppermute | solution.py:165
  6.3 4.6 %collective-permute-start.3 = (f32[76,1,256]{2,0,1:T(8,128)}, f32[76,1,256]{2,0,1:T(8,128)S(1)}, u32[]{:S(2)}, u32[]{:S(2)}) collective-permute-start(f32[76,1,256]{2,0,1:T(8,128)} %get-tuple-element.31), channel_id=1, source_target_pairs={{0,28},{4,24},{8,20},{12,16},{16,12},{20,8},{24,4},{28,0},{1,29},{... | collective-permute-start | bytes 233480 | tf_op jit(solution)/shard_map/ppermute | solution.py:171
  10.9 3.4 %collective-permute-start.4 = (f32[76,1,256]{2,0,1:T(8,128)}, f32[76,1,256]{2,0,1:T(8,128)}, u32[]{:S(2)}, u32[]{:S(2)}) collective-permute-start(f32[76,1,256]{2,0,1:T(8,128)} %get-tuple-element.32), channel_id=1, source_target_pairs={{1,0},{2,1},{3,2},{5,4},{6,5},{7,6},{9,8},{10,9},{11,10},{13,12},{... | collective-permute-start | bytes 233480 | tf_op jit(solution)/shard_map/ppermute | solution.py:168
  14.2 2.4 %copy.29 = f32[1,16,256]{0,1,2:T(8,128)} copy(f32[1,16,256]{2,1,0:T(8,128)S(1)} %get-tuple-element.25) | data formatting | bytes 32768 | tf_op jit(solution)/shard_map/broadcast_in_dim | solution.py:152
  16.6 2.6 %copy.28 = f32[25,16,256]{0,1,2:T(8,128)} copy(f32[25,16,256]{2,1,0:T(8,128)S(1)} %copy-done.2) | data formatting | bytes 819200 | tf_op args[1]
  19.2 2.6 %copy.27 = f32[25,16,256]{0,1,2:T(8,128)} copy(f32[25,16,256]{2,1,0:T(8,128)S(1)} %copy-done) | data formatting | bytes 819200 | tf_op args[0]
  21.9 2.6 %copy.30 = f32[25,16,256]{0,1,2:T(8,128)} copy(f32[25,16,256]{2,1,0:T(8,128)S(1)} %copy-done.5) | data formatting | bytes 819200 | tf_op args[2]
  24.4 0.9 %pad_maximum_fusion.22 = (f32[76,16,1]{0,1,2:T(8,128)S(1)}, f32[76,16,1]{0,1,2:T(8,128)S(1)}) fusion(f32[25,16,256]{0,1,2:T(8,128)} %copy.30, f32[1,16,256]{0,1,2:T(8,128)} %copy.29, f32[25,16,256]{0,1,2:T(8,128)} %copy.28, f32[25,16,256]{0,1,2:T(8,128)} %copy.27), kind=kLoop, calls=%fused_computation.152 | loop fusion | flops 7296 | bytes 1254912 | tf_op jit(solution)/shard_map/slice | solution.py:159
  25.7 1.7 %collective-permute-start = (f32[76,16,1]{0,1,2:T(8,128)S(1)}, f32[76,16,1]{0,1,2:T(8,128)S(1)}, u32[]{:S(2)}, u32[]{:S(2)}) collective-permute-start(f32[76,16,1]{0,1,2:T(8,128)S(1)} %get-tuple-element.26), channel_id=1, source_target_pairs={{0,4},{4,8},{8,12},{12,16},{16,20},{20,24},{24,28},{28,0},{1,5},{5... | collective-permute-start | bytes 14600 | tf_op jit(solution)/shard_map/ppermute | solution.py:158
  27.6 1.5 %collective-permute-done.1 = f32[76,16,1]{0,1,2:T(8,128)S(1)} collective-permute-done((f32[76,16,1]{0,1,2:T(8,128)S(1)}, f32[76,16,1]{0,1,2:T(8,128)S(1)}, u32[]{:S(2)}, u32[]{:S(2)}) %collective-permute-start.1) | collective-permute-done | bytes 4896 | tf_op jit(solution)/shard_map/ppermute | solution.py:161
  29.5 2.6 %collective-permute-done = f32[76,16,1]{0,1,2:T(8,128)S(1)} collective-permute-done((f32[76,16,1]{0,1,2:T(8,128)S(1)}, f32[76,16,1]{0,1,2:T(8,128)S(1)}, u32[]{:S(2)}, u32[]{:S(2)}) %collective-permute-start) | collective-permute-done | bytes 4896 | tf_op jit(solution)/shard_map/ppermute | solution.py:158
  32.0 1.2 %copy.43 = f32[76,16,1]{2,1,0:T(8,128)} copy(f32[76,16,1]{0,1,2:T(8,128)S(1)} %collective-permute-done) | data formatting | bytes 9728
  33.2 1.1 %concatenate.85.clone = f32[101,16,1]{2,1,0:T(8,128)S(1)} pad(f32[76,16,1]{2,1,0:T(8,128)} %copy.43, f32[]{:T(128)} %constant.9.clone.1), padding=0_25x0_0x0_0 | pad | bytes 11332 | tf_op jit(solution)/shard_map/concatenate | solution.py:178
  35.1 0.8 %slice.453 = f32[51,1,256]{2,0,1:T(8,128)S(1)} slice(f32[76,1,256]{2,0,1:T(8,128)} %copy-done.7), slice={[0:51], [0:1], [0:256]} | slice | bytes 104448 | tf_op jit(solution)/shard_map/slice | solution.py:174
  36.1 0.9 %maximum_select_fusion = f32[76,1,256]{2,0,1:T(8,128)S(1)} fusion(f32[76,1,256]{2,0,1:T(8,128)} %collective-permute-done.4, f32[25,1,256]{2,0,1:T(8,128)S(1)} %neg.15, f32[51,1,256]{2,0,1:T(8,128)S(1)} %slice.362, pred[]{:T(512)S(6)} %eq.3), kind=kLoop, calls=%fused_computation.141 | loop fusion | flops 38912 | bytes 233473 | tf_op jit(solution)/shard_map/jit(_where)/select_n | solution.py:175
  38.2 1.6 %pad_maximum_fusion = f32[101,18,258]{2,1,0:T(8,128)S(1)} fusion(f32[101,1,258]{2,1,0:T(1,128)S(1)} %pad.20.clone, f32[101,16,1]{2,1,0:T(8,128)S(1)} %concatenate.88.clone, f32[101,16,256]{2,1,0:T(8,128)S(1)} %constant_dynamic-update-slice_fusion, f32[101,16,1]{2,1,0:T(8,128)S(1)} %concatenate.85.clone, f32[101,1,258]{2,1,0:T(1,128)S(1)} %pad.19.clone), kind=kLoop, calls=%fused_computation | loop fusion | flops 1876176 | bytes 3752352 | tf_op jit(solution)/shard_map/concatenate | solution.py:138
  42.3 1.4 %fusion.13 = (f32[25,16,257]{2,1,0:T(8,128)S(1)}, f32[25,16,257]{2,1,0:T(8,128)S(1)}, f32[25,16,257]{2,1,0:T(8,128)S(1)}, f32[25,16,257]{2,1,0:T(8,128)S(1)}, f3...) fusion(f32[25,18,258]{2,1,0:T(8,128)S(1)} %add_multiply_fusion, f32[25,16,257]{2,1,0:T(8,128)S(1)} %get-tuple-element.4, ...), kind=kLoop, calls=%fused_computation.32 | loop fusion | flops 3186800 | bytes 7835712 | tf_op jit(solution)/shard_map/sub | solution.py:101
  44.0 1.5 %fusion.8 = (f32[25,17,256]{2,1,0:T(8,128)S(1)}, f32[25,17,256]{2,1,0:T(8,128)S(1)}, f32[25,17,256]{2,1,0:T(8,128)S(1)}) fusion(f32[25,18,258]{2,1,0:T(8,128)S(1)} %add_multiply_fusion, f32[25,17,256]{2,1,0:T(8,128)S(1)} %get-tuple-element.8, f32[25,17,256]{2,1,0:T(8,128)S(1)} %get-tuple-element.7, f32[25,17,256]{2,1,0:T(8,128)S(1)} %get-tuple-element.9, ...), kind=kLoop, calls=%fused_computation.20 | loop fusion | flops 3372800 | bytes 7098576 | tf_op jit(solution)/shard_map/sub | solution.py:106
  48.3 0.9 %fusion.18 = f32[25,17,256]{2,1,0:T(8,128)S(1)} fusion(f32[25,18,258]{2,1,0:T(8,128)S(1)} %get-tuple-element.37, f32[25,17,256]{2,1,0:T(8,128)S(1)} %get-tuple-element.23, f32[25,17,256]{2,1,0:T(8,128)S(1)} %get-tuple-element.22, f32[25,17,256]{2,1,0:T(8,128)S(1)} %get-tuple-element.9, f32[25,17,256]{2,1,0:T(8,128)S(1)} %get-tuple-element.15, ...), kind=kLoop, calls=%fused_computation.40 | loop fusion | flops 2176000 | bytes 4352000 | tf_op jit(solution)/shard_map/sub | solution.py:106
  49.2 0.8 %fusion.30 = f32[25,16,257]{2,1,0:T(8,128)S(1)} fusion(f32[25,18,258]{2,1,0:T(8,128)S(1)} %get-tuple-element.37, f32[25,16,257]{2,1,0:T(8,128)S(1)} %get-tuple-element.30, f32[25,16,257]{2,1,0:T(8,128)S(1)} %get-tuple-element.29, f32[25,16,257]{2,1,0:T(8,128)S(1)} %get-tuple-element.5, f32[25,16,257]{2,1,0:T(8,128)S(1)} %get-tuple-element.12, ...), kind=kLoop, calls=%fused_computation.59 | loop fusion | flops 2056000 | bytes 4112000 | tf_op jit(solution)/shard_map/sub | solution.py:101
  50.0 1.0 %fusion.49 = f32[25,16,256]{2,1,0:T(8,128)} fusion(f32[25,16,256]{2,1,0:T(8,128)S(1)} %copy-done.1, f32[25,17,256]{2,1,0:T(8,128)S(1)} %fusion.18, f32[25,16,257]{2,1,0:T(8,128)S(1)} %fusion.30, f32[24,16,256]{2,1,0:T(8,128)S(1)} %fusion.60), kind=kLoop, calls=%fused_computation.97 | loop fusion | flops 614400 | bytes 2850816 | tf_op jit(solution)/shard_map/sub | solution.py:129
  51.0 1.0 %fusion.42 = f32[25,16,256]{2,1,0:T(8,128)} fusion(f32[25,16,256]{2,1,0:T(8,128)S(1)} %copy-done.3, f32[25,17,256]{2,1,0:T(8,128)S(1)} %get-tuple-element.13, f32[25,16,257]{2,1,0:T(8,128)S(1)} %get-tuple-element.10, f32[24,16,256]{2,1,0:T(8,128)S(1)} %fusion.52), kind=kLoop, calls=%fused_computation.84 | loop fusion | flops 614400 | bytes 2850816 | tf_op jit(solution)/shard_map/sub | solution.py:129
  (67 shorter events, 9.7 us)
Async XLA Ops:
  0.6 2.4 %copy-start.6 = (f32[25,16,256]{2,1,0:T(8,128)S(1)}, f32[25,16,256]{2,1,0:T(8,128)}, u32[]{:S(2)}) copy-start(f32[25,16,256]{2,1,0:T(8,128)} %param.10) | copy-start | bytes 1228804
  0.6 2.7 %copy-start.2 = (f32[25,16,256]{2,1,0:T(8,128)S(1)}, f32[25,16,256]{2,1,0:T(8,128)}, u32[]{:S(2)}) copy-start(f32[25,16,256]{2,1,0:T(8,128)} %param.8) | copy-start | bytes 1228804
  1.8 1.8 %copy-start.8 = (s32[16,256]{1,0:T(8,128)S(1)}, s32[16,256]{1,0:T(8,128)}, u32[]{:S(2)}) copy-start(s32[16,256]{1,0:T(8,128)} %param.12) | copy-start | bytes 49156
  1.8 1.8 %copy-start.9 = (s32[16,256]{1,0:T(8,128)S(1)}, s32[16,256]{1,0:T(8,128)}, u32[]{:S(2)}) copy-start(s32[16,256]{1,0:T(8,128)} %param.13) | copy-start | bytes 49156
  4.3 32.7 %collective-permute-start.2 = (f32[76,1,256]{2,0,1:T(8,128)}, f32[76,1,256]{2,0,1:T(8,128)S(1)}, u32[]{:S(2)}, u32[]{:S(2)}) collective-permute-start(f32[76,1,256]{2,0,1:T(8,128)} %get-tuple-element.31), channel_id=1, source_target_pairs={{0,1},{1,2},{2,3},{4,5},{5,6},{6,7},{8,9},{9,10},{10,11},{12,13},{... | collective-permute-start | bytes 233480 | tf_op jit(solution)/shard_map/ppermute | solution.py:165
  6.3 28.1 %collective-permute-start.3 = (f32[76,1,256]{2,0,1:T(8,128)}, f32[76,1,256]{2,0,1:T(8,128)S(1)}, u32[]{:S(2)}, u32[]{:S(2)}) collective-permute-start(f32[76,1,256]{2,0,1:T(8,128)} %get-tuple-element.31), channel_id=1, source_target_pairs={{0,28},{4,24},{8,20},{12,16},{16,12},{20,8},{24,4},{28,0},{1,29},{... | collective-permute-start | bytes 233480 | tf_op jit(solution)/shard_map/ppermute | solution.py:171
  10.9 25.3 %collective-permute-start.4 = (f32[76,1,256]{2,0,1:T(8,128)}, f32[76,1,256]{2,0,1:T(8,128)}, u32[]{:S(2)}, u32[]{:S(2)}) collective-permute-start(f32[76,1,256]{2,0,1:T(8,128)} %get-tuple-element.32), channel_id=1, source_target_pairs={{1,0},{2,1},{3,2},{5,4},{6,5},{7,6},{9,8},{10,9},{11,10},{13,12},{... | collective-permute-start | bytes 233480 | tf_op jit(solution)/shard_map/ppermute | solution.py:168
  16.6 2.6 %copy-start = (f32[25,16,256]{2,1,0:T(8,128)S(1)}, f32[25,16,256]{2,1,0:T(8,128)}, u32[]{:S(2)}) copy-start(f32[25,16,256]{2,1,0:T(8,128)} %param.7) | copy-start | bytes 1228804
  19.2 2.6 %copy-start.5 = (f32[25,16,256]{2,1,0:T(8,128)S(1)}, f32[25,16,256]{2,1,0:T(8,128)}, u32[]{:S(2)}) copy-start(f32[25,16,256]{2,1,0:T(8,128)} %param.9) | copy-start | bytes 1228804
  25.3 3.7 %collective-permute-start.1 = (f32[76,16,1]{0,1,2:T(8,128)S(1)}, f32[76,16,1]{0,1,2:T(8,128)S(1)}, u32[]{:S(2)}, u32[]{:S(2)}) collective-permute-start(f32[76,16,1]{0,1,2:T(8,128)S(1)} %get-tuple-element.27), channel_id=1, source_target_pairs={{4,0},{8,4},{12,8},{16,12},{20,16},{24,20},{28,24},{0,28},{5,1},{9... | collective-permute-start | bytes 14600 | tf_op jit(solution)/shard_map/ppermute | solution.py:161
  25.7 6.3 %collective-permute-start = (f32[76,16,1]{0,1,2:T(8,128)S(1)}, f32[76,16,1]{0,1,2:T(8,128)S(1)}, u32[]{:S(2)}, u32[]{:S(2)}) collective-permute-start(f32[76,16,1]{0,1,2:T(8,128)S(1)} %get-tuple-element.26), channel_id=1, source_target_pairs={{0,4},{4,8},{8,12},{12,16},{16,20},{20,24},{24,28},{28,0},{1,5},{5... | collective-permute-start | bytes 14600 | tf_op jit(solution)/shard_map/ppermute | solution.py:158
  34.4 0.6 %copy-start.7 = (f32[76,1,256]{2,0,1:T(8,128)}, f32[76,1,256]{2,0,1:T(8,128)S(1)}, u32[]{:S(2)}) copy-start(f32[76,1,256]{2,0,1:T(8,128)S(1)} %collective-permute-done.3) | copy-start | bytes 233476
  45.5 1.0 %copy-start.1 = (f32[25,16,256]{2,1,0:T(8,128)S(1)}, f32[25,16,256]{2,1,0:T(8,128)}, u32[]{:S(2)}) copy-start(f32[25,16,256]{2,1,0:T(8,128)} %param.7) | copy-start | bytes 1228804
  45.5 1.1 %copy-start.4 = (f32[25,16,256]{2,1,0:T(8,128)S(1)}, f32[25,16,256]{2,1,0:T(8,128)}, u32[]{:S(2)}) copy-start(f32[25,16,256]{2,1,0:T(8,128)} %param.11) | copy-start | bytes 1228804
  46.6 1.0 %copy-start.3 = (f32[25,16,256]{2,1,0:T(8,128)S(1)}, f32[25,16,256]{2,1,0:T(8,128)}, u32[]{:S(2)}) copy-start(f32[25,16,256]{2,1,0:T(8,128)} %param.8) | copy-start | bytes 1228804

commit v2 on v1

v2 whole, which is shorter than its diff:
```python
import jax
import jax.numpy as jnp
from jax import lax
from jax.experimental import pallas as pl
from jax.experimental.pallas import tpu as pltpu
from jax.sharding import PartitionSpec as P

DIFFUSIVITY = 0.15
DENSITY_FLOOR = 0.5
SLOPE_LIMIT = 1.0
THERMAL = 0.25
HALINE = 0.75


def stencil_kernel(
    t_ref, s_ref, u_ref, v_ref, w_ref, d_ref, hw_ref, he_ref, hs_ref, hn_ref,
    ot_ref, os_ref, tsh, ssh, ush, vsh, dsh,
):
    layer_total, rows, cols = t_ref.shape
    lane = lax.broadcasted_iota(jnp.int32, (rows, cols), 1)
    row = lax.broadcasted_iota(jnp.int32, (rows, cols), 0)
    east_edge = lane == cols - 1
    west_edge = lane == 0
    north_edge = row == rows - 1
    south_edge = row == 0

    def east_of(x, h):
        return jnp.where(east_edge, h, pltpu.roll(x, cols - 1, 1))

    def west_of(x, h):
        return jnp.where(west_edge, h, pltpu.roll(x, 1, 1))

    def north_of(x, h):
        return jnp.where(north_edge, h, pltpu.roll(x, rows - 1, 0))

    def south_of(x, h):
        return jnp.where(south_edge, h, pltpu.roll(x, 1, 0))

    depth_plane = 2 * layer_total
    depth = d_ref[...]
    dsh[0] = depth
    dsh[1] = east_of(depth, he_ref[depth_plane])
    dsh[2] = west_of(depth, hw_ref[depth_plane])
    dsh[3] = north_of(depth, hn_ref[depth_plane])
    dsh[4] = south_of(depth, hs_ref[depth_plane])

    def prepare(k, carry):
        for src, dst, base in ((t_ref, tsh, 0), (s_ref, ssh, layer_total)):
            x = src[k]
            dst[0, k] = east_of(x, he_ref[base + k])
            dst[1, k] = west_of(x, hw_ref[base + k])
            dst[2, k] = north_of(x, hn_ref[base + k])
            dst[3, k] = south_of(x, hs_ref[base + k])
        x = u_ref[k]
        ush[0, k] = east_of(x, he_ref[depth_plane + 1 + k])
        ush[1, k] = west_of(x, hw_ref[depth_plane + 1 + k])
        x = v_ref[k]
        vsh[0, k] = north_of(x, hn_ref[depth_plane + 1 + k])
        vsh[1, k] = south_of(x, hs_ref[depth_plane + 1 + k])
        return carry

    lax.fori_loop(0, layer_total, prepare, 0)

    def planes(k):
        at = jnp.clip(k, 0, layer_total - 1)
        temp = [t_ref[at]] + [tsh[i, at] for i in range(4)]
        salt = [s_ref[at]] + [ssh[i, at] for i in range(4)]
        rho = [HALINE * sv - THERMAL * tv for tv, sv in zip(temp, salt)]
        return temp, salt, rho

    def wet_at(k):
        inside = jnp.logical_and(k >= 0, k < layer_total)
        level = k.astype(jnp.float32)
        return [
            jnp.where(jnp.logical_and(inside, level < dsh[i]), 1.0, 0.0) for i in range(5)
        ]

    def horizontal(fields, kcs, wet, a, b, speed_a, speed_b, slope_of):
        face = wet[a] * wet[b]
        temp, salt, rho = fields
        k_temp, k_salt, k_rho = kcs
        slope = jnp.clip(
            -((rho[b] - rho[a]) * face)
            / jnp.maximum(0.5 * (k_rho[a] + k_rho[b]), DENSITY_FLOOR),
            -SLOPE_LIMIT,
            SLOPE_LIMIT,
        )
        flow = 0.5 * (speed_a + speed_b) * face
        up, down = jnp.maximum(flow, 0.0), jnp.minimum(flow, 0.0)
        out = []
        for x, kx in ((temp, k_temp), (salt, k_salt)):
            grad = (x[b] - x[a]) * face
            out.append(
                up * x[a] + down * x[b]
                - DIFFUSIVITY * face * (grad + slope * (0.5 * (kx[a] + kx[b])))
            )
        return out

    def cell_means(x, wet):
        east_grad = (x[1] - x[0]) * (wet[0] * wet[1])
        west_grad = (x[0] - x[2]) * (wet[2] * wet[0])
        north_grad = (x[3] - x[0]) * (wet[0] * wet[3])
        south_grad = (x[0] - x[4]) * (wet[4] * wet[0])
        return 0.5 * (west_grad + east_grad), 0.5 * (south_grad + north_grad)

    def level_step(k, carry):
        down_temp, down_salt = carry
        lower = planes(k - 1)
        here = planes(k)
        upper = planes(k + 1)
        wet_lower = wet_at(k - 1)
        wet_here = wet_at(k)
        wet_upper = wet_at(k + 1)
        face_top = [wet_here[i] * wet_lower[i] for i in range(5)]
        face_bottom = [wet_upper[i] * wet_here[i] for i in range(5)]
        kcs = [
            [
                0.5 * ((h[i] - lo[i]) * face_top[i] + (up[i] - h[i]) * face_bottom[i])
                for i in range(5)
            ]
            for lo, h, up in zip(lower, here, upper)
        ]
        zonal = u_ref[k]
        meridional = v_ref[k]
        east = horizontal(here, kcs, wet_here, 0, 1, zonal, ush[0, k], None)
        west = horizontal(here, kcs, wet_here, 2, 0, ush[1, k], zonal, None)
        north = horizontal(here, kcs, wet_here, 0, 3, meridional, vsh[0, k], None)
        south = horizontal(here, kcs, wet_here, 4, 0, vsh[1, k], meridional, None)
        means_here = [cell_means(f, wet_here) for f in here]
        means_upper = [cell_means(f, wet_upper) for f in upper]
        face = face_bottom[0]
        xu = [0.5 * (mh[0] + mu[0]) for mh, mu in zip(means_here, means_upper)]
        yu = [0.5 * (mh[1] + mu[1]) for mh, mu in zip(means_here, means_upper)]
        dk = [(up[0] - h[0]) * face for h, up in zip(here, upper)]
        floor = jnp.maximum(dk[2], DENSITY_FLOOR)
        slope_x = jnp.clip(-xu[2] / floor, -SLOPE_LIMIT, SLOPE_LIMIT)
        slope_y = jnp.clip(-yu[2] / floor, -SLOPE_LIMIT, SLOPE_LIMIT)
        above = jnp.clip(k + 1, 0, layer_total - 1)
        flow = 0.5 * (w_ref[k] + w_ref[above]) * face
        up, down = jnp.maximum(flow, 0.0), jnp.minimum(flow, 0.0)
        squares = slope_x * slope_x + slope_y * slope_y
        below = []
        for n in range(2):
            below.append(
                up * here[n][0] + down * upper[n][0]
                - DIFFUSIVITY * face * (slope_x * xu[n] + slope_y * yu[n] + squares * dk[n])
            )
        for n, (dst, top) in enumerate(((ot_ref, down_temp), (os_ref, down_salt))):
            divergence = (east[n] - west[n]) + (north[n] - south[n])
            divergence = divergence + (below[n] - top)
            dst[k] = here[n][0] - divergence
        return tuple(below)

    zero = jnp.zeros((rows, cols), jnp.float32)
    lax.fori_loop(0, layer_total, level_step, (zero, zero))


def on_device(
    potential_warmth,
    saltiness_anomaly,
    zonal_speed,
    meridional_speed,
    sinking_speed,
    water_indicator,
    seabed_layer_index,
):
    layer_total, rows, cols = potential_warmth.shape
    base_planes = 2 * layer_total + 1
    depth = (water_indicator * seabed_layer_index).astype(jnp.float32)
    lon_count = lax.axis_size("lon")
    lat_count = lax.axis_size("lat")
    top_row = lax.axis_index("lat") == lat_count - 1

    def column(at):
        return jnp.concatenate(
            [
                potential_warmth[:, :, at],
                saltiness_anomaly[:, :, at],
                depth[None, :, at],
                zonal_speed[:, :, at],
            ],
            0,
        )[:, :, None]

    def line(at):
        return jnp.concatenate(
            [
                potential_warmth[:, at],
                saltiness_anomaly[:, at],
                depth[None, at],
                meridional_speed[:, at],
            ],
            0,
        )[:, None]

    west_cols = lax.ppermute(
        column(cols - 1), "lon", [(i, (i + 1) % lon_count) for i in range(lon_count)]
    )
    east_cols = lax.ppermute(
        column(0), "lon", [((i + 1) % lon_count, i) for i in range(lon_count)]
    )
    top_line = line(rows - 1)
    south_rows = lax.ppermute(top_line, "lat", [(i, i + 1) for i in range(lat_count - 1)])
    north_rows = lax.ppermute(line(0), "lat", [(i + 1, i) for i in range(lat_count - 1)])
    facing = lax.ppermute(
        top_line, "lon", [(i, lon_count - 1 - i) for i in range(lon_count)]
    )[:, :, ::-1]
    ghost_row = jnp.concatenate([facing[:base_planes], -facing[base_planes:]], 0)
    north_rows = jnp.where(top_row, ghost_row, north_rows)

    field = jax.ShapeDtypeStruct(potential_warmth.shape, jnp.float32)
    vmem = pltpu.MemorySpace.VMEM
    return pl.pallas_call(
        stencil_kernel,
        out_shape=(field, field),
        in_specs=[pl.BlockSpec(memory_space=vmem)] * 10,
        out_specs=(pl.BlockSpec(memory_space=vmem), pl.BlockSpec(memory_space=vmem)),
        scratch_shapes=[
            pltpu.VMEM((4, layer_total, rows, cols), jnp.float32),
            pltpu.VMEM((4, layer_total, rows, cols), jnp.float32),
            pltpu.VMEM((2, layer_total, rows, cols), jnp.float32),
            pltpu.VMEM((2, layer_total, rows, cols), jnp.float32),
            pltpu.VMEM((5, rows, cols), jnp.float32),
        ],
    )(
        potential_warmth,
        saltiness_anomaly,
        zonal_speed,
        meridional_speed,
        sinking_speed,
        depth,
        west_cols,
        east_cols,
        south_rows,
        north_rows,
    )


def solution(mesh):
    placed = (
        P(None, "lat", "lon"),
        P(None, "lat", "lon"),
        P(None, "lat", "lon"),
        P(None, "lat", "lon"),
        P(None, "lat", "lon"),
        P("lat", "lon"),
        P("lat", "lon"),
    )
    return jax.shard_map(
        on_device,
        mesh=mesh,
        in_specs=placed,
        out_specs=(P(None, "lat", "lon"), P(None, "lat", "lon")),
        check_vma=False,
    )
```

time: 52.4 us -> 39 us (0.74)
  the two profiles are of different devices: /device:TPU:2 before, /device:TPU:1 now
where the time goes in v2:
time: 39 us; the launch traced here: 38.6 us
  starting transfers between devices  13.1 us (34%)
  Pallas kernels  12.6 us (32%)
  local copies, waits for them, and re-layouts  10.5 us (27%)
  other arithmetic  1.68 us (4%)
  between operations  0.81 us (2%)
    pallas_call x1, Pallas kernels, on_device(): pl.pallas_call(stencil_kernel, out_shape=(field, field), in_specs=[pl.Blo...  12.6 us
    ppermute x1, starting transfers between devices, on_device(): lax.ppermute(top_line, 'lon', [(i, lon_count - 1 - i) for i in range(lon_...  5.17 us
    unnamed x16, local copies, waits for them, and re-layouts  3.63 us
    ppermute x1, starting transfers between devices, on_device(): lax.ppermute(top_line, 'lat', [(i, i + 1) for i in range(lat_count - 1)])  3.56 us
    ppermute x1, starting transfers between devices, on_device(): lax.ppermute(line(0), 'lat', [(i + 1, i) for i in range(lat_count - 1)])  2.86 us
    ppermute x1, starting transfers between devices, on_device(): lax.ppermute(column(cols - 1), 'lon', [(i, (i + 1) % lon_count) for i in...  1.46 us
    ppermute x1, local copies, waits for them, and re-layouts, on_device(): lax.ppermute(column(0), 'lon', [((i + 1) % lon_count, i) for i in range(l...  1.19 us
    ppermute x1, local copies, waits for them, and re-layouts, on_device(): lax.ppermute(column(cols - 1), 'lon', [(i, (i + 1) % lon_count) for i in...  1.16 us
  transfers between devices with their start and end apart: 5, of which 0 were waited for; matrix products, arithmetic and copies ran while one was open for 15% of the time, Pallas kernels for 0%

profile of v2, /device:TPU:1, one launch (start us, length us, event | category | flops | bytes accessed | tf_op | source)
XLA Modules:
  0.0 38.6 jit_solution(8545690018923414317)
XLA Ops:
  0.6 0.7 %multiply_convert_fusion.d_ref = f32[16,256]{1,0:T(8,128)S(1)} fusion(s32[16,256]{1,0:T(8,128)} %param.12, s32[16,256]{1,0:T(8,128)} %param.13), kind=kLoop, calls=%fused_computation.9 | loop fusion | flops 8192 | bytes 49152 | tf_op jit(solution)/shard_map/convert_element_type | solution.py:169
  1.4 1.1 %fusion.2 = (f32[25,1,256]{2,1,0:T(1,128)S(1)}, f32[25,1,256]{2,1,0:T(1,128)S(1)}) fusion(f32[25,16,256]{2,1,0:T(8,128)} %v_ref.1), kind=kLoop, calls=%fused_computation.16 | loop fusion | bytes 102400 | tf_op jit(solution)/shard_map/slice | solution.py:191
  2.5 1.1 %fusion = (f32[25,1,256]{2,1,0:T(1,128)S(1)}, f32[25,1,256]{2,1,0:T(1,128)S(1)}) fusion(f32[25,16,256]{2,1,0:T(8,128)} %t_ref.1), kind=kLoop, calls=%fused_computation.14 | loop fusion | bytes 102400 | tf_op jit(solution)/shard_map/slice | solution.py:188
  3.5 1.1 %fusion.1 = (f32[25,1,256]{2,1,0:T(1,128)S(1)}, f32[25,1,256]{2,1,0:T(1,128)S(1)}) fusion(f32[25,16,256]{2,1,0:T(8,128)} %s_ref.1), kind=kLoop, calls=%fused_computation.15 | loop fusion | bytes 102400 | tf_op jit(solution)/shard_map/slice | solution.py:189
  4.7 5.2 %collective-permute-start.3 = (f32[76,1,256]{2,1,0:T(1,128)S(1)}, f32[76,1,256]{2,1,0:T(1,128)S(1)}, u32[]{:S(2)}, u32[]{:S(2)}) collective-permute-start(f32[76,1,256]{2,1,0:T(1,128)S(1)} %broadcast_in_dim.14), channel_id=1, source_target_pairs={{0,28},{4,24},{8,20},{12,16},{16,12},{20,8},{24,4},{28,0},{1,29},{... | collective-permute-start | bytes 233480 | tf_op jit(solution)/shard_map/ppermute | solution.py:205
  10.0 2.9 %collective-permute-start.4 = (f32[76,1,256]{2,1,0:T(1,128)S(1)}, f32[76,1,256]{2,1,0:T(1,128)S(1)}, u32[]{:S(2)}, u32[]{:S(2)}) collective-permute-start(f32[76,1,256]{2,1,0:T(1,128)S(1)} %broadcast_in_dim.15), channel_id=1, source_target_pairs={{1,0},{2,1},{3,2},{5,4},{6,5},{7,6},{9,8},{10,9},{11,10},{13,12},{... | collective-permute-start | bytes 233480 | tf_op jit(solution)/shard_map/ppermute | solution.py:204
  13.0 0.1 fusion.3
  13.1 0.9 %copy-done.1 = f32[25,16,256]{2,1,0:T(8,128)S(1)} copy-done((f32[25,16,256]{2,1,0:T(8,128)S(1)}, f32[25,16,256]{2,1,0:T(8,128)}, u32[]{:S(2)}) %copy-start.1) | copy-done | bytes 409624
  14.1 0.9 %copy-done.2 = f32[25,16,256]{2,1,0:T(8,128)S(1)} copy-done((f32[25,16,256]{2,1,0:T(8,128)S(1)}, f32[25,16,256]{2,1,0:T(8,128)}, u32[]{:S(2)}) %copy-start.2) | copy-done | bytes 409624
  15.1 0.2 copy.58
  15.3 0.2 copy.56
  15.5 0.2 copy.57
  15.8 0.2 copy.55
  16.0 0.2 copy.53
  16.2 0.2 copy.54
  16.5 1.5 %collective-permute-start = (f32[76,16,1]{0,1,2:T(8,128)S(1)}, f32[76,16,1]{0,1,2:T(8,128)S(1)}, u32[]{:S(2)}, u32[]{:S(2)}) collective-permute-start(f32[76,16,1]{0,1,2:T(8,128)S(1)} %maximum_bitcast_fusion), channel_id=1, source_target_pairs={{0,4},{4,8},{8,12},{12,16},{16,20},{20,24},{24,28},{28,0},{1,5},{5... | collective-permute-start | bytes 14600 | tf_op jit(solution)/shard_map/ppermute | solution.py:196
  17.9 3.6 %collective-permute-start.2 = (f32[76,1,256]{2,1,0:T(1,128)S(1)}, f32[76,1,256]{2,1,0:T(1,128)S(1)}, u32[]{:S(2)}, u32[]{:S(2)}) collective-permute-start(f32[76,1,256]{2,1,0:T(1,128)S(1)} %broadcast_in_dim.14), channel_id=1, source_target_pairs={{0,1},{1,2},{2,3},{4,5},{5,6},{6,7},{8,9},{9,10},{10,11},{12,13},{... | collective-permute-start | bytes 233480 | tf_op jit(solution)/shard_map/ppermute | solution.py:203
  21.5 1.2 %copy.52.he_ref = f32[76,16,1]{2,1,0:T(8,128)} copy(f32[76,16,1]{0,1,2:T(8,128)S(1)} %collective-permute-done.1) | data formatting | bytes 9728 | tf_op jit(solution)/shard_map/ppermute | solution.py:199
  22.7 1.2 %copy.51.hw_ref = f32[76,16,1]{2,1,0:T(8,128)} copy(f32[76,16,1]{0,1,2:T(8,128)S(1)} %collective-permute-done) | data formatting | bytes 9728 | tf_op jit(solution)/shard_map/ppermute | solution.py:196
  23.9 0.4 %slice.73 = f32[51,1,256]{2,1,0:T(1,128)S(1)} reverse(f32[51,1,256]{2,1,0:T(1,128)S(1)} %slice.83), dimensions={2} | reverse | bytes 104448 | tf_op jit(solution)/shard_map/slice | solution.py:208
  24.3 0.3 slice.75
  24.7 0.7 %broadcast_select_fusion.hn_ref = f32[76,1,256]{2,1,0:T(1,128)} fusion(f32[76,1,256]{2,1,0:T(1,128)S(1)} %collective-permute-done.4, pred[]{:T(512)S(6)} %eq.3, f32[25,1,256]{2,1,0:T(1,128)S(1)} %neg.3, f32[51,1,256]{2,1,0:T(1,128)S(1)} %slice.73), kind=kLoop, calls=%fused_computation | loop fusion | flops 38912 | bytes 233473 | tf_op jit(solution)/shard_map/jit(_where)/select_n | solution.py:209
  25.4 0.6 %copy-done.4 = f32[76,1,256]{2,1,0:T(1,128)} copy-done((f32[76,1,256]{2,1,0:T(1,128)}, f32[76,1,256]{2,1,0:T(1,128)S(1)}, u32[]{:S(2)}) %copy-start.4) | copy-done | bytes 77848
  26.0 12.6 %shard_map.86 = (f32[25,16,256]{2,1,0:T(8,128)}, f32[25,16,256]{2,1,0:T(8,128)}) custom-call(f32[25,16,256]{2,1,0:T(8,128)} %t_ref.1, f32[25,16,256]{2,1,0:T(8,128)} %s_ref.1, f32[25,16,256]{2,1,0:T(8,128)} %u_ref.1, f32[25,16,256]{2,1,0:T(8,128)} %v_ref.1, f32[25,16,256]{2,1,0:T(8,128)} %w_ref.1, f32[16,256]{1,0:T(8,128)} %copy-done.3, ...), custom_call_target="tpu_custom_call" | custom-call | tf_op jit(solution)/shard_map/pallas_call | solution.py:213
  (29 shorter events, 0.7 us)
Async XLA Ops:
  1.4 11.5 %copy-start.3 = (f32[16,256]{1,0:T(8,128)}, f32[16,256]{1,0:T(8,128)S(1)}, u32[]{:S(2)}) copy-start(f32[16,256]{1,0:T(8,128)S(1)} %multiply_convert_fusion.d_ref) | copy-start | bytes 49156
  4.6 8.3 %copy-start = (f32[25,16,256]{2,1,0:T(8,128)S(1)}, f32[25,16,256]{2,1,0:T(8,128)}, u32[]{:S(2)}) copy-start(f32[25,16,256]{2,1,0:T(8,128)} %t_ref.1) | copy-start | bytes 1228804
  4.7 19.1 %collective-permute-start.3 = (f32[76,1,256]{2,1,0:T(1,128)S(1)}, f32[76,1,256]{2,1,0:T(1,128)S(1)}, u32[]{:S(2)}, u32[]{:S(2)}) collective-permute-start(f32[76,1,256]{2,1,0:T(1,128)S(1)} %broadcast_in_dim.14), channel_id=1, source_target_pairs={{0,28},{4,24},{8,20},{12,16},{16,12},{20,8},{24,4},{28,0},{1,29},{... | collective-permute-start | bytes 233480 | tf_op jit(solution)/shard_map/ppermute | solution.py:205
  10.0 14.7 %collective-permute-start.4 = (f32[76,1,256]{2,1,0:T(1,128)S(1)}, f32[76,1,256]{2,1,0:T(1,128)S(1)}, u32[]{:S(2)}, u32[]{:S(2)}) collective-permute-start(f32[76,1,256]{2,1,0:T(1,128)S(1)} %broadcast_in_dim.15), channel_id=1, source_target_pairs={{1,0},{2,1},{3,2},{5,4},{6,5},{7,6},{9,8},{10,9},{11,10},{13,12},{... | collective-permute-start | bytes 233480 | tf_op jit(solution)/shard_map/ppermute | solution.py:204
  12.9 1.0 %copy-start.1 = (f32[25,16,256]{2,1,0:T(8,128)S(1)}, f32[25,16,256]{2,1,0:T(8,128)}, u32[]{:S(2)}) copy-start(f32[25,16,256]{2,1,0:T(8,128)} %s_ref.1) | copy-start | bytes 1228804
  14.0 1.0 %copy-start.2 = (f32[25,16,256]{2,1,0:T(8,128)S(1)}, f32[25,16,256]{2,1,0:T(8,128)}, u32[]{:S(2)}) copy-start(f32[25,16,256]{2,1,0:T(8,128)} %u_ref.1) | copy-start | bytes 1228804
  15.8 5.7 %collective-permute-start.1 = (f32[76,16,1]{0,1,2:T(8,128)S(1)}, f32[76,16,1]{0,1,2:T(8,128)S(1)}, u32[]{:S(2)}, u32[]{:S(2)}) collective-permute-start(f32[76,16,1]{0,1,2:T(8,128)S(1)} %maximum_bitcast_fusion.1), channel_id=1, source_target_pairs={{4,0},{8,4},{12,8},{16,12},{20,16},{24,20},{28,24},{0,28},{5,1},{9... | collective-permute-start | bytes 14600 | tf_op jit(solution)/shard_map/ppermute | solution.py:199
  16.5 6.2 %collective-permute-start = (f32[76,16,1]{0,1,2:T(8,128)S(1)}, f32[76,16,1]{0,1,2:T(8,128)S(1)}, u32[]{:S(2)}, u32[]{:S(2)}) collective-permute-start(f32[76,16,1]{0,1,2:T(8,128)S(1)} %maximum_bitcast_fusion), channel_id=1, source_target_pairs={{0,4},{4,8},{8,12},{12,16},{16,20},{20,24},{24,28},{28,0},{1,5},{5... | collective-permute-start | bytes 14600 | tf_op jit(solution)/shard_map/ppermute | solution.py:196
  17.9 7.5 %collective-permute-start.2 = (f32[76,1,256]{2,1,0:T(1,128)S(1)}, f32[76,1,256]{2,1,0:T(1,128)S(1)}, u32[]{:S(2)}, u32[]{:S(2)}) collective-permute-start(f32[76,1,256]{2,1,0:T(1,128)S(1)} %broadcast_in_dim.14), channel_id=1, source_target_pairs={{0,1},{1,2},{2,3},{4,5},{5,6},{6,7},{8,9},{9,10},{10,11},{12,13},{... | collective-permute-start | bytes 233480 | tf_op jit(solution)/shard_map/ppermute | solution.py:203
  25.4 0.6 %copy-start.4 = (f32[76,1,256]{2,1,0:T(1,128)}, f32[76,1,256]{2,1,0:T(1,128)S(1)}, u32[]{:S(2)}) copy-start(f32[76,1,256]{2,1,0:T(1,128)S(1)} %collective-permute-done.2.hs_ref) | copy-start | bytes 233476

commit v3 on v2

--- a/solution.py
+++ b/solution.py
@@ -36,30 +36,48 @@
     def south_of(x, h):
         return jnp.where(south_edge, h, pltpu.roll(x, 1, 0))
 
+    lane_tile = hw_ref.shape[1]
+
+    def column_of(ref, p, at):
+        packed = ref[...]
+        shift = (at - p) % lane_tile
+        if shift:
+            packed = pltpu.roll(packed, shift, 1)
+        return jnp.concatenate([packed] * (cols // lane_tile), 1)
+
+    def east_halo(p):
+        return column_of(he_ref, p, lane_tile - 1)
+
+    def west_halo(p):
+        return column_of(hw_ref, p, 0)
+
+    def north_halo(p):
+        return hn_ref[p : p + 1, :]
+
+    def south_halo(p):
+        return hs_ref[p : p + 1, :]
+
     depth_plane = 2 * layer_total
-    depth = d_ref[...]
+    depth = (d_ref[0] * d_ref[1]).astype(jnp.float32)
     dsh[0] = depth
-    dsh[1] = east_of(depth, he_ref[depth_plane])
-    dsh[2] = west_of(depth, hw_ref[depth_plane])
-    dsh[3] = north_of(depth, hn_ref[depth_plane])
-    dsh[4] = south_of(depth, hs_ref[depth_plane])
-
-    def prepare(k, carry):
+    dsh[1] = east_of(depth, east_halo(depth_plane))
+    dsh[2] = west_of(depth, west_halo(depth_plane))
+    dsh[3] = north_of(depth, north_halo(depth_plane))
+    dsh[4] = south_of(depth, south_halo(depth_plane))
+
+    for k in range(layer_total):
         for src, dst, base in ((t_ref, tsh, 0), (s_ref, ssh, layer_total)):
             x = src[k]
-            dst[0, k] = east_of(x, he_ref[base + k])
-            dst[1, k] = west_of(x, hw_ref[base + k])
-            dst[2, k] = north_of(x, hn_ref[base + k])
-            dst[3, k] = south_of(x, hs_ref[base + k])
+            dst[0, k] = east_of(x, east_halo(base + k))
+            dst[1, k] = west_of(x, west_halo(base + k))
+            dst[2, k] = north_of(x, north_halo(base + k))
+            dst[3, k] = south_of(x, south_halo(base + k))
         x = u_ref[k]
-        ush[0, k] = east_of(x, he_ref[depth_plane + 1 + k])
-        ush[1, k] = west_of(x, hw_ref[depth_plane + 1 + k])
+        ush[0, k] = east_of(x, east_halo(depth_plane + 1 + k))
+        ush[1, k] = west_of(x, west_halo(depth_plane + 1 + k))
         x = v_ref[k]
-        vsh[0, k] = north_of(x, hn_ref[depth_plane + 1 + k])
-        vsh[1, k] = south_of(x, hs_ref[depth_plane + 1 + k])
-        return carry
-
-    lax.fori_loop(0, layer_total, prepare, 0)
+        vsh[0, k] = north_of(x, north_halo(depth_plane + 1 + k))
+        vsh[1, k] = south_of(x, south_halo(depth_plane + 1 + k))
 
     def planes(k):
         at = jnp.clip(k, 0, layer_total - 1)
@@ -155,6 +173,35 @@
     lax.fori_loop(0, layer_total, level_step, (zero, zero))
 
 
+def edge_kernel(
+    flag_ref, t_ref, s_ref, u_ref, v_ref, d_ref, west_ref, east_ref, first_ref, second_ref
+):
+    layer_total, rows, cols = t_ref.shape
+    lane_tile = west_ref.shape[1]
+    odd = flag_ref[0] == 1
+    depth = (d_ref[0] * d_ref[1]).astype(jnp.float32)
+    lane = lax.broadcasted_iota(jnp.int32, (rows, lane_tile), 1)
+    column_planes = (
+        [t_ref[k] for k in range(layer_total)]
+        + [s_ref[k] for k in range(layer_total)]
+        + [depth]
+        + [u_ref[k] for k in range(layer_total)]
+    )
+    west = jnp.zeros((rows, lane_tile), jnp.float32)
+    east = jnp.zeros((rows, lane_tile), jnp.float32)
+    for p, x in enumerate(column_planes):
+        west = jnp.where(lane == p, x[:, cols - 1 :], west)
+        east = jnp.where(lane == p, x[:, :1], east)
+    west_ref[...] = west
+    east_ref[...] = east
+    row_planes = column_planes[: 2 * layer_total + 1] + [v_ref[k] for k in range(layer_total)]
+    for p, x in enumerate(row_planes):
+        top = x[rows - 1 :, :]
+        bottom = x[:1, :]
+        first_ref[p : p + 1, :] = jnp.where(odd, top, bottom)
+        second_ref[p : p + 1, :] = jnp.where(odd, bottom, top)
+
+
 def on_device(
     potential_warmth,
     saltiness_anomaly,
@@ -166,50 +213,54 @@
 ):
     layer_total, rows, cols = potential_warmth.shape
     base_planes = 2 * layer_total + 1
-    depth = (water_indicator * seabed_layer_index).astype(jnp.float32)
+    halo_planes = 3 * layer_total + 1
+    lane_tile = 128
     lon_count = lax.axis_size("lon")
     lat_count = lax.axis_size("lat")
-    top_row = lax.axis_index("lat") == lat_count - 1
-
-    def column(at):
-        return jnp.concatenate(
-            [
-                potential_warmth[:, :, at],
-                saltiness_anomaly[:, :, at],
-                depth[None, :, at],
-                zonal_speed[:, :, at],
-            ],
-            0,
-        )[:, :, None]
-
-    def line(at):
-        return jnp.concatenate(
-            [
-                potential_warmth[:, at],
-                saltiness_anomaly[:, at],
-                depth[None, at],
-                meridional_speed[:, at],
-            ],
-            0,
-        )[:, None]
+    lat_index = lax.axis_index("lat")
+    odd = lat_index % 2
+    flag = jnp.full((1,), odd, jnp.int32)
+    columns = jnp.stack([water_indicator, seabed_layer_index])
+    vmem = pltpu.MemorySpace.VMEM
+    smem = pltpu.MemorySpace.SMEM
+    packed = jax.ShapeDtypeStruct((rows, lane_tile), jnp.float32)
+    lines = jax.ShapeDtypeStruct((halo_planes, cols), jnp.float32)
+    west_pack, east_pack, first_lines, second_lines = pl.pallas_call(
+        edge_kernel,
+        out_shape=(packed, packed, lines, lines),
+        in_specs=[pl.BlockSpec(memory_space=smem)] + [pl.BlockSpec(memory_space=vmem)] * 5,
+        out_specs=tuple(pl.BlockSpec(memory_space=vmem) for _ in range(4)),
+    )(flag, potential_warmth, saltiness_anomaly, zonal_speed, meridional_speed, columns)
 
     west_cols = lax.ppermute(
-        column(cols - 1), "lon", [(i, (i + 1) % lon_count) for i in range(lon_count)]
+        west_pack, "lon", [(i, (i + 1) % lon_count) for i in range(lon_count)]
     )
     east_cols = lax.ppermute(
-        column(0), "lon", [((i + 1) % lon_count, i) for i in range(lon_count)]
-    )
-    top_line = line(rows - 1)
-    south_rows = lax.ppermute(top_line, "lat", [(i, i + 1) for i in range(lat_count - 1)])
-    north_rows = lax.ppermute(line(0), "lat", [(i + 1, i) for i in range(lat_count - 1)])
-    facing = lax.ppermute(
-        top_line, "lon", [(i, lon_count - 1 - i) for i in range(lon_count)]
-    )[:, :, ::-1]
-    ghost_row = jnp.concatenate([facing[:base_planes], -facing[base_planes:]], 0)
-    north_rows = jnp.where(top_row, ghost_row, north_rows)
+        east_pack, "lon", [((i + 1) % lon_count, i) for i in range(lon_count)]
+    )
+
+    def device(lat, lon):
+        return lon * lat_count + lat
+
+    first_pairs = []
+    second_pairs = []
+    for lon in range(lon_count):
+        for lat in range(lat_count - 1):
+            pairs = first_pairs if lat % 2 else second_pairs
+            pairs.append((device(lat, lon), device(lat + 1, lon)))
+            pairs.append((device(lat + 1, lon), device(lat, lon)))
+        first_pairs.append(
+            (device(lat_count - 1, lon), device(lat_count - 1, lon_count - 1 - lon))
+        )
+    first_got = lax.ppermute(first_lines, ("lon", "lat"), first_pairs)
+    second_got = lax.ppermute(second_lines, ("lon", "lat"), second_pairs)
+    mirrored = first_got[:, ::-1]
+    folded = jnp.concatenate([mirrored[:base_planes], -mirrored[base_planes:]], 0)
+    top_row = lat_index == lat_count - 1
+    north_rows = jnp.where(odd == 0, second_got, jnp.where(top_row, folded, first_got))
+    south_rows = jnp.where(odd == 1, second_got, first_got)
 
     field = jax.ShapeDtypeStruct(potential_warmth.shape, jnp.float32)
-    vmem = pltpu.MemorySpace.VMEM
     return pl.pallas_call(
         stencil_kernel,
         out_shape=(field, field),
@@ -228,7 +279,7 @@
         zonal_speed,
         meridional_speed,
         sinking_speed,
-        depth,
+        columns,
         west_cols,
         east_cols,
         south_rows,

time: 39 us -> 29.6 us (0.76)
  the two profiles are of different devices: /device:TPU:1 before, /device:TPU:2 now
where the time goes in v3:
time: 29.6 us; the launch traced here: 29.1 us
  Pallas kernels  13.2 us (45%)
  starting transfers between devices  10.8 us (36%)
  other arithmetic  2.03 us (7%)
  local copies, waits for them, and re-layouts  1.65 us (6%)
  waiting for transfers between devices  0.78 us (3%)
  between operations  0.67 us (2%)
    pallas_call x1, Pallas kernels, on_device(): pl.pallas_call(stencil_kernel, out_shape=(field, field), in_specs=[pl.Blo...  10.6 us
    ppermute x1, starting transfers between devices, on_device(): lax.ppermute(east_pack, 'lon', [((i + 1) % lon_count, i) for i in range(l...  4.22 us
    ppermute x1, starting transfers between devices, on_device(): second_got = lax.ppermute(second_lines, ('lon', 'lat'), second_pairs)  4.17 us
    pallas_call x1, Pallas kernels, on_device(): pl.pallas_call(edge_kernel, out_shape=(packed, packed, lines, lines), in_...  2.57 us
    ppermute x1, starting transfers between devices, on_device(): first_got = lax.ppermute(first_lines, ('lon', 'lat'), first_pairs)  1.91 us
    another operation x1, other arithmetic, on_device(): columns = jnp.stack([water_indicator, seabed_layer_index])  1.33 us
    unnamed x6, local copies, waits for them, and re-layouts  1.3 us
    ppermute x1, waiting for transfers between devices, on_device(): lax.ppermute(west_pack, 'lon', [(i, (i + 1) % lon_count) for i in range(l...  0.77 us
  transfers between devices with their start and end apart: 4, of which 1 were waited for; matrix products, arithmetic and copies ran while one was open for 4% of the time, Pallas kernels for 0%

profile of v3, /device:TPU:2, one launch (start us, length us, event | category | flops | bytes accessed | tf_op | source)
XLA Modules:
  0.0 29.1 jit_solution(6651996559113741530)
XLA Ops:
  0.6 0.0 copy-start
  0.7 0.7 %copy-done = s32[16,256]{1,0:T(8,128)S(1)} copy-done((s32[16,256]{1,0:T(8,128)S(1)}, s32[16,256]{1,0:T(8,128)}, u32[]{:S(2)}) %copy-start) | copy-done | bytes 16408
  1.3 1.3 %pad_add_fusion.d_ref = s32[2,16,256]{2,1,0:T(8,128)} fusion(s32[1,16,256]{2,1,0:T(8,128)S(1)} %bitcast.3, s32[1,16,256]{2,1,0:T(8,128)} %bitcast.4), kind=kLoop, calls=%fused_computation.3 | loop fusion | flops 8192 | bytes 65536 | tf_op jit(solution)/shard_map/stack | solution.py:223
  2.7 2.6 %shard_map.86 = (f32[16,128]{1,0:T(8,128)}, f32[16,128]{1,0:T(8,128)}, f32[76,256]{1,0:T(8,128)}, f32[76,256]{1,0:T(8,128)}) custom-call(s32[1]{0:T(128)} %bitcast.2.flag_ref, f32[25,16,256]{2,1,0:T(8,128)} %t_ref.3, f32[25,16,256]{2,1,0:T(8,128)} %s_ref.3, f32[25,16,256]{2,1,0:T(8,128)} %u_ref.3, f32[25,16,256]{2,1,0:T(8,128)} %v_ref.3, ...), custom_call_target="tpu_custom_call" | custom-call | tf_op jit(solution)/shard_map/pallas_call | solution.py:228
  5.3 1.9 %collective-permute-start.3 = (f32[76,256]{1,0:T(8,128)}, f32[76,256]{1,0:T(8,128)S(1)}, u32[]{:S(2)}, u32[]{:S(2)}) collective-permute-start(f32[76,256]{1,0:T(8,128)} %get-tuple-element.9), channel_id=1, source_target_pairs={{1,2},{2,1},{3,31},{5,6},{6,5},{7,27},{9,10},{10,9},{11,23},{13,14... | collective-permute-start | bytes 233480 | tf_op jit(solution)/shard_map/ppermute | solution.py:255
  7.2 4.2 %collective-permute-start.2 = (f32[76,256]{1,0:T(8,128)}, f32[76,256]{1,0:T(8,128)S(1)}, u32[]{:S(2)}, u32[]{:S(2)}) collective-permute-start(f32[76,256]{1,0:T(8,128)} %get-tuple-element.8), channel_id=1, source_target_pairs={{0,1},{1,0},{2,3},{3,2},{4,5},{5,4},{6,7},{7,6},{8,9},{9,8},{10,11... | collective-permute-start | bytes 233480 | tf_op jit(solution)/shard_map/ppermute | solution.py:256
  11.3 0.5 %collective-permute-start = (f32[16,128]{1,0:T(8,128)}, f32[16,128]{1,0:T(8,128)S(1)}, u32[]{:S(2)}, u32[]{:S(2)}) collective-permute-start(f32[16,128]{1,0:T(8,128)} %get-tuple-element.6), channel_id=1, source_target_pairs={{0,4},{4,8},{8,12},{12,16},{16,20},{20,24},{24,28},{28,0},{1,5},{5... | collective-permute-start | bytes 24584 | tf_op jit(solution)/shard_map/ppermute | solution.py:235
  11.8 4.2 %collective-permute-start.1 = (f32[16,128]{1,0:T(8,128)}, f32[16,128]{1,0:T(8,128)S(1)}, u32[]{:S(2)}, u32[]{:S(2)}) collective-permute-start(f32[16,128]{1,0:T(8,128)} %get-tuple-element.7), channel_id=1, source_target_pairs={{4,0},{8,4},{12,8},{16,12},{20,16},{24,20},{28,24},{0,28},{5,1},{9... | collective-permute-start | bytes 24584 | tf_op jit(solution)/shard_map/ppermute | solution.py:238
  16.1 0.0 collective-permute-done.3
  16.1 0.2 slice.15
  16.3 0.2 slice.13
  16.4 0.0 collective-permute-done.2
  16.4 0.7 %fusion = (f32[76,256]{1,0:T(8,128)}, f32[76,256]{1,0:T(8,128)}) fusion(f32[76,256]{1,0:T(8,128)S(1)} %collective-permute-done.2, f32[76,256]{1,0:T(8,128)S(1)} %collective-permute-done.3, f32[25,256]{1,0:T(8,128)S(1)} %neg.3, f32[51,256]{1,0:T(8,128)S(1)} %slice.13, pred[]{:T(512)S(6)} %eq.13, pred[]{:T(512)S(6)} %eq.12, pred[]{:T(512)S(6)} %eq.11), kind=kLoop, calls=%fused_computation.1 | loop fusion | flops 77824 | bytes 389123 | tf_op jit(solution)/shard_map/jit(_where)/select_n | solution.py:260
  17.1 0.8 %collective-permute-done.hw_ref = f32[16,128]{1,0:T(8,128)S(1)} collective-permute-done((f32[16,128]{1,0:T(8,128)}, f32[16,128]{1,0:T(8,128)S(1)}, u32[]{:S(2)}, u32[]{:S(2)}) %collective-permute-start) | collective-permute-done | bytes 8224 | tf_op jit(solution)/shard_map/ppermute | solution.py:235
  17.9 0.0 copy-start.1
  17.9 0.0 collective-permute-done.1.he_ref
  17.9 0.0 copy-start.2
  17.9 0.6 %copy-done.1 = f32[16,128]{1,0:T(8,128)} copy-done((f32[16,128]{1,0:T(8,128)}, f32[16,128]{1,0:T(8,128)S(1)}, u32[]{:S(2)}) %copy-start.1) | copy-done | bytes 8216
  18.5 0.0 copy-done.2
  18.5 10.6 %shard_map.87 = (f32[25,16,256]{2,1,0:T(8,128)}, f32[25,16,256]{2,1,0:T(8,128)}) custom-call(f32[25,16,256]{2,1,0:T(8,128)} %t_ref.3, f32[25,16,256]{2,1,0:T(8,128)} %s_ref.3, f32[25,16,256]{2,1,0:T(8,128)} %u_ref.3, f32[25,16,256]{2,1,0:T(8,128)} %v_ref.3, f32[25,16,256]{2,1,0:T(8,128)} %w_ref.1, s32[2,16,256]{2,1,0:T(8,128)} %pad_add_fusion.d_ref, ...), custom_call_target="tpu_custom_call" | custom-call | tf_op jit(solution)/shard_map/pallas_call | solution.py:264
  (3 shorter events, 0.0 us)
Async XLA Ops:
  0.6 0.7 %copy-start = (s32[16,256]{1,0:T(8,128)S(1)}, s32[16,256]{1,0:T(8,128)}, u32[]{:S(2)}) copy-start(s32[16,256]{1,0:T(8,128)} %param.13) | copy-start | bytes 49156
  5.3 10.8 %collective-permute-start.3 = (f32[76,256]{1,0:T(8,128)}, f32[76,256]{1,0:T(8,128)S(1)}, u32[]{:S(2)}, u32[]{:S(2)}) collective-permute-start(f32[76,256]{1,0:T(8,128)} %get-tuple-element.9), channel_id=1, source_target_pairs={{1,2},{2,1},{3,31},{5,6},{6,5},{7,27},{9,10},{10,9},{11,23},{13,14... | collective-permute-start | bytes 233480 | tf_op jit(solution)/shard_map/ppermute | solution.py:255
  7.2 9.3 %collective-permute-start.2 = (f32[76,256]{1,0:T(8,128)}, f32[76,256]{1,0:T(8,128)S(1)}, u32[]{:S(2)}, u32[]{:S(2)}) collective-permute-start(f32[76,256]{1,0:T(8,128)} %get-tuple-element.8), channel_id=1, source_target_pairs={{0,1},{1,0},{2,3},{3,2},{4,5},{5,4},{6,7},{7,6},{8,9},{9,8},{10,11... | collective-permute-start | bytes 233480 | tf_op jit(solution)/shard_map/ppermute | solution.py:256
  11.3 6.6 %collective-permute-start = (f32[16,128]{1,0:T(8,128)}, f32[16,128]{1,0:T(8,128)S(1)}, u32[]{:S(2)}, u32[]{:S(2)}) collective-permute-start(f32[16,128]{1,0:T(8,128)} %get-tuple-element.6), channel_id=1, source_target_pairs={{0,4},{4,8},{8,12},{12,16},{16,20},{20,24},{24,28},{28,0},{1,5},{5... | collective-permute-start | bytes 24584 | tf_op jit(solution)/shard_map/ppermute | solution.py:235
  11.8 6.1 %collective-permute-start.1 = (f32[16,128]{1,0:T(8,128)}, f32[16,128]{1,0:T(8,128)S(1)}, u32[]{:S(2)}, u32[]{:S(2)}) collective-permute-start(f32[16,128]{1,0:T(8,128)} %get-tuple-element.7), channel_id=1, source_target_pairs={{4,0},{8,4},{12,8},{16,12},{20,16},{24,20},{28,24},{0,28},{5,1},{9... | collective-permute-start | bytes 24584 | tf_op jit(solution)/shard_map/ppermute | solution.py:238
  17.9 0.6 %copy-start.1 = (f32[16,128]{1,0:T(8,128)}, f32[16,128]{1,0:T(8,128)S(1)}, u32[]{:S(2)}) copy-start(f32[16,128]{1,0:T(8,128)S(1)} %collective-permute-done.hw_ref) | copy-start | bytes 24580
  17.9 0.6 %copy-start.2 = (f32[16,128]{1,0:T(8,128)}, f32[16,128]{1,0:T(8,128)S(1)}, u32[]{:S(2)}) copy-start(f32[16,128]{1,0:T(8,128)S(1)} %collective-permute-done.1.he_ref) | copy-start | bytes 24580

commit v4 on v3

--- a/solution.py
+++ b/solution.py
@@ -13,8 +13,8 @@
 
 
 def stencil_kernel(
-    t_ref, s_ref, u_ref, v_ref, w_ref, d_ref, hw_ref, he_ref, hs_ref, hn_ref,
-    ot_ref, os_ref, tsh, ssh, ush, vsh, dsh,
+    flag_ref, t_ref, s_ref, u_ref, v_ref, w_ref, wi_ref, sb_ref, hw_ref, he_ref,
+    first_ref, second_ref, ot_ref, os_ref, tsh, ssh, ush, vsh, dsh,
 ):
     layer_total, rows, cols = t_ref.shape
     lane = lax.broadcasted_iota(jnp.int32, (rows, cols), 1)
@@ -51,14 +51,16 @@
     def west_halo(p):
         return column_of(hw_ref, p, 0)
 
+    odd = flag_ref[0] == 1
+
     def north_halo(p):
-        return hn_ref[p : p + 1, :]
+        return jnp.where(odd, first_ref[p : p + 1, :], second_ref[p : p + 1, :])
 
     def south_halo(p):
-        return hs_ref[p : p + 1, :]
+        return jnp.where(odd, second_ref[p : p + 1, :], first_ref[p : p + 1, :])
 
     depth_plane = 2 * layer_total
-    depth = (d_ref[0] * d_ref[1]).astype(jnp.float32)
+    depth = (wi_ref[...] * sb_ref[...]).astype(jnp.float32)
     dsh[0] = depth
     dsh[1] = east_of(depth, east_halo(depth_plane))
     dsh[2] = west_of(depth, west_halo(depth_plane))
@@ -174,12 +176,14 @@
 
 
 def edge_kernel(
-    flag_ref, t_ref, s_ref, u_ref, v_ref, d_ref, west_ref, east_ref, first_ref, second_ref
+    flag_ref, t_ref, s_ref, u_ref, v_ref, wi_ref, sb_ref,
+    west_ref, east_ref, first_ref, second_ref, tops_ref, bottoms_ref,
 ):
     layer_total, rows, cols = t_ref.shape
     lane_tile = west_ref.shape[1]
     odd = flag_ref[0] == 1
-    depth = (d_ref[0] * d_ref[1]).astype(jnp.float32)
+    top = flag_ref[1] == 1
+    depth = (wi_ref[...] * sb_ref[...]).astype(jnp.float32)
     lane = lax.broadcasted_iota(jnp.int32, (rows, lane_tile), 1)
     column_planes = (
         [t_ref[k] for k in range(layer_total)]
@@ -194,12 +198,27 @@
         east = jnp.where(lane == p, x[:, :1], east)
     west_ref[...] = west
     east_ref[...] = east
-    row_planes = column_planes[: 2 * layer_total + 1] + [v_ref[k] for k in range(layer_total)]
+    base_planes = 2 * layer_total + 1
+    row_planes = column_planes[:base_planes] + [v_ref[k] for k in range(layer_total)]
     for p, x in enumerate(row_planes):
-        top = x[rows - 1 :, :]
-        bottom = x[:1, :]
-        first_ref[p : p + 1, :] = jnp.where(odd, top, bottom)
-        second_ref[p : p + 1, :] = jnp.where(odd, bottom, top)
+        tops_ref[p : p + 1, :] = x[rows - 1 :, :]
+        bottoms_ref[p : p + 1, :] = x[:1, :]
+    tops = tops_ref[...]
+    bottoms = bottoms_ref[...]
+    line_lane = lax.broadcasted_iota(jnp.int32, tops.shape, 1)
+    mirrored = tops
+    step = 1
+    while step < cols:
+        mirrored = jnp.where(
+            (line_lane & step) != 0,
+            pltpu.roll(mirrored, step, 1),
+            pltpu.roll(mirrored, cols - step, 1),
+        )
+        step *= 2
+    plane = lax.broadcasted_iota(jnp.int32, tops.shape, 0)
+    folded = jnp.where(plane >= base_planes, -mirrored, mirrored)
+    first_ref[...] = jnp.where(top, folded, jnp.where(odd, tops, bottoms))
+    second_ref[...] = jnp.where(odd, bottoms, tops)
 
 
 def on_device(
@@ -219,8 +238,8 @@
     lat_count = lax.axis_size("lat")
     lat_index = lax.axis_index("lat")
     odd = lat_index % 2
-    flag = jnp.full((1,), odd, jnp.int32)
-    columns = jnp.stack([water_indicator, seabed_layer_index])
+    top_row = lat_index == lat_count - 1
+    flag = jnp.stack([odd, top_row.astype(jnp.int32)]).astype(jnp.int32)
     vmem = pltpu.MemorySpace.VMEM
     smem = pltpu.MemorySpace.SMEM
     packed = jax.ShapeDtypeStruct((rows, lane_tile), jnp.float32)
@@ -228,9 +247,21 @@
     west_pack, east_pack, first_lines, second_lines = pl.pallas_call(
         edge_kernel,
         out_shape=(packed, packed, lines, lines),
-        in_specs=[pl.BlockSpec(memory_space=smem)] + [pl.BlockSpec(memory_space=vmem)] * 5,
+        in_specs=[pl.BlockSpec(memory_space=smem)] + [pl.BlockSpec(memory_space=vmem)] * 6,
         out_specs=tuple(pl.BlockSpec(memory_space=vmem) for _ in range(4)),
-    )(flag, potential_warmth, saltiness_anomaly, zonal_speed, meridional_speed, columns)
+        scratch_shapes=[
+            pltpu.VMEM((halo_planes, cols), jnp.float32),
+            pltpu.VMEM((halo_planes, cols), jnp.float32),
+        ],
+    )(
+        flag,
+        potential_warmth,
+        saltiness_anomaly,
+        zonal_speed,
+        meridional_speed,
+        water_indicator,
+        seabed_layer_index,
+    )
 
     west_cols = lax.ppermute(
         west_pack, "lon", [(i, (i + 1) % lon_count) for i in range(lon_count)]
@@ -254,17 +285,11 @@
         )
     first_got = lax.ppermute(first_lines, ("lon", "lat"), first_pairs)
     second_got = lax.ppermute(second_lines, ("lon", "lat"), second_pairs)
-    mirrored = first_got[:, ::-1]
-    folded = jnp.concatenate([mirrored[:base_planes], -mirrored[base_planes:]], 0)
-    top_row = lat_index == lat_count - 1
-    north_rows = jnp.where(odd == 0, second_got, jnp.where(top_row, folded, first_got))
-    south_rows = jnp.where(odd == 1, second_got, first_got)
-
     field = jax.ShapeDtypeStruct(potential_warmth.shape, jnp.float32)
     return pl.pallas_call(
         stencil_kernel,
         out_shape=(field, field),
-        in_specs=[pl.BlockSpec(memory_space=vmem)] * 10,
+        in_specs=[pl.BlockSpec(memory_space=smem)] + [pl.BlockSpec(memory_space=vmem)] * 11,
         out_specs=(pl.BlockSpec(memory_space=vmem), pl.BlockSpec(memory_space=vmem)),
         scratch_shapes=[
             pltpu.VMEM((4, layer_total, rows, cols), jnp.float32),
@@ -274,16 +299,18 @@
             pltpu.VMEM((5, rows, cols), jnp.float32),
         ],
     )(
+        flag,
         potential_warmth,
         saltiness_anomaly,
         zonal_speed,
         meridional_speed,
         sinking_speed,
-        columns,
+        water_indicator,
+        seabed_layer_index,
         west_cols,
         east_cols,
-        south_rows,
-        north_rows,
+        first_got,
+        second_got,
     )
 
 

time: 29.6 us -> 29.2 us (0.986)
  other arithmetic: 2.03 us -> 0.59 us
  waiting for transfers between devices: 0.78 us -> 1.84 us
  Pallas kernels: 13.2 us -> 13.7 us
  local copies, waits for them, and re-layouts: 1.65 us -> 1.24 us
    ppermute x1, waiting for transfers between devices: 0.77 us -> 1.83 us  [on_device(): lax.ppermute(west_pack, 'lon', [(i, (i + 1) % lon_count) for i in range(l...]
    another operation x1, other arithmetic: 1.33 us -> 0.59 us  [on_device(): flag = jnp.stack([odd, top_row.astype(jnp.int32)]).astype(jnp.int32)]
    select_n x1 -> x0, other arithmetic: 0.69 us -> none  [on_device(): jnp.where(odd == 0, second_got, jnp.where(top_row, folded, first_got))]
    pallas_call x1, Pallas kernels: 2.57 us -> 3.18 us  [on_device(): pl.pallas_call(edge_kernel, out_shape=(packed, packed, lines, lines), in_...]
    slice x4 -> x0, local copies, waits for them, and re-layouts: 0.35 us -> none  [the longest x2 0.18 us: on_device(): mirrored[:base_planes]]
    unnamed x6 -> x8, local copies, waits for them, and re-layouts: 1.3 us -> 1.24 us
  transfers between devices with their start and end apart: 4 -> 4, of which waited for: 1 -> 1; matrix products, arithmetic and copies ran while one was open for 4% -> 0% of each run, Pallas kernels for 0% -> 0%
where the time goes in v4:
time: 29.2 us; the launch traced here: 28.9 us
  Pallas kernels  13.7 us (47%)
  starting transfers between devices  10.8 us (37%)
  waiting for transfers between devices  1.84 us (6%)
  local copies, waits for them, and re-layouts  1.24 us (4%)
  between operations  0.68 us (2%)
  other arithmetic  0.59 us (2%)
    pallas_call x1, Pallas kernels, on_device(): pl.pallas_call(stencil_kernel, out_shape=(field, field), in_specs=[pl.Blo...  10.5 us
    ppermute x1, starting transfers between devices, on_device(): lax.ppermute(east_pack, 'lon', [((i + 1) % lon_count, i) for i in range(l...  4.22 us
    ppermute x1, starting transfers between devices, on_device(): second_got = lax.ppermute(second_lines, ('lon', 'lat'), second_pairs)  4.17 us
    pallas_call x1, Pallas kernels, on_device(): pl.pallas_call(edge_kernel, out_shape=(packed, packed, lines, lines), in_...  3.18 us
    ppermute x1, starting transfers between devices, on_device(): first_got = lax.ppermute(first_lines, ('lon', 'lat'), first_pairs)  1.91 us
    ppermute x1, waiting for transfers between devices, on_device(): lax.ppermute(west_pack, 'lon', [(i, (i + 1) % lon_count) for i in range(l...  1.83 us
    unnamed x8, local copies, waits for them, and re-layouts  1.24 us
    another operation x1, other arithmetic, on_device(): flag = jnp.stack([odd, top_row.astype(jnp.int32)]).astype(jnp.int32)  0.59 us
  transfers between devices with their start and end apart: 4, of which 1 were waited for; matrix products, arithmetic and copies ran while one was open for 0% of the time, Pallas kernels for 0%

profile of v4, /device:TPU:2, one launch (start us, length us, event | category | flops | bytes accessed | tf_op | source)
XLA Modules:
  0.0 28.9 jit_solution(4468159318703500033)
XLA Ops:
  0.6 0.6 %pad_add_fusion.flag_ref = s32[2]{0:T(128)} fusion(s32[1]{0:T(128)} %bitcast.1, s32[1]{0:T(128)} %bitcast), kind=kLoop, calls=%fused_computation | loop fusion | flops 2 | bytes 16 | tf_op jit(solution)/shard_map/stack | solution.py:242
  1.2 3.2 %shard_map.86 = (f32[16,128]{1,0:T(8,128)}, f32[16,128]{1,0:T(8,128)}, f32[76,256]{1,0:T(8,128)}, f32[76,256]{1,0:T(8,128)}) custom-call(s32[2]{0:T(128)} %pad_add_fusion.flag_ref, f32[25,16,256]{2,1,0:T(8,128)} %t_ref.3, f32[25,16,256]{2,1,0:T(8,128)} %s_ref.3, f32[25,16,256]{2,1,0:T(8,128)} %u_ref.3, f32[25,16,256]{2,1,0:T(8,128)} %v_ref.3, ...), custom_call_target="tpu_custom_call" | custom-call | tf_op jit(solution)/shard_map/pallas_call | solution.py:247
  4.4 1.9 %collective-permute-start.2 = (f32[76,256]{1,0:T(8,128)}, f32[76,256]{1,0:T(8,128)S(1)}, u32[]{:S(2)}, u32[]{:S(2)}) collective-permute-start(f32[76,256]{1,0:T(8,128)} %get-tuple-element.8), channel_id=1, source_target_pairs={{1,2},{2,1},{3,31},{5,6},{6,5},{7,27},{9,10},{10,9},{11,23},{13,14... | collective-permute-start | bytes 233480 | tf_op jit(solution)/shard_map/ppermute | solution.py:286
  6.3 4.2 %collective-permute-start.3 = (f32[76,256]{1,0:T(8,128)}, f32[76,256]{1,0:T(8,128)S(1)}, u32[]{:S(2)}, u32[]{:S(2)}) collective-permute-start(f32[76,256]{1,0:T(8,128)} %get-tuple-element.9), channel_id=1, source_target_pairs={{0,1},{1,0},{2,3},{3,2},{4,5},{5,4},{6,7},{7,6},{8,9},{9,8},{10,11... | collective-permute-start | bytes 233480 | tf_op jit(solution)/shard_map/ppermute | solution.py:287
  10.5 0.5 %collective-permute-start = (f32[16,128]{1,0:T(8,128)}, f32[16,128]{1,0:T(8,128)S(1)}, u32[]{:S(2)}, u32[]{:S(2)}) collective-permute-start(f32[16,128]{1,0:T(8,128)} %get-tuple-element.6), channel_id=1, source_target_pairs={{0,4},{4,8},{8,12},{12,16},{16,20},{20,24},{24,28},{28,0},{1,5},{5... | collective-permute-start | bytes 24584 | tf_op jit(solution)/shard_map/ppermute | solution.py:266
  11.0 4.2 %collective-permute-start.1 = (f32[16,128]{1,0:T(8,128)}, f32[16,128]{1,0:T(8,128)S(1)}, u32[]{:S(2)}, u32[]{:S(2)}) collective-permute-start(f32[16,128]{1,0:T(8,128)} %get-tuple-element.7), channel_id=1, source_target_pairs={{4,0},{8,4},{12,8},{16,12},{20,16},{24,20},{28,24},{0,28},{5,1},{9... | collective-permute-start | bytes 24584 | tf_op jit(solution)/shard_map/ppermute | solution.py:269
  15.2 1.8 %collective-permute-done.hw_ref = f32[16,128]{1,0:T(8,128)S(1)} collective-permute-done((f32[16,128]{1,0:T(8,128)}, f32[16,128]{1,0:T(8,128)S(1)}, u32[]{:S(2)}, u32[]{:S(2)}) %collective-permute-start) | collective-permute-done | bytes 8224 | tf_op jit(solution)/shard_map/ppermute | solution.py:266
  17.1 0.0 copy-start.2
  17.1 0.0 collective-permute-done.1.he_ref
  17.1 0.0 copy-start.3
  17.1 0.0 collective-permute-done.2.first_ref
  17.1 0.0 copy-start
  17.1 0.0 collective-permute-done.3.second_ref
  17.1 0.6 %copy-done.2 = f32[16,128]{1,0:T(8,128)} copy-done((f32[16,128]{1,0:T(8,128)}, f32[16,128]{1,0:T(8,128)S(1)}, u32[]{:S(2)}) %copy-start.2) | copy-done | bytes 8216
  17.6 0.0 copy-done.3
  17.7 0.0 copy-done
  17.7 0.0 copy-start.1
  17.7 0.6 %copy-done.1 = f32[76,256]{1,0:T(8,128)} copy-done((f32[76,256]{1,0:T(8,128)}, f32[76,256]{1,0:T(8,128)S(1)}, u32[]{:S(2)}) %copy-start.1) | copy-done | bytes 77848
  18.3 10.5 %shard_map.87 = (f32[25,16,256]{2,1,0:T(8,128)}, f32[25,16,256]{2,1,0:T(8,128)}) custom-call(s32[2]{0:T(128)} %pad_add_fusion.flag_ref, f32[25,16,256]{2,1,0:T(8,128)} %t_ref.3, f32[25,16,256]{2,1,0:T(8,128)} %s_ref.3, f32[25,16,256]{2,1,0:T(8,128)} %u_ref.3, f32[25,16,256]{2,1,0:T(8,128)} %v_ref.3, f32[25,16,256]{2,1,0:T(8,128)} %w_ref.1, ...), custom_call_target="tpu_custom_call" | custom-call | tf_op jit(solution)/shard_map/pallas_call | solution.py:289
Async XLA Ops:
  4.4 12.7 %collective-permute-start.2 = (f32[76,256]{1,0:T(8,128)}, f32[76,256]{1,0:T(8,128)S(1)}, u32[]{:S(2)}, u32[]{:S(2)}) collective-permute-start(f32[76,256]{1,0:T(8,128)} %get-tuple-element.8), channel_id=1, source_target_pairs={{1,2},{2,1},{3,31},{5,6},{6,5},{7,27},{9,10},{10,9},{11,23},{13,14... | collective-permute-start | bytes 233480 | tf_op jit(solution)/shard_map/ppermute | solution.py:286
  6.3 10.8 %collective-permute-start.3 = (f32[76,256]{1,0:T(8,128)}, f32[76,256]{1,0:T(8,128)S(1)}, u32[]{:S(2)}, u32[]{:S(2)}) collective-permute-start(f32[76,256]{1,0:T(8,128)} %get-tuple-element.9), channel_id=1, source_target_pairs={{0,1},{1,0},{2,3},{3,2},{4,5},{5,4},{6,7},{7,6},{8,9},{9,8},{10,11... | collective-permute-start | bytes 233480 | tf_op jit(solution)/shard_map/ppermute | solution.py:287
  10.5 6.6 %collective-permute-start = (f32[16,128]{1,0:T(8,128)}, f32[16,128]{1,0:T(8,128)S(1)}, u32[]{:S(2)}, u32[]{:S(2)}) collective-permute-start(f32[16,128]{1,0:T(8,128)} %get-tuple-element.6), channel_id=1, source_target_pairs={{0,4},{4,8},{8,12},{12,16},{16,20},{20,24},{24,28},{28,0},{1,5},{5... | collective-permute-start | bytes 24584 | tf_op jit(solution)/shard_map/ppermute | solution.py:266
  11.0 6.1 %collective-permute-start.1 = (f32[16,128]{1,0:T(8,128)}, f32[16,128]{1,0:T(8,128)S(1)}, u32[]{:S(2)}, u32[]{:S(2)}) collective-permute-start(f32[16,128]{1,0:T(8,128)} %get-tuple-element.7), channel_id=1, source_target_pairs={{4,0},{8,4},{12,8},{16,12},{20,16},{24,20},{28,24},{0,28},{5,1},{9... | collective-permute-start | bytes 24584 | tf_op jit(solution)/shard_map/ppermute | solution.py:269
  17.1 0.6 %copy-start.2 = (f32[16,128]{1,0:T(8,128)}, f32[16,128]{1,0:T(8,128)S(1)}, u32[]{:S(2)}) copy-start(f32[16,128]{1,0:T(8,128)S(1)} %collective-permute-done.hw_ref) | copy-start | bytes 24580
  17.1 0.6 %copy-start.3 = (f32[16,128]{1,0:T(8,128)}, f32[16,128]{1,0:T(8,128)S(1)}, u32[]{:S(2)}) copy-start(f32[16,128]{1,0:T(8,128)S(1)} %collective-permute-done.1.he_ref) | copy-start | bytes 24580
  17.1 0.6 %copy-start = (f32[76,256]{1,0:T(8,128)}, f32[76,256]{1,0:T(8,128)S(1)}, u32[]{:S(2)}) copy-start(f32[76,256]{1,0:T(8,128)S(1)} %collective-permute-done.2.first_ref) | copy-start | bytes 233476
  17.7 0.6 %copy-start.1 = (f32[76,256]{1,0:T(8,128)}, f32[76,256]{1,0:T(8,128)S(1)}, u32[]{:S(2)}) copy-start(f32[76,256]{1,0:T(8,128)S(1)} %collective-permute-done.3.second_ref) | copy-start | bytes 233476

commit v5 on v4

--- a/solution.py
+++ b/solution.py
@@ -95,23 +95,35 @@
             jnp.where(jnp.logical_and(inside, level < dsh[i]), 1.0, 0.0) for i in range(5)
         ]
 
-    def horizontal(fields, kcs, wet, a, b, speed_a, speed_b, slope_of):
-        face = wet[a] * wet[b]
+    sub_tile = 8
+
+    def whole(x):
+        return x
+
+    def west_part(x):
+        return x[:, :lane_tile]
+
+    def south_part(x):
+        return x[:sub_tile, :]
+
+    def horizontal(fields, kcs, wet, a, b, speed_a, speed_b, part):
+        face = part(wet[a]) * part(wet[b])
         temp, salt, rho = fields
         k_temp, k_salt, k_rho = kcs
         slope = jnp.clip(
-            -((rho[b] - rho[a]) * face)
+            -((part(rho[b]) - part(rho[a])) * face)
             / jnp.maximum(0.5 * (k_rho[a] + k_rho[b]), DENSITY_FLOOR),
             -SLOPE_LIMIT,
             SLOPE_LIMIT,
         )
-        flow = 0.5 * (speed_a + speed_b) * face
+        flow = 0.5 * (part(speed_a) + part(speed_b)) * face
         up, down = jnp.maximum(flow, 0.0), jnp.minimum(flow, 0.0)
         out = []
         for x, kx in ((temp, k_temp), (salt, k_salt)):
-            grad = (x[b] - x[a]) * face
+            xa, xb = part(x[a]), part(x[b])
+            grad = (xb - xa) * face
             out.append(
-                up * x[a] + down * x[b]
+                up * xa + down * xb
                 - DIFFUSIVITY * face * (grad + slope * (0.5 * (kx[a] + kx[b])))
             )
         return out
@@ -122,6 +134,12 @@
         north_grad = (x[3] - x[0]) * (wet[0] * wet[3])
         south_grad = (x[0] - x[4]) * (wet[4] * wet[0])
         return 0.5 * (west_grad + east_grad), 0.5 * (south_grad + north_grad)
+
+    def vertical_mean(lo, h, up, face_top, face_bottom, i, part):
+        return 0.5 * (
+            (part(h[i]) - part(lo[i])) * part(face_top[i])
+            + (part(up[i]) - part(h[i])) * part(face_bottom[i])
+        )
 
     def level_step(k, carry):
         down_temp, down_salt = carry
@@ -133,19 +151,41 @@
         wet_upper = wet_at(k + 1)
         face_top = [wet_here[i] * wet_lower[i] for i in range(5)]
         face_bottom = [wet_upper[i] * wet_here[i] for i in range(5)]
-        kcs = [
-            [
-                0.5 * ((h[i] - lo[i]) * face_top[i] + (up[i] - h[i]) * face_bottom[i])
-                for i in range(5)
+
+        def kc_set(i, part):
+            return [
+                vertical_mean(lo, h, up, face_top, face_bottom, i, part)
+                for lo, h, up in zip(lower, here, upper)
             ]
-            for lo, h, up in zip(lower, here, upper)
-        ]
+
+        kc_full = [kc_set(i, whole) for i in (0, 1, 3)]
+        kcs = [[kc_full[0][n], kc_full[1][n], None, kc_full[2][n], None] for n in range(3)]
+        west_kcs = [[kc_set(0, west_part)[n], None, kc_set(2, west_part)[n], None, None] for n in range(3)]
+        south_kcs = [[kc_set(0, south_part)[n], None, None, None, kc_set(4, south_part)[n]] for n in range(3)]
         zonal = u_ref[k]
         meridional = v_ref[k]
-        east = horizontal(here, kcs, wet_here, 0, 1, zonal, ush[0, k], None)
-        west = horizontal(here, kcs, wet_here, 2, 0, ush[1, k], zonal, None)
-        north = horizontal(here, kcs, wet_here, 0, 3, meridional, vsh[0, k], None)
-        south = horizontal(here, kcs, wet_here, 4, 0, vsh[1, k], meridional, None)
+        east = horizontal(here, kcs, wet_here, 0, 1, zonal, ush[0, k], whole)
+        west_edge_flux = horizontal(here, west_kcs, wet_here, 2, 0, ush[1, k], zonal, west_part)
+        north = horizontal(here, kcs, wet_here, 0, 3, meridional, vsh[0, k], whole)
+        south_edge_flux = horizontal(
+            here, south_kcs, wet_here, 4, 0, vsh[1, k], meridional, south_part
+        )
+        west = [
+            jnp.where(
+                west_edge,
+                jnp.concatenate([w] * (cols // lane_tile), 1),
+                pltpu.roll(f, 1, 1),
+            )
+            for w, f in zip(west_edge_flux, east)
+        ]
+        south = [
+            jnp.where(
+                south_edge,
+                jnp.concatenate([s] * (rows // sub_tile), 0),
+                pltpu.roll(f, 1, 0),
+            )
+            for s, f in zip(south_edge_flux, north)
+        ]
         means_here = [cell_means(f, wet_here) for f in here]
         means_upper = [cell_means(f, wet_upper) for f in upper]
         face = face_bottom[0]

time: 29.2 us -> 28.2 us (0.966)
  Pallas kernels: 13.7 us -> 12.7 us
    pallas_call x1, Pallas kernels: 10.5 us -> 9.56 us  [on_device(): pl.pallas_call(stencil_kernel, out_shape=(field, field), in_specs=[pl.Blo...]
where the time goes in v5:
time: 28.2 us; the launch traced here: 27.9 us
  Pallas kernels  12.7 us (45%)
  starting transfers between devices  10.8 us (38%)
  waiting for transfers between devices  1.84 us (7%)
  local copies, waits for them, and re-layouts  1.24 us (4%)
  between operations  0.68 us (2%)
  other arithmetic  0.59 us (2%)
    pallas_call x1, Pallas kernels, on_device(): pl.pallas_call(stencil_kernel, out_shape=(field, field), in_specs=[pl.Blo...  9.56 us
    ppermute x1, starting transfers between devices, on_device(): lax.ppermute(east_pack, 'lon', [((i + 1) % lon_count, i) for i in range(l...  4.22 us
    ppermute x1, starting transfers between devices, on_device(): second_got = lax.ppermute(second_lines, ('lon', 'lat'), second_pairs)  4.17 us
    pallas_call x1, Pallas kernels, on_device(): pl.pallas_call(edge_kernel, out_shape=(packed, packed, lines, lines), in_...  3.18 us
    ppermute x1, starting transfers between devices, on_device(): first_got = lax.ppermute(first_lines, ('lon', 'lat'), first_pairs)  1.91 us
    ppermute x1, waiting for transfers between devices, on_device(): lax.ppermute(west_pack, 'lon', [(i, (i + 1) % lon_count) for i in range(l...  1.83 us
    unnamed x8, local copies, waits for them, and re-layouts  1.24 us
    another operation x1, other arithmetic, on_device(): flag = jnp.stack([odd, top_row.astype(jnp.int32)]).astype(jnp.int32)  0.59 us
  transfers between devices with their start and end apart: 4, of which 1 were waited for; matrix products, arithmetic and copies ran while one was open for 0% of the time, Pallas kernels for 0%

profile of v5, /device:TPU:2, one launch (start us, length us, event | category | flops | bytes accessed | tf_op | source)
XLA Modules:
  0.0 27.9 jit_solution(1357248777221686782)
XLA Ops:
  0.6 0.6 %pad_add_fusion.flag_ref = s32[2]{0:T(128)} fusion(s32[1]{0:T(128)} %bitcast.1, s32[1]{0:T(128)} %bitcast), kind=kLoop, calls=%fused_computation | loop fusion | flops 2 | bytes 16 | tf_op jit(solution)/shard_map/stack | solution.py:282
  1.2 3.2 %shard_map.86 = (f32[16,128]{1,0:T(8,128)}, f32[16,128]{1,0:T(8,128)}, f32[76,256]{1,0:T(8,128)}, f32[76,256]{1,0:T(8,128)}) custom-call(s32[2]{0:T(128)} %pad_add_fusion.flag_ref, f32[25,16,256]{2,1,0:T(8,128)} %t_ref.3, f32[25,16,256]{2,1,0:T(8,128)} %s_ref.3, f32[25,16,256]{2,1,0:T(8,128)} %u_ref.3, f32[25,16,256]{2,1,0:T(8,128)} %v_ref.3, ...), custom_call_target="tpu_custom_call" | custom-call | tf_op jit(solution)/shard_map/pallas_call | solution.py:287
  4.4 1.9 %collective-permute-start.2 = (f32[76,256]{1,0:T(8,128)}, f32[76,256]{1,0:T(8,128)S(1)}, u32[]{:S(2)}, u32[]{:S(2)}) collective-permute-start(f32[76,256]{1,0:T(8,128)} %get-tuple-element.8), channel_id=1, source_target_pairs={{1,2},{2,1},{3,31},{5,6},{6,5},{7,27},{9,10},{10,9},{11,23},{13,14... | collective-permute-start | bytes 233480 | tf_op jit(solution)/shard_map/ppermute | solution.py:326
  6.3 4.2 %collective-permute-start.3 = (f32[76,256]{1,0:T(8,128)}, f32[76,256]{1,0:T(8,128)S(1)}, u32[]{:S(2)}, u32[]{:S(2)}) collective-permute-start(f32[76,256]{1,0:T(8,128)} %get-tuple-element.9), channel_id=1, source_target_pairs={{0,1},{1,0},{2,3},{3,2},{4,5},{5,4},{6,7},{7,6},{8,9},{9,8},{10,11... | collective-permute-start | bytes 233480 | tf_op jit(solution)/shard_map/ppermute | solution.py:327
  10.5 0.5 %collective-permute-start = (f32[16,128]{1,0:T(8,128)}, f32[16,128]{1,0:T(8,128)S(1)}, u32[]{:S(2)}, u32[]{:S(2)}) collective-permute-start(f32[16,128]{1,0:T(8,128)} %get-tuple-element.6), channel_id=1, source_target_pairs={{0,4},{4,8},{8,12},{12,16},{16,20},{20,24},{24,28},{28,0},{1,5},{5... | collective-permute-start | bytes 24584 | tf_op jit(solution)/shard_map/ppermute | solution.py:306
  11.0 4.2 %collective-permute-start.1 = (f32[16,128]{1,0:T(8,128)}, f32[16,128]{1,0:T(8,128)S(1)}, u32[]{:S(2)}, u32[]{:S(2)}) collective-permute-start(f32[16,128]{1,0:T(8,128)} %get-tuple-element.7), channel_id=1, source_target_pairs={{4,0},{8,4},{12,8},{16,12},{20,16},{24,20},{28,24},{0,28},{5,1},{9... | collective-permute-start | bytes 24584 | tf_op jit(solution)/shard_map/ppermute | solution.py:309
  15.2 1.8 %collective-permute-done.hw_ref = f32[16,128]{1,0:T(8,128)S(1)} collective-permute-done((f32[16,128]{1,0:T(8,128)}, f32[16,128]{1,0:T(8,128)S(1)}, u32[]{:S(2)}, u32[]{:S(2)}) %collective-permute-start) | collective-permute-done | bytes 8224 | tf_op jit(solution)/shard_map/ppermute | solution.py:306
  17.1 0.0 copy-start.2
  17.1 0.0 collective-permute-done.1.he_ref
  17.1 0.0 copy-start.3
  17.1 0.0 collective-permute-done.2.first_ref
  17.1 0.0 copy-start
  17.1 0.0 collective-permute-done.3.second_ref
  17.1 0.6 %copy-done.2 = f32[16,128]{1,0:T(8,128)} copy-done((f32[16,128]{1,0:T(8,128)}, f32[16,128]{1,0:T(8,128)S(1)}, u32[]{:S(2)}) %copy-start.2) | copy-done | bytes 8216
  17.6 0.0 copy-done.3
  17.7 0.0 copy-done
  17.7 0.0 copy-start.1
  17.7 0.6 %copy-done.1 = f32[76,256]{1,0:T(8,128)} copy-done((f32[76,256]{1,0:T(8,128)}, f32[76,256]{1,0:T(8,128)S(1)}, u32[]{:S(2)}) %copy-start.1) | copy-done | bytes 77848
  18.3 9.6 %shard_map.87 = (f32[25,16,256]{2,1,0:T(8,128)}, f32[25,16,256]{2,1,0:T(8,128)}) custom-call(s32[2]{0:T(128)} %pad_add_fusion.flag_ref, f32[25,16,256]{2,1,0:T(8,128)} %t_ref.3, f32[25,16,256]{2,1,0:T(8,128)} %s_ref.3, f32[25,16,256]{2,1,0:T(8,128)} %u_ref.3, f32[25,16,256]{2,1,0:T(8,128)} %v_ref.3, f32[25,16,256]{2,1,0:T(8,128)} %w_ref.1, ...), custom_call_target="tpu_custom_call" | custom-call | tf_op jit(solution)/shard_map/pallas_call | solution.py:329
Async XLA Ops:
  4.4 12.7 %collective-permute-start.2 = (f32[76,256]{1,0:T(8,128)}, f32[76,256]{1,0:T(8,128)S(1)}, u32[]{:S(2)}, u32[]{:S(2)}) collective-permute-start(f32[76,256]{1,0:T(8,128)} %get-tuple-element.8), channel_id=1, source_target_pairs={{1,2},{2,1},{3,31},{5,6},{6,5},{7,27},{9,10},{10,9},{11,23},{13,14... | collective-permute-start | bytes 233480 | tf_op jit(solution)/shard_map/ppermute | solution.py:326
  6.3 10.8 %collective-permute-start.3 = (f32[76,256]{1,0:T(8,128)}, f32[76,256]{1,0:T(8,128)S(1)}, u32[]{:S(2)}, u32[]{:S(2)}) collective-permute-start(f32[76,256]{1,0:T(8,128)} %get-tuple-element.9), channel_id=1, source_target_pairs={{0,1},{1,0},{2,3},{3,2},{4,5},{5,4},{6,7},{7,6},{8,9},{9,8},{10,11... | collective-permute-start | bytes 233480 | tf_op jit(solution)/shard_map/ppermute | solution.py:327
  10.5 6.6 %collective-permute-start = (f32[16,128]{1,0:T(8,128)}, f32[16,128]{1,0:T(8,128)S(1)}, u32[]{:S(2)}, u32[]{:S(2)}) collective-permute-start(f32[16,128]{1,0:T(8,128)} %get-tuple-element.6), channel_id=1, source_target_pairs={{0,4},{4,8},{8,12},{12,16},{16,20},{20,24},{24,28},{28,0},{1,5},{5... | collective-permute-start | bytes 24584 | tf_op jit(solution)/shard_map/ppermute | solution.py:306
  11.0 6.1 %collective-permute-start.1 = (f32[16,128]{1,0:T(8,128)}, f32[16,128]{1,0:T(8,128)S(1)}, u32[]{:S(2)}, u32[]{:S(2)}) collective-permute-start(f32[16,128]{1,0:T(8,128)} %get-tuple-element.7), channel_id=1, source_target_pairs={{4,0},{8,4},{12,8},{16,12},{20,16},{24,20},{28,24},{0,28},{5,1},{9... | collective-permute-start | bytes 24584 | tf_op jit(solution)/shard_map/ppermute | solution.py:309
  17.1 0.6 %copy-start.2 = (f32[16,128]{1,0:T(8,128)}, f32[16,128]{1,0:T(8,128)S(1)}, u32[]{:S(2)}) copy-start(f32[16,128]{1,0:T(8,128)S(1)} %collective-permute-done.hw_ref) | copy-start | bytes 24580
  17.1 0.6 %copy-start.3 = (f32[16,128]{1,0:T(8,128)}, f32[16,128]{1,0:T(8,128)S(1)}, u32[]{:S(2)}) copy-start(f32[16,128]{1,0:T(8,128)S(1)} %collective-permute-done.1.he_ref) | copy-start | bytes 24580
  17.1 0.6 %copy-start = (f32[76,256]{1,0:T(8,128)}, f32[76,256]{1,0:T(8,128)S(1)}, u32[]{:S(2)}) copy-start(f32[76,256]{1,0:T(8,128)S(1)} %collective-permute-done.2.first_ref) | copy-start | bytes 233476
  17.7 0.6 %copy-start.1 = (f32[76,256]{1,0:T(8,128)}, f32[76,256]{1,0:T(8,128)S(1)}, u32[]{:S(2)}) copy-start(f32[76,256]{1,0:T(8,128)S(1)} %collective-permute-done.3.second_ref) | copy-start | bytes 233476

commit v6 on v5

--- a/solution.py
+++ b/solution.py
@@ -13,10 +13,31 @@
 
 
 def stencil_kernel(
-    flag_ref, t_ref, s_ref, u_ref, v_ref, w_ref, wi_ref, sb_ref, hw_ref, he_ref,
-    first_ref, second_ref, ot_ref, os_ref, tsh, ssh, ush, vsh, dsh,
+    flag_ref, t_hbm, s_hbm, u_hbm, v_hbm, w_hbm, wi_ref, sb_ref, hw_hbm, he_hbm,
+    first_hbm, second_hbm, ot_ref, os_ref, tsh, ssh, ush, vsh, dsh,
+    t_ref, s_ref, u_ref, v_ref, w_ref, hw_ref, he_ref, first_ref, second_ref, sems,
 ):
     layer_total, rows, cols = t_ref.shape
+    copies = [
+        pltpu.make_async_copy(source, target, sems.at[n])
+        for n, (source, target) in enumerate(
+            (
+                (hw_hbm, hw_ref),
+                (he_hbm, he_ref),
+                (first_hbm, first_ref),
+                (second_hbm, second_ref),
+                (t_hbm, t_ref),
+                (s_hbm, s_ref),
+                (u_hbm, u_ref),
+                (v_hbm, v_ref),
+                (w_hbm, w_ref),
+            )
+        )
+    ]
+    for copy in copies:
+        copy.start()
+    for copy in copies[:6]:
+        copy.wait()
     lane = lax.broadcasted_iota(jnp.int32, (rows, cols), 1)
     row = lax.broadcasted_iota(jnp.int32, (rows, cols), 0)
     east_edge = lane == cols - 1
@@ -74,6 +95,9 @@
             dst[1, k] = west_of(x, west_halo(base + k))
             dst[2, k] = north_of(x, north_halo(base + k))
             dst[3, k] = south_of(x, south_halo(base + k))
+    copies[6].wait()
+    copies[7].wait()
+    for k in range(layer_total):
         x = u_ref[k]
         ush[0, k] = east_of(x, east_halo(depth_plane + 1 + k))
         ush[1, k] = west_of(x, west_halo(depth_plane + 1 + k))
@@ -211,6 +235,7 @@
             dst[k] = here[n][0] - divergence
         return tuple(below)
 
+    copies[8].wait()
     zero = jnp.zeros((rows, cols), jnp.float32)
     lax.fori_loop(0, layer_total, level_step, (zero, zero))
 
@@ -329,7 +354,10 @@
     return pl.pallas_call(
         stencil_kernel,
         out_shape=(field, field),
-        in_specs=[pl.BlockSpec(memory_space=smem)] + [pl.BlockSpec(memory_space=vmem)] * 11,
+        in_specs=[pl.BlockSpec(memory_space=smem)]
+        + [pl.BlockSpec(memory_space=pl.ANY)] * 5
+        + [pl.BlockSpec(memory_space=vmem)] * 2
+        + [pl.BlockSpec(memory_space=pl.ANY)] * 4,
         out_specs=(pl.BlockSpec(memory_space=vmem), pl.BlockSpec(memory_space=vmem)),
         scratch_shapes=[
             pltpu.VMEM((4, layer_total, rows, cols), jnp.float32),
@@ -337,7 +365,11 @@
             pltpu.VMEM((2, layer_total, rows, cols), jnp.float32),
             pltpu.VMEM((2, layer_total, rows, cols), jnp.float32),
             pltpu.VMEM((5, rows, cols), jnp.float32),
-        ],
+        ]
+        + [pltpu.VMEM(potential_warmth.shape, jnp.float32)] * 5
+        + [pltpu.VMEM(west_cols.shape, jnp.float32)] * 2
+        + [pltpu.VMEM(first_got.shape, jnp.float32)] * 2
+        + [pltpu.SemaphoreType.DMA((9,))],
     )(
         flag,
         potential_warmth,

time: 28.2 us -> 28.9 us (1.025)
  Pallas kernels: 12.7 us -> 13.3 us
    pallas_call x1, Pallas kernels: 9.56 us -> 10.1 us  [on_device(): pl.pallas_call(stencil_kernel, out_shape=(field, field), in_specs=[pl.Blo...]
where the time goes in v6:
time: 28.9 us; the launch traced here: 28.4 us
  Pallas kernels  13.3 us (46%)
  starting transfers between devices  10.8 us (37%)
  waiting for transfers between devices  1.84 us (6%)
  local copies, waits for them, and re-layouts  1.24 us (4%)
  between operations  0.68 us (2%)
  other arithmetic  0.59 us (2%)
    pallas_call x1, Pallas kernels, on_device(): pl.pallas_call(stencil_kernel, out_shape=(field, field), in_specs=[pl.Blo...  10.1 us
    ppermute x1, starting transfers between devices, on_device(): lax.ppermute(east_pack, 'lon', [((i + 1) % lon_count, i) for i in range(l...  4.22 us
    ppermute x1, starting transfers between devices, on_device(): second_got = lax.ppermute(second_lines, ('lon', 'lat'), second_pairs)  4.17 us
    pallas_call x1, Pallas kernels, on_device(): pl.pallas_call(edge_kernel, out_shape=(packed, packed, lines, lines), in_...  3.18 us
    ppermute x1, starting transfers between devices, on_device(): first_got = lax.ppermute(first_lines, ('lon', 'lat'), first_pairs)  1.91 us
    ppermute x1, waiting for transfers between devices, on_device(): lax.ppermute(west_pack, 'lon', [(i, (i + 1) % lon_count) for i in range(l...  1.83 us
    unnamed x8, local copies, waits for them, and re-layouts  1.24 us
    another operation x1, other arithmetic, on_device(): flag = jnp.stack([odd, top_row.astype(jnp.int32)]).astype(jnp.int32)  0.59 us
  transfers between devices with their start and end apart: 4, of which 1 were waited for; matrix products, arithmetic and copies ran while one was open for 0% of the time, Pallas kernels for 0%

profile of v6, /device:TPU:2, one launch (start us, length us, event | category | flops | bytes accessed | tf_op | source)
XLA Modules:
  0.0 28.4 jit_solution(7414803034730801078)
XLA Ops:
  0.6 0.6 %pad_add_fusion.flag_ref = s32[2]{0:T(128)} fusion(s32[1]{0:T(128)} %bitcast.1, s32[1]{0:T(128)} %bitcast), kind=kLoop, calls=%fused_computation | loop fusion | flops 2 | bytes 16 | tf_op jit(solution)/shard_map/stack | solution.py:307
  1.2 3.2 %shard_map.86 = (f32[16,128]{1,0:T(8,128)}, f32[16,128]{1,0:T(8,128)}, f32[76,256]{1,0:T(8,128)}, f32[76,256]{1,0:T(8,128)}) custom-call(s32[2]{0:T(128)} %pad_add_fusion.flag_ref, f32[25,16,256]{2,1,0:T(8,128)} %t_hbm.1, f32[25,16,256]{2,1,0:T(8,128)} %s_hbm.1, f32[25,16,256]{2,1,0:T(8,128)} %u_hbm.1, f32[25,16,256]{2,1,0:T(8,128)} %v_hbm.1, ...), custom_call_target="tpu_custom_call" | custom-call | tf_op jit(solution)/shard_map/pallas_call | solution.py:312
  4.4 1.9 %collective-permute-start.2 = (f32[76,256]{1,0:T(8,128)}, f32[76,256]{1,0:T(8,128)S(1)}, u32[]{:S(2)}, u32[]{:S(2)}) collective-permute-start(f32[76,256]{1,0:T(8,128)} %get-tuple-element.8), channel_id=1, source_target_pairs={{1,2},{2,1},{3,31},{5,6},{6,5},{7,27},{9,10},{10,9},{11,23},{13,14... | collective-permute-start | bytes 233480 | tf_op jit(solution)/shard_map/ppermute | solution.py:351
  6.3 4.2 %collective-permute-start.3 = (f32[76,256]{1,0:T(8,128)}, f32[76,256]{1,0:T(8,128)S(1)}, u32[]{:S(2)}, u32[]{:S(2)}) collective-permute-start(f32[76,256]{1,0:T(8,128)} %get-tuple-element.9), channel_id=1, source_target_pairs={{0,1},{1,0},{2,3},{3,2},{4,5},{5,4},{6,7},{7,6},{8,9},{9,8},{10,11... | collective-permute-start | bytes 233480 | tf_op jit(solution)/shard_map/ppermute | solution.py:352
  10.5 0.5 %collective-permute-start = (f32[16,128]{1,0:T(8,128)}, f32[16,128]{1,0:T(8,128)S(1)}, u32[]{:S(2)}, u32[]{:S(2)}) collective-permute-start(f32[16,128]{1,0:T(8,128)} %get-tuple-element.6), channel_id=1, source_target_pairs={{0,4},{4,8},{8,12},{12,16},{16,20},{20,24},{24,28},{28,0},{1,5},{5... | collective-permute-start | bytes 24584 | tf_op jit(solution)/shard_map/ppermute | solution.py:331
  11.0 4.2 %collective-permute-start.1 = (f32[16,128]{1,0:T(8,128)}, f32[16,128]{1,0:T(8,128)S(1)}, u32[]{:S(2)}, u32[]{:S(2)}) collective-permute-start(f32[16,128]{1,0:T(8,128)} %get-tuple-element.7), channel_id=1, source_target_pairs={{4,0},{8,4},{12,8},{16,12},{20,16},{24,20},{28,24},{0,28},{5,1},{9... | collective-permute-start | bytes 24584 | tf_op jit(solution)/shard_map/ppermute | solution.py:334
  15.2 1.8 %collective-permute-done.hw_hbm = f32[16,128]{1,0:T(8,128)S(1)} collective-permute-done((f32[16,128]{1,0:T(8,128)}, f32[16,128]{1,0:T(8,128)S(1)}, u32[]{:S(2)}, u32[]{:S(2)}) %collective-permute-start) | collective-permute-done | bytes 8224 | tf_op jit(solution)/shard_map/ppermute | solution.py:331
  17.1 0.0 copy-start.2
  17.1 0.0 collective-permute-done.1.he_hbm
  17.1 0.0 copy-start.3
  17.1 0.0 collective-permute-done.2.first_hbm
  17.1 0.0 copy-start
  17.1 0.0 collective-permute-done.3.second_hbm
  17.1 0.6 %copy-done.2 = f32[16,128]{1,0:T(8,128)} copy-done((f32[16,128]{1,0:T(8,128)}, f32[16,128]{1,0:T(8,128)S(1)}, u32[]{:S(2)}) %copy-start.2) | copy-done | bytes 8216
  17.6 0.0 copy-done.3
  17.7 0.0 copy-done
  17.7 0.0 copy-start.1
  17.7 0.6 %copy-done.1 = f32[76,256]{1,0:T(8,128)} copy-done((f32[76,256]{1,0:T(8,128)}, f32[76,256]{1,0:T(8,128)S(1)}, u32[]{:S(2)}) %copy-start.1) | copy-done | bytes 77848
  18.3 10.1 %shard_map.87 = (f32[25,16,256]{2,1,0:T(8,128)}, f32[25,16,256]{2,1,0:T(8,128)}) custom-call(s32[2]{0:T(128)} %pad_add_fusion.flag_ref, f32[25,16,256]{2,1,0:T(8,128)} %t_hbm.1, f32[25,16,256]{2,1,0:T(8,128)} %s_hbm.1, f32[25,16,256]{2,1,0:T(8,128)} %u_hbm.1, f32[25,16,256]{2,1,0:T(8,128)} %v_hbm.1, f32[25,16,256]{2,1,0:T(8,128)} %w_hbm.1, ...), custom_call_target="tpu_custom_call" | custom-call | tf_op jit(solution)/shard_map/pallas_call | solution.py:354
Async XLA Ops:
  4.4 12.7 %collective-permute-start.2 = (f32[76,256]{1,0:T(8,128)}, f32[76,256]{1,0:T(8,128)S(1)}, u32[]{:S(2)}, u32[]{:S(2)}) collective-permute-start(f32[76,256]{1,0:T(8,128)} %get-tuple-element.8), channel_id=1, source_target_pairs={{1,2},{2,1},{3,31},{5,6},{6,5},{7,27},{9,10},{10,9},{11,23},{13,14... | collective-permute-start | bytes 233480 | tf_op jit(solution)/shard_map/ppermute | solution.py:351
  6.3 10.8 %collective-permute-start.3 = (f32[76,256]{1,0:T(8,128)}, f32[76,256]{1,0:T(8,128)S(1)}, u32[]{:S(2)}, u32[]{:S(2)}) collective-permute-start(f32[76,256]{1,0:T(8,128)} %get-tuple-element.9), channel_id=1, source_target_pairs={{0,1},{1,0},{2,3},{3,2},{4,5},{5,4},{6,7},{7,6},{8,9},{9,8},{10,11... | collective-permute-start | bytes 233480 | tf_op jit(solution)/shard_map/ppermute | solution.py:352
  10.5 6.6 %collective-permute-start = (f32[16,128]{1,0:T(8,128)}, f32[16,128]{1,0:T(8,128)S(1)}, u32[]{:S(2)}, u32[]{:S(2)}) collective-permute-start(f32[16,128]{1,0:T(8,128)} %get-tuple-element.6), channel_id=1, source_target_pairs={{0,4},{4,8},{8,12},{12,16},{16,20},{20,24},{24,28},{28,0},{1,5},{5... | collective-permute-start | bytes 24584 | tf_op jit(solution)/shard_map/ppermute | solution.py:331
  11.0 6.1 %collective-permute-start.1 = (f32[16,128]{1,0:T(8,128)}, f32[16,128]{1,0:T(8,128)S(1)}, u32[]{:S(2)}, u32[]{:S(2)}) collective-permute-start(f32[16,128]{1,0:T(8,128)} %get-tuple-element.7), channel_id=1, source_target_pairs={{4,0},{8,4},{12,8},{16,12},{20,16},{24,20},{28,24},{0,28},{5,1},{9... | collective-permute-start | bytes 24584 | tf_op jit(solution)/shard_map/ppermute | solution.py:334
  17.1 0.6 %copy-start.2 = (f32[16,128]{1,0:T(8,128)}, f32[16,128]{1,0:T(8,128)S(1)}, u32[]{:S(2)}) copy-start(f32[16,128]{1,0:T(8,128)S(1)} %collective-permute-done.hw_hbm) | copy-start | bytes 24580
  17.1 0.6 %copy-start.3 = (f32[16,128]{1,0:T(8,128)}, f32[16,128]{1,0:T(8,128)S(1)}, u32[]{:S(2)}) copy-start(f32[16,128]{1,0:T(8,128)S(1)} %collective-permute-done.1.he_hbm) | copy-start | bytes 24580
  17.1 0.6 %copy-start = (f32[76,256]{1,0:T(8,128)}, f32[76,256]{1,0:T(8,128)S(1)}, u32[]{:S(2)}) copy-start(f32[76,256]{1,0:T(8,128)S(1)} %collective-permute-done.2.first_hbm) | copy-start | bytes 233476
  17.7 0.6 %copy-start.1 = (f32[76,256]{1,0:T(8,128)}, f32[76,256]{1,0:T(8,128)S(1)}, u32[]{:S(2)}) copy-start(f32[76,256]{1,0:T(8,128)S(1)} %collective-permute-done.3.second_hbm) | copy-start | bytes 233476

commit v7 on v5

--- a/solution.py
+++ b/solution.py
@@ -13,7 +13,7 @@
 
 
 def stencil_kernel(
-    flag_ref, t_ref, s_ref, u_ref, v_ref, w_ref, wi_ref, sb_ref, hw_ref, he_ref,
+    t_ref, s_ref, u_ref, v_ref, w_ref, wi_ref, sb_ref, hw_ref, he_ref,
     first_ref, second_ref, ot_ref, os_ref, tsh, ssh, ush, vsh, dsh,
 ):
     layer_total, rows, cols = t_ref.shape
@@ -51,7 +51,7 @@
     def west_halo(p):
         return column_of(hw_ref, p, 0)
 
-    odd = flag_ref[0] == 1
+    odd = lax.axis_index("lat") % 2 == 1
 
     def north_halo(p):
         return jnp.where(odd, first_ref[p : p + 1, :], second_ref[p : p + 1, :])
@@ -216,13 +216,14 @@
 
 
 def edge_kernel(
-    flag_ref, t_ref, s_ref, u_ref, v_ref, wi_ref, sb_ref,
+    t_ref, s_ref, u_ref, v_ref, wi_ref, sb_ref,
     west_ref, east_ref, first_ref, second_ref, tops_ref, bottoms_ref,
 ):
     layer_total, rows, cols = t_ref.shape
     lane_tile = west_ref.shape[1]
-    odd = flag_ref[0] == 1
-    top = flag_ref[1] == 1
+    lat_index = lax.axis_index("lat")
+    odd = lat_index % 2 == 1
+    top = lat_index == lax.axis_size("lat") - 1
     depth = (wi_ref[...] * sb_ref[...]).astype(jnp.float32)
     lane = lax.broadcasted_iota(jnp.int32, (rows, lane_tile), 1)
     column_planes = (
@@ -278,8 +279,6 @@
     lat_count = lax.axis_size("lat")
     lat_index = lax.axis_index("lat")
     odd = lat_index % 2
-    top_row = lat_index == lat_count - 1
-    flag = jnp.stack([odd, top_row.astype(jnp.int32)]).astype(jnp.int32)
     vmem = pltpu.MemorySpace.VMEM
     smem = pltpu.MemorySpace.SMEM
     packed = jax.ShapeDtypeStruct((rows, lane_tile), jnp.float32)
@@ -287,14 +286,13 @@
     west_pack, east_pack, first_lines, second_lines = pl.pallas_call(
         edge_kernel,
         out_shape=(packed, packed, lines, lines),
-        in_specs=[pl.BlockSpec(memory_space=smem)] + [pl.BlockSpec(memory_space=vmem)] * 6,
+        in_specs=[pl.BlockSpec(memory_space=vmem)] * 6,
         out_specs=tuple(pl.BlockSpec(memory_space=vmem) for _ in range(4)),
         scratch_shapes=[
             pltpu.VMEM((halo_planes, cols), jnp.float32),
             pltpu.VMEM((halo_planes, cols), jnp.float32),
         ],
     )(
-        flag,
         potential_warmth,
         saltiness_anomaly,
         zonal_speed,
@@ -329,7 +327,7 @@
     return pl.pallas_call(
         stencil_kernel,
         out_shape=(field, field),
-        in_specs=[pl.BlockSpec(memory_space=smem)] + [pl.BlockSpec(memory_space=vmem)] * 11,
+        in_specs=[pl.BlockSpec(memory_space=vmem)] * 11,
         out_specs=(pl.BlockSpec(memory_space=vmem), pl.BlockSpec(memory_space=vmem)),
         scratch_shapes=[
             pltpu.VMEM((4, layer_total, rows, cols), jnp.float32),
@@ -339,7 +337,6 @@
             pltpu.VMEM((5, rows, cols), jnp.float32),
         ],
     )(
-        flag,
         potential_warmth,
         saltiness_anomaly,
         zonal_speed,

time: 28.2 us -> 27.7 us (0.982)
  other arithmetic: 0.59 us -> 0 us
    another operation x1 -> x0, other arithmetic: 0.59 us -> none  [on_device(): flag = jnp.stack([odd, top_row.astype(jnp.int32)]).astype(jnp.int32)]
where the time goes in v7:
time: 27.7 us; the launch traced here: 27.3 us
  Pallas kernels  12.8 us (46%)
  starting transfers between devices  10.8 us (39%)
  waiting for transfers between devices  1.84 us (7%)
  local copies, waits for them, and re-layouts  1.24 us (4%)
  between operations  0.66 us (2%)
    pallas_call x1, Pallas kernels, on_device(): pl.pallas_call(stencil_kernel, out_shape=(field, field), in_specs=[pl.Blo...  9.62 us
    ppermute x1, starting transfers between devices, on_device(): lax.ppermute(east_pack, 'lon', [((i + 1) % lon_count, i) for i in range(l...  4.22 us
    ppermute x1, starting transfers between devices, on_device(): second_got = lax.ppermute(second_lines, ('lon', 'lat'), second_pairs)  4.17 us
    pallas_call x1, Pallas kernels, on_device(): pl.pallas_call(edge_kernel, out_shape=(packed, packed, lines, lines), in_...  3.18 us
    ppermute x1, starting transfers between devices, on_device(): first_got = lax.ppermute(first_lines, ('lon', 'lat'), first_pairs)  1.91 us
    ppermute x1, waiting for transfers between devices, on_device(): lax.ppermute(west_pack, 'lon', [(i, (i + 1) % lon_count) for i in range(l...  1.83 us
    unnamed x8, local copies, waits for them, and re-layouts  1.24 us
  transfers between devices with their start and end apart: 4, of which 1 were waited for; matrix products, arithmetic and copies ran while one was open for 0% of the time, Pallas kernels for 0%

profile of v7, /device:TPU:2, one launch (start us, length us, event | category | flops | bytes accessed | tf_op | source)
XLA Modules:
  0.0 27.3 jit_solution(7105480524316795672)
XLA Ops:
  0.6 3.2 %shard_map.86 = (f32[16,128]{1,0:T(8,128)}, f32[16,128]{1,0:T(8,128)}, f32[76,256]{1,0:T(8,128)}, f32[76,256]{1,0:T(8,128)}) custom-call(f32[25,16,256]{2,1,0:T(8,128)} %t_ref.3, f32[25,16,256]{2,1,0:T(8,128)} %s_ref.3, f32[25,16,256]{2,1,0:T(8,128)} %u_ref.3, f32[25,16,256]{2,1,0:T(8,128)} %v_ref.3, s32[16,256]{1,0:T(8,128)} %wi_ref.3, s32[16,256]{1,0:T(8,128)} %sb_ref.3), custom_call_target="tpu_custom_call" | custom-call | tf_op jit(solution)/shard_map/pallas_call | solution.py:286
  3.8 1.9 %collective-permute-start.2 = (f32[76,256]{1,0:T(8,128)}, f32[76,256]{1,0:T(8,128)S(1)}, u32[]{:S(2)}, u32[]{:S(2)}) collective-permute-start(f32[76,256]{1,0:T(8,128)} %get-tuple-element.8), channel_id=1, source_target_pairs={{1,2},{2,1},{3,31},{5,6},{6,5},{7,27},{9,10},{10,9},{11,23},{13,14... | collective-permute-start | bytes 233480 | tf_op jit(solution)/shard_map/ppermute | solution.py:324
  5.7 4.2 %collective-permute-start.3 = (f32[76,256]{1,0:T(8,128)}, f32[76,256]{1,0:T(8,128)S(1)}, u32[]{:S(2)}, u32[]{:S(2)}) collective-permute-start(f32[76,256]{1,0:T(8,128)} %get-tuple-element.9), channel_id=1, source_target_pairs={{0,1},{1,0},{2,3},{3,2},{4,5},{5,4},{6,7},{7,6},{8,9},{9,8},{10,11... | collective-permute-start | bytes 233480 | tf_op jit(solution)/shard_map/ppermute | solution.py:325
  9.9 0.5 %collective-permute-start = (f32[16,128]{1,0:T(8,128)}, f32[16,128]{1,0:T(8,128)S(1)}, u32[]{:S(2)}, u32[]{:S(2)}) collective-permute-start(f32[16,128]{1,0:T(8,128)} %get-tuple-element.6), channel_id=1, source_target_pairs={{0,4},{4,8},{8,12},{12,16},{16,20},{20,24},{24,28},{28,0},{1,5},{5... | collective-permute-start | bytes 24584 | tf_op jit(solution)/shard_map/ppermute | solution.py:304
  10.4 4.2 %collective-permute-start.1 = (f32[16,128]{1,0:T(8,128)}, f32[16,128]{1,0:T(8,128)S(1)}, u32[]{:S(2)}, u32[]{:S(2)}) collective-permute-start(f32[16,128]{1,0:T(8,128)} %get-tuple-element.7), channel_id=1, source_target_pairs={{4,0},{8,4},{12,8},{16,12},{20,16},{24,20},{28,24},{0,28},{5,1},{9... | collective-permute-start | bytes 24584 | tf_op jit(solution)/shard_map/ppermute | solution.py:307
  14.6 1.8 %collective-permute-done.hw_ref = f32[16,128]{1,0:T(8,128)S(1)} collective-permute-done((f32[16,128]{1,0:T(8,128)}, f32[16,128]{1,0:T(8,128)S(1)}, u32[]{:S(2)}, u32[]{:S(2)}) %collective-permute-start) | collective-permute-done | bytes 8224 | tf_op jit(solution)/shard_map/ppermute | solution.py:304
  16.4 0.0 copy-start.2
  16.5 0.0 collective-permute-done.1.he_ref
  16.5 0.0 copy-start.3
  16.5 0.0 collective-permute-done.2.first_ref
  16.5 0.0 copy-start
  16.5 0.0 collective-permute-done.3.second_ref
  16.5 0.6 %copy-done.2 = f32[16,128]{1,0:T(8,128)} copy-done((f32[16,128]{1,0:T(8,128)}, f32[16,128]{1,0:T(8,128)S(1)}, u32[]{:S(2)}) %copy-start.2) | copy-done | bytes 8216
  17.0 0.0 copy-done.3
  17.1 0.0 copy-done
  17.1 0.0 copy-start.1
  17.1 0.6 %copy-done.1 = f32[76,256]{1,0:T(8,128)} copy-done((f32[76,256]{1,0:T(8,128)}, f32[76,256]{1,0:T(8,128)S(1)}, u32[]{:S(2)}) %copy-start.1) | copy-done | bytes 77848
  17.7 9.6 %shard_map.87 = (f32[25,16,256]{2,1,0:T(8,128)}, f32[25,16,256]{2,1,0:T(8,128)}) custom-call(f32[25,16,256]{2,1,0:T(8,128)} %t_ref.3, f32[25,16,256]{2,1,0:T(8,128)} %s_ref.3, f32[25,16,256]{2,1,0:T(8,128)} %u_ref.3, f32[25,16,256]{2,1,0:T(8,128)} %v_ref.3, f32[25,16,256]{2,1,0:T(8,128)} %w_ref.1, s32[16,256]{1,0:T(8,128)} %wi_ref.3, s32[16,256]{1,0:T(8,128)} %sb_ref.3, ...), custom_call_target="tpu_custom_call" | custom-call | tf_op jit(solution)/shard_map/pallas_call | solution.py:327
Async XLA Ops:
  3.8 12.7 %collective-permute-start.2 = (f32[76,256]{1,0:T(8,128)}, f32[76,256]{1,0:T(8,128)S(1)}, u32[]{:S(2)}, u32[]{:S(2)}) collective-permute-start(f32[76,256]{1,0:T(8,128)} %get-tuple-element.8), channel_id=1, source_target_pairs={{1,2},{2,1},{3,31},{5,6},{6,5},{7,27},{9,10},{10,9},{11,23},{13,14... | collective-permute-start | bytes 233480 | tf_op jit(solution)/shard_map/ppermute | solution.py:324
  5.7 10.8 %collective-permute-start.3 = (f32[76,256]{1,0:T(8,128)}, f32[76,256]{1,0:T(8,128)S(1)}, u32[]{:S(2)}, u32[]{:S(2)}) collective-permute-start(f32[76,256]{1,0:T(8,128)} %get-tuple-element.9), channel_id=1, source_target_pairs={{0,1},{1,0},{2,3},{3,2},{4,5},{5,4},{6,7},{7,6},{8,9},{9,8},{10,11... | collective-permute-start | bytes 233480 | tf_op jit(solution)/shard_map/ppermute | solution.py:325
  9.9 6.6 %collective-permute-start = (f32[16,128]{1,0:T(8,128)}, f32[16,128]{1,0:T(8,128)S(1)}, u32[]{:S(2)}, u32[]{:S(2)}) collective-permute-start(f32[16,128]{1,0:T(8,128)} %get-tuple-element.6), channel_id=1, source_target_pairs={{0,4},{4,8},{8,12},{12,16},{16,20},{20,24},{24,28},{28,0},{1,5},{5... | collective-permute-start | bytes 24584 | tf_op jit(solution)/shard_map/ppermute | solution.py:304
  10.4 6.1 %collective-permute-start.1 = (f32[16,128]{1,0:T(8,128)}, f32[16,128]{1,0:T(8,128)S(1)}, u32[]{:S(2)}, u32[]{:S(2)}) collective-permute-start(f32[16,128]{1,0:T(8,128)} %get-tuple-element.7), channel_id=1, source_target_pairs={{4,0},{8,4},{12,8},{16,12},{20,16},{24,20},{28,24},{0,28},{5,1},{9... | collective-permute-start | bytes 24584 | tf_op jit(solution)/shard_map/ppermute | solution.py:307
  16.4 0.6 %copy-start.2 = (f32[16,128]{1,0:T(8,128)}, f32[16,128]{1,0:T(8,128)S(1)}, u32[]{:S(2)}) copy-start(f32[16,128]{1,0:T(8,128)S(1)} %collective-permute-done.hw_ref) | copy-start | bytes 24580
  16.5 0.6 %copy-start.3 = (f32[16,128]{1,0:T(8,128)}, f32[16,128]{1,0:T(8,128)S(1)}, u32[]{:S(2)}) copy-start(f32[16,128]{1,0:T(8,128)S(1)} %collective-permute-done.1.he_ref) | copy-start | bytes 24580
  16.5 0.6 %copy-start = (f32[76,256]{1,0:T(8,128)}, f32[76,256]{1,0:T(8,128)S(1)}, u32[]{:S(2)}) copy-start(f32[76,256]{1,0:T(8,128)S(1)} %collective-permute-done.2.first_ref) | copy-start | bytes 233476
  17.1 0.6 %copy-start.1 = (f32[76,256]{1,0:T(8,128)}, f32[76,256]{1,0:T(8,128)S(1)}, u32[]{:S(2)}) copy-start(f32[76,256]{1,0:T(8,128)S(1)} %collective-permute-done.3.second_ref) | copy-start | bytes 233476

commit v8 on v7

--- a/solution.py
+++ b/solution.py
@@ -216,34 +216,52 @@
 
 
 def edge_kernel(
-    t_ref, s_ref, u_ref, v_ref, wi_ref, sb_ref,
+    t_hbm, s_hbm, u_hbm, v_hbm, wi_ref, sb_ref,
     west_ref, east_ref, first_ref, second_ref, tops_ref, bottoms_ref,
+    t_ref, s_ref, u_ref, v_ref, sems,
 ):
     layer_total, rows, cols = t_ref.shape
+    copies = [
+        pltpu.make_async_copy(source, target, sems.at[n])
+        for n, (source, target) in enumerate(
+            ((t_hbm, t_ref), (s_hbm, s_ref), (u_hbm, u_ref), (v_hbm, v_ref))
+        )
+    ]
+    for copy in copies:
+        copy.start()
     lane_tile = west_ref.shape[1]
     lat_index = lax.axis_index("lat")
     odd = lat_index % 2 == 1
     top = lat_index == lax.axis_size("lat") - 1
     depth = (wi_ref[...] * sb_ref[...]).astype(jnp.float32)
     lane = lax.broadcasted_iota(jnp.int32, (rows, lane_tile), 1)
-    column_planes = (
-        [t_ref[k] for k in range(layer_total)]
-        + [s_ref[k] for k in range(layer_total)]
-        + [depth]
-        + [u_ref[k] for k in range(layer_total)]
-    )
     west = jnp.zeros((rows, lane_tile), jnp.float32)
     east = jnp.zeros((rows, lane_tile), jnp.float32)
-    for p, x in enumerate(column_planes):
-        west = jnp.where(lane == p, x[:, cols - 1 :], west)
-        east = jnp.where(lane == p, x[:, :1], east)
+
+    def edges(x, p, west, east, column, line):
+        if column:
+            west = jnp.where(lane == p, x[:, cols - 1 :], west)
+            east = jnp.where(lane == p, x[:, :1], east)
+        if line:
+            tops_ref[p : p + 1, :] = x[rows - 1 :, :]
+            bottoms_ref[p : p + 1, :] = x[:1, :]
+        return west, east
+
+    base_planes = 2 * layer_total + 1
+    sources = ((t_ref, 0, True, True), (s_ref, layer_total, True, True))
+    for n, (ref, base, column, line) in enumerate(sources):
+        copies[n].wait()
+        for k in range(layer_total):
+            west, east = edges(ref[k], base + k, west, east, column, line)
+    west, east = edges(depth, base_planes - 1, west, east, True, True)
+    copies[2].wait()
+    for k in range(layer_total):
+        west, east = edges(u_ref[k], base_planes + k, west, east, True, False)
     west_ref[...] = west
     east_ref[...] = east
-    base_planes = 2 * layer_total + 1
-    row_planes = column_planes[:base_planes] + [v_ref[k] for k in range(layer_total)]
-    for p, x in enumerate(row_planes):
-        tops_ref[p : p + 1, :] = x[rows - 1 :, :]
-        bottoms_ref[p : p + 1, :] = x[:1, :]
+    copies[3].wait()
+    for k in range(layer_total):
+        west, east = edges(v_ref[k], base_planes + k, west, east, False, True)
     tops = tops_ref[...]
     bottoms = bottoms_ref[...]
     line_lane = lax.broadcasted_iota(jnp.int32, tops.shape, 1)
@@ -286,12 +304,15 @@
     west_pack, east_pack, first_lines, second_lines = pl.pallas_call(
         edge_kernel,
         out_shape=(packed, packed, lines, lines),
-        in_specs=[pl.BlockSpec(memory_space=vmem)] * 6,
+        in_specs=[pl.BlockSpec(memory_space=pltpu.MemorySpace.HBM)] * 4
+        + [pl.BlockSpec(memory_space=vmem)] * 2,
         out_specs=tuple(pl.BlockSpec(memory_space=vmem) for _ in range(4)),
         scratch_shapes=[
             pltpu.VMEM((halo_planes, cols), jnp.float32),
             pltpu.VMEM((halo_planes, cols), jnp.float32),
-        ],
+        ]
+        + [pltpu.VMEM(potential_warmth.shape, jnp.float32)] * 4
+        + [pltpu.SemaphoreType.DMA((4,))],
     )(
         potential_warmth,
         saltiness_anomaly,

time: 27.7 us -> 28.4 us (1.025)
  Pallas kernels: 12.8 us -> 13.4 us
    pallas_call x1, Pallas kernels: 3.18 us -> 3.77 us  [on_device(): pl.pallas_call(edge_kernel, out_shape=(packed, packed, lines, lines), in_...]
where the time goes in v8:
time: 28.4 us; the launch traced here: 27.9 us
  Pallas kernels  13.4 us (47%)
  starting transfers between devices  10.8 us (38%)
  waiting for transfers between devices  1.84 us (6%)
  local copies, waits for them, and re-layouts  1.24 us (4%)
  between operations  0.67 us (2%)
    pallas_call x1, Pallas kernels, on_device(): pl.pallas_call(stencil_kernel, out_shape=(field, field), in_specs=[pl.Blo...  9.62 us
    ppermute x1, starting transfers between devices, on_device(): lax.ppermute(east_pack, 'lon', [((i + 1) % lon_count, i) for i in range(l...  4.22 us
    ppermute x1, starting transfers between devices, on_device(): second_got = lax.ppermute(second_lines, ('lon', 'lat'), second_pairs)  4.17 us
    pallas_call x1, Pallas kernels, on_device(): pl.pallas_call(edge_kernel, out_shape=(packed, packed, lines, lines), in_...  3.77 us
    ppermute x1, starting transfers between devices, on_device(): first_got = lax.ppermute(first_lines, ('lon', 'lat'), first_pairs)  1.92 us
    ppermute x1, waiting for transfers between devices, on_device(): lax.ppermute(west_pack, 'lon', [(i, (i + 1) % lon_count) for i in range(l...  1.83 us
    unnamed x8, local copies, waits for them, and re-layouts  1.24 us
  transfers between devices with their start and end apart: 4, of which 1 were waited for; matrix products, arithmetic and copies ran while one was open for 0% of the time, Pallas kernels for 0%

profile of v8, /device:TPU:2, one launch (start us, length us, event | category | flops | bytes accessed | tf_op | source)
XLA Modules:
  0.0 27.9 jit_solution(17115299738810365908)
XLA Ops:
  0.6 3.8 %shard_map.86 = (f32[16,128]{1,0:T(8,128)}, f32[16,128]{1,0:T(8,128)}, f32[76,256]{1,0:T(8,128)}, f32[76,256]{1,0:T(8,128)}) custom-call(f32[25,16,256]{2,1,0:T(8,128)} %t_ref.1, f32[25,16,256]{2,1,0:T(8,128)} %s_ref.1, f32[25,16,256]{2,1,0:T(8,128)} %u_ref.1, f32[25,16,256]{2,1,0:T(8,128)} %v_ref.1, s32[16,256]{1,0:T(8,128)} %wi_ref.3, s32[16,256]{1,0:T(8,128)} %sb_ref.3), custom_call_target="tpu_custom_call" | custom-call | tf_op jit(solution)/shard_map/pallas_call | solution.py:304
  4.4 1.9 %collective-permute-start.2 = (f32[76,256]{1,0:T(8,128)}, f32[76,256]{1,0:T(8,128)S(1)}, u32[]{:S(2)}, u32[]{:S(2)}) collective-permute-start(f32[76,256]{1,0:T(8,128)} %get-tuple-element.8), channel_id=1, source_target_pairs={{1,2},{2,1},{3,31},{5,6},{6,5},{7,27},{9,10},{10,9},{11,23},{13,14... | collective-permute-start | bytes 233480 | tf_op jit(solution)/shard_map/ppermute | solution.py:345
  6.3 4.2 %collective-permute-start.3 = (f32[76,256]{1,0:T(8,128)}, f32[76,256]{1,0:T(8,128)S(1)}, u32[]{:S(2)}, u32[]{:S(2)}) collective-permute-start(f32[76,256]{1,0:T(8,128)} %get-tuple-element.9), channel_id=1, source_target_pairs={{0,1},{1,0},{2,3},{3,2},{4,5},{5,4},{6,7},{7,6},{8,9},{9,8},{10,11... | collective-permute-start | bytes 233480 | tf_op jit(solution)/shard_map/ppermute | solution.py:346
  10.5 0.5 %collective-permute-start = (f32[16,128]{1,0:T(8,128)}, f32[16,128]{1,0:T(8,128)S(1)}, u32[]{:S(2)}, u32[]{:S(2)}) collective-permute-start(f32[16,128]{1,0:T(8,128)} %get-tuple-element.6), channel_id=1, source_target_pairs={{0,4},{4,8},{8,12},{12,16},{16,20},{20,24},{24,28},{28,0},{1,5},{5... | collective-permute-start | bytes 24584 | tf_op jit(solution)/shard_map/ppermute | solution.py:325
  11.0 4.2 %collective-permute-start.1 = (f32[16,128]{1,0:T(8,128)}, f32[16,128]{1,0:T(8,128)S(1)}, u32[]{:S(2)}, u32[]{:S(2)}) collective-permute-start(f32[16,128]{1,0:T(8,128)} %get-tuple-element.7), channel_id=1, source_target_pairs={{4,0},{8,4},{12,8},{16,12},{20,16},{24,20},{28,24},{0,28},{5,1},{9... | collective-permute-start | bytes 24584 | tf_op jit(solution)/shard_map/ppermute | solution.py:328
  15.2 1.8 %collective-permute-done.hw_ref = f32[16,128]{1,0:T(8,128)S(1)} collective-permute-done((f32[16,128]{1,0:T(8,128)}, f32[16,128]{1,0:T(8,128)S(1)}, u32[]{:S(2)}, u32[]{:S(2)}) %collective-permute-start) | collective-permute-done | bytes 8224 | tf_op jit(solution)/shard_map/ppermute | solution.py:325
  17.1 0.0 copy-start.2
  17.1 0.0 collective-permute-done.1.he_ref
  17.1 0.0 copy-start.3
  17.1 0.0 collective-permute-done.2.first_ref
  17.1 0.0 copy-start
  17.1 0.0 collective-permute-done.3.second_ref
  17.1 0.6 %copy-done.2 = f32[16,128]{1,0:T(8,128)} copy-done((f32[16,128]{1,0:T(8,128)}, f32[16,128]{1,0:T(8,128)S(1)}, u32[]{:S(2)}) %copy-start.2) | copy-done | bytes 8216
  17.6 0.0 copy-done.3
  17.7 0.0 copy-done
  17.7 0.0 copy-start.1
  17.7 0.6 %copy-done.1 = f32[76,256]{1,0:T(8,128)} copy-done((f32[76,256]{1,0:T(8,128)}, f32[76,256]{1,0:T(8,128)S(1)}, u32[]{:S(2)}) %copy-start.1) | copy-done | bytes 77848
  18.3 9.6 %shard_map.87 = (f32[25,16,256]{2,1,0:T(8,128)}, f32[25,16,256]{2,1,0:T(8,128)}) custom-call(f32[25,16,256]{2,1,0:T(8,128)} %t_ref.1, f32[25,16,256]{2,1,0:T(8,128)} %s_ref.1, f32[25,16,256]{2,1,0:T(8,128)} %u_ref.1, f32[25,16,256]{2,1,0:T(8,128)} %v_ref.1, f32[25,16,256]{2,1,0:T(8,128)} %w_ref.1, s32[16,256]{1,0:T(8,128)} %wi_ref.3, s32[16,256]{1,0:T(8,128)} %sb_ref.3, ...), custom_call_target="tpu_custom_call" | custom-call | tf_op jit(solution)/shard_map/pallas_call | solution.py:348
Async XLA Ops:
  4.4 12.7 %collective-permute-start.2 = (f32[76,256]{1,0:T(8,128)}, f32[76,256]{1,0:T(8,128)S(1)}, u32[]{:S(2)}, u32[]{:S(2)}) collective-permute-start(f32[76,256]{1,0:T(8,128)} %get-tuple-element.8), channel_id=1, source_target_pairs={{1,2},{2,1},{3,31},{5,6},{6,5},{7,27},{9,10},{10,9},{11,23},{13,14... | collective-permute-start | bytes 233480 | tf_op jit(solution)/shard_map/ppermute | solution.py:345
  6.3 10.8 %collective-permute-start.3 = (f32[76,256]{1,0:T(8,128)}, f32[76,256]{1,0:T(8,128)S(1)}, u32[]{:S(2)}, u32[]{:S(2)}) collective-permute-start(f32[76,256]{1,0:T(8,128)} %get-tuple-element.9), channel_id=1, source_target_pairs={{0,1},{1,0},{2,3},{3,2},{4,5},{5,4},{6,7},{7,6},{8,9},{9,8},{10,11... | collective-permute-start | bytes 233480 | tf_op jit(solution)/shard_map/ppermute | solution.py:346
  10.5 6.6 %collective-permute-start = (f32[16,128]{1,0:T(8,128)}, f32[16,128]{1,0:T(8,128)S(1)}, u32[]{:S(2)}, u32[]{:S(2)}) collective-permute-start(f32[16,128]{1,0:T(8,128)} %get-tuple-element.6), channel_id=1, source_target_pairs={{0,4},{4,8},{8,12},{12,16},{16,20},{20,24},{24,28},{28,0},{1,5},{5... | collective-permute-start | bytes 24584 | tf_op jit(solution)/shard_map/ppermute | solution.py:325
  11.0 6.1 %collective-permute-start.1 = (f32[16,128]{1,0:T(8,128)}, f32[16,128]{1,0:T(8,128)S(1)}, u32[]{:S(2)}, u32[]{:S(2)}) collective-permute-start(f32[16,128]{1,0:T(8,128)} %get-tuple-element.7), channel_id=1, source_target_pairs={{4,0},{8,4},{12,8},{16,12},{20,16},{24,20},{28,24},{0,28},{5,1},{9... | collective-permute-start | bytes 24584 | tf_op jit(solution)/shard_map/ppermute | solution.py:328
  17.1 0.6 %copy-start.2 = (f32[16,128]{1,0:T(8,128)}, f32[16,128]{1,0:T(8,128)S(1)}, u32[]{:S(2)}) copy-start(f32[16,128]{1,0:T(8,128)S(1)} %collective-permute-done.hw_ref) | copy-start | bytes 24580
  17.1 0.6 %copy-start.3 = (f32[16,128]{1,0:T(8,128)}, f32[16,128]{1,0:T(8,128)S(1)}, u32[]{:S(2)}) copy-start(f32[16,128]{1,0:T(8,128)S(1)} %collective-permute-done.1.he_ref) | copy-start | bytes 24580
  17.1 0.6 %copy-start = (f32[76,256]{1,0:T(8,128)}, f32[76,256]{1,0:T(8,128)S(1)}, u32[]{:S(2)}) copy-start(f32[76,256]{1,0:T(8,128)S(1)} %collective-permute-done.2.first_ref) | copy-start | bytes 233476
  17.7 0.6 %copy-start.1 = (f32[76,256]{1,0:T(8,128)}, f32[76,256]{1,0:T(8,128)S(1)}, u32[]{:S(2)}) copy-start(f32[76,256]{1,0:T(8,128)S(1)} %collective-permute-done.3.second_ref) | copy-start | bytes 233476

commit v9 on v7

--- a/solution.py
+++ b/solution.py
@@ -142,7 +142,8 @@
         )
 
     def level_step(k, carry):
-        down_temp, down_salt = carry
+        down_temp, down_salt = carry[:2]
+        means_here = [carry[2 + 2 * n : 4 + 2 * n] for n in range(3)]
         lower = planes(k - 1)
         here = planes(k)
         upper = planes(k + 1)
@@ -186,7 +187,6 @@
             )
             for s, f in zip(south_edge_flux, north)
         ]
-        means_here = [cell_means(f, wet_here) for f in here]
         means_upper = [cell_means(f, wet_upper) for f in upper]
         face = face_bottom[0]
         xu = [0.5 * (mh[0] + mu[0]) for mh, mu in zip(means_here, means_upper)]
@@ -209,10 +209,17 @@
             divergence = (east[n] - west[n]) + (north[n] - south[n])
             divergence = divergence + (below[n] - top)
             dst[k] = here[n][0] - divergence
-        return tuple(below)
+        return tuple(below) + tuple(m for pair in means_upper for m in pair)
 
     zero = jnp.zeros((rows, cols), jnp.float32)
-    lax.fori_loop(0, layer_total, level_step, (zero, zero))
+    first_wet = wet_at(jnp.int32(0))
+    first_means = [cell_means(f, first_wet) for f in planes(jnp.int32(0))]
+    lax.fori_loop(
+        0,
+        layer_total,
+        level_step,
+        (zero, zero) + tuple(m for pair in first_means for m in pair),
+    )
 
 
 def edge_kernel(

time: 27.7 us -> 27.4 us (0.989)
  Pallas kernels: 12.8 us -> 12.5 us
    pallas_call x1, Pallas kernels: 9.62 us -> 9.3 us  [on_device(): pl.pallas_call(stencil_kernel, out_shape=(field, field), in_specs=[pl.Blo...]
where the time goes in v9:
time: 27.4 us; the launch traced here: 27 us
  Pallas kernels  12.5 us (46%)
  starting transfers between devices  10.8 us (39%)
  waiting for transfers between devices  1.84 us (7%)
  local copies, waits for them, and re-layouts  1.24 us (5%)
  between operations  0.66 us (2%)
    pallas_call x1, Pallas kernels, on_device(): pl.pallas_call(stencil_kernel, out_shape=(field, field), in_specs=[pl.Blo...  9.3 us
    ppermute x1, starting transfers between devices, on_device(): lax.ppermute(east_pack, 'lon', [((i + 1) % lon_count, i) for i in range(l...  4.22 us
    ppermute x1, starting transfers between devices, on_device(): second_got = lax.ppermute(second_lines, ('lon', 'lat'), second_pairs)  4.17 us
    pallas_call x1, Pallas kernels, on_device(): pl.pallas_call(edge_kernel, out_shape=(packed, packed, lines, lines), in_...  3.18 us
    ppermute x1, starting transfers between devices, on_device(): first_got = lax.ppermute(first_lines, ('lon', 'lat'), first_pairs)  1.91 us
    ppermute x1, waiting for transfers between devices, on_device(): lax.ppermute(west_pack, 'lon', [(i, (i + 1) % lon_count) for i in range(l...  1.83 us
    unnamed x8, local copies, waits for them, and re-layouts  1.24 us
  transfers between devices with their start and end apart: 4, of which 1 were waited for; matrix products, arithmetic and copies ran while one was open for 0% of the time, Pallas kernels for 0%

profile of v9, /device:TPU:2, one launch (start us, length us, event | category | flops | bytes accessed | tf_op | source)
XLA Modules:
  0.0 27.0 jit_solution(16941044156609826556)
XLA Ops:
  0.6 3.2 %shard_map.86 = (f32[16,128]{1,0:T(8,128)}, f32[16,128]{1,0:T(8,128)}, f32[76,256]{1,0:T(8,128)}, f32[76,256]{1,0:T(8,128)}) custom-call(f32[25,16,256]{2,1,0:T(8,128)} %t_ref.3, f32[25,16,256]{2,1,0:T(8,128)} %s_ref.3, f32[25,16,256]{2,1,0:T(8,128)} %u_ref.3, f32[25,16,256]{2,1,0:T(8,128)} %v_ref.3, s32[16,256]{1,0:T(8,128)} %wi_ref.3, s32[16,256]{1,0:T(8,128)} %sb_ref.3), custom_call_target="tpu_custom_call" | custom-call | tf_op jit(solution)/shard_map/pallas_call | solution.py:293
  3.8 1.9 %collective-permute-start.2 = (f32[76,256]{1,0:T(8,128)}, f32[76,256]{1,0:T(8,128)S(1)}, u32[]{:S(2)}, u32[]{:S(2)}) collective-permute-start(f32[76,256]{1,0:T(8,128)} %get-tuple-element.8), channel_id=1, source_target_pairs={{1,2},{2,1},{3,31},{5,6},{6,5},{7,27},{9,10},{10,9},{11,23},{13,14... | collective-permute-start | bytes 233480 | tf_op jit(solution)/shard_map/ppermute | solution.py:331
  5.7 4.2 %collective-permute-start.3 = (f32[76,256]{1,0:T(8,128)}, f32[76,256]{1,0:T(8,128)S(1)}, u32[]{:S(2)}, u32[]{:S(2)}) collective-permute-start(f32[76,256]{1,0:T(8,128)} %get-tuple-element.9), channel_id=1, source_target_pairs={{0,1},{1,0},{2,3},{3,2},{4,5},{5,4},{6,7},{7,6},{8,9},{9,8},{10,11... | collective-permute-start | bytes 233480 | tf_op jit(solution)/shard_map/ppermute | solution.py:332
  9.9 0.5 %collective-permute-start = (f32[16,128]{1,0:T(8,128)}, f32[16,128]{1,0:T(8,128)S(1)}, u32[]{:S(2)}, u32[]{:S(2)}) collective-permute-start(f32[16,128]{1,0:T(8,128)} %get-tuple-element.6), channel_id=1, source_target_pairs={{0,4},{4,8},{8,12},{12,16},{16,20},{20,24},{24,28},{28,0},{1,5},{5... | collective-permute-start | bytes 24584 | tf_op jit(solution)/shard_map/ppermute | solution.py:311
  10.4 4.2 %collective-permute-start.1 = (f32[16,128]{1,0:T(8,128)}, f32[16,128]{1,0:T(8,128)S(1)}, u32[]{:S(2)}, u32[]{:S(2)}) collective-permute-start(f32[16,128]{1,0:T(8,128)} %get-tuple-element.7), channel_id=1, source_target_pairs={{4,0},{8,4},{12,8},{16,12},{20,16},{24,20},{28,24},{0,28},{5,1},{9... | collective-permute-start | bytes 24584 | tf_op jit(solution)/shard_map/ppermute | solution.py:314
  14.6 1.8 %collective-permute-done.hw_ref = f32[16,128]{1,0:T(8,128)S(1)} collective-permute-done((f32[16,128]{1,0:T(8,128)}, f32[16,128]{1,0:T(8,128)S(1)}, u32[]{:S(2)}, u32[]{:S(2)}) %collective-permute-start) | collective-permute-done | bytes 8224 | tf_op jit(solution)/shard_map/ppermute | solution.py:311
  16.4 0.0 copy-start.2
  16.5 0.0 collective-permute-done.1.he_ref
  16.5 0.0 copy-start.3
  16.5 0.0 collective-permute-done.2.first_ref
  16.5 0.0 copy-start
  16.5 0.0 collective-permute-done.3.second_ref
  16.5 0.6 %copy-done.2 = f32[16,128]{1,0:T(8,128)} copy-done((f32[16,128]{1,0:T(8,128)}, f32[16,128]{1,0:T(8,128)S(1)}, u32[]{:S(2)}) %copy-start.2) | copy-done | bytes 8216
  17.0 0.0 copy-done.3
  17.1 0.0 copy-done
  17.1 0.0 copy-start.1
  17.1 0.6 %copy-done.1 = f32[76,256]{1,0:T(8,128)} copy-done((f32[76,256]{1,0:T(8,128)}, f32[76,256]{1,0:T(8,128)S(1)}, u32[]{:S(2)}) %copy-start.1) | copy-done | bytes 77848
  17.7 9.3 %shard_map.87 = (f32[25,16,256]{2,1,0:T(8,128)}, f32[25,16,256]{2,1,0:T(8,128)}) custom-call(f32[25,16,256]{2,1,0:T(8,128)} %t_ref.3, f32[25,16,256]{2,1,0:T(8,128)} %s_ref.3, f32[25,16,256]{2,1,0:T(8,128)} %u_ref.3, f32[25,16,256]{2,1,0:T(8,128)} %v_ref.3, f32[25,16,256]{2,1,0:T(8,128)} %w_ref.1, s32[16,256]{1,0:T(8,128)} %wi_ref.3, s32[16,256]{1,0:T(8,128)} %sb_ref.3, ...), custom_call_target="tpu_custom_call" | custom-call | tf_op jit(solution)/shard_map/pallas_call | solution.py:334
Async XLA Ops:
  3.8 12.7 %collective-permute-start.2 = (f32[76,256]{1,0:T(8,128)}, f32[76,256]{1,0:T(8,128)S(1)}, u32[]{:S(2)}, u32[]{:S(2)}) collective-permute-start(f32[76,256]{1,0:T(8,128)} %get-tuple-element.8), channel_id=1, source_target_pairs={{1,2},{2,1},{3,31},{5,6},{6,5},{7,27},{9,10},{10,9},{11,23},{13,14... | collective-permute-start | bytes 233480 | tf_op jit(solution)/shard_map/ppermute | solution.py:331
  5.7 10.8 %collective-permute-start.3 = (f32[76,256]{1,0:T(8,128)}, f32[76,256]{1,0:T(8,128)S(1)}, u32[]{:S(2)}, u32[]{:S(2)}) collective-permute-start(f32[76,256]{1,0:T(8,128)} %get-tuple-element.9), channel_id=1, source_target_pairs={{0,1},{1,0},{2,3},{3,2},{4,5},{5,4},{6,7},{7,6},{8,9},{9,8},{10,11... | collective-permute-start | bytes 233480 | tf_op jit(solution)/shard_map/ppermute | solution.py:332
  9.9 6.6 %collective-permute-start = (f32[16,128]{1,0:T(8,128)}, f32[16,128]{1,0:T(8,128)S(1)}, u32[]{:S(2)}, u32[]{:S(2)}) collective-permute-start(f32[16,128]{1,0:T(8,128)} %get-tuple-element.6), channel_id=1, source_target_pairs={{0,4},{4,8},{8,12},{12,16},{16,20},{20,24},{24,28},{28,0},{1,5},{5... | collective-permute-start | bytes 24584 | tf_op jit(solution)/shard_map/ppermute | solution.py:311
  10.4 6.1 %collective-permute-start.1 = (f32[16,128]{1,0:T(8,128)}, f32[16,128]{1,0:T(8,128)S(1)}, u32[]{:S(2)}, u32[]{:S(2)}) collective-permute-start(f32[16,128]{1,0:T(8,128)} %get-tuple-element.7), channel_id=1, source_target_pairs={{4,0},{8,4},{12,8},{16,12},{20,16},{24,20},{28,24},{0,28},{5,1},{9... | collective-permute-start | bytes 24584 | tf_op jit(solution)/shard_map/ppermute | solution.py:314
  16.4 0.6 %copy-start.2 = (f32[16,128]{1,0:T(8,128)}, f32[16,128]{1,0:T(8,128)S(1)}, u32[]{:S(2)}) copy-start(f32[16,128]{1,0:T(8,128)S(1)} %collective-permute-done.hw_ref) | copy-start | bytes 24580
  16.5 0.6 %copy-start.3 = (f32[16,128]{1,0:T(8,128)}, f32[16,128]{1,0:T(8,128)S(1)}, u32[]{:S(2)}) copy-start(f32[16,128]{1,0:T(8,128)S(1)} %collective-permute-done.1.he_ref) | copy-start | bytes 24580
  16.5 0.6 %copy-start = (f32[76,256]{1,0:T(8,128)}, f32[76,256]{1,0:T(8,128)S(1)}, u32[]{:S(2)}) copy-start(f32[76,256]{1,0:T(8,128)S(1)} %collective-permute-done.2.first_ref) | copy-start | bytes 233476
  17.1 0.6 %copy-start.1 = (f32[76,256]{1,0:T(8,128)}, f32[76,256]{1,0:T(8,128)S(1)}, u32[]{:S(2)}) copy-start(f32[76,256]{1,0:T(8,128)S(1)} %collective-permute-done.3.second_ref) | copy-start | bytes 233476

commit v10 on v9

--- a/solution.py
+++ b/solution.py
@@ -144,13 +144,12 @@
     def level_step(k, carry):
         down_temp, down_salt = carry[:2]
         means_here = [carry[2 + 2 * n : 4 + 2 * n] for n in range(3)]
+        face_top = list(carry[8:13])
         lower = planes(k - 1)
         here = planes(k)
         upper = planes(k + 1)
-        wet_lower = wet_at(k - 1)
         wet_here = wet_at(k)
         wet_upper = wet_at(k + 1)
-        face_top = [wet_here[i] * wet_lower[i] for i in range(5)]
         face_bottom = [wet_upper[i] * wet_here[i] for i in range(5)]
 
         def kc_set(i, part):
@@ -209,7 +208,9 @@
             divergence = (east[n] - west[n]) + (north[n] - south[n])
             divergence = divergence + (below[n] - top)
             dst[k] = here[n][0] - divergence
-        return tuple(below) + tuple(m for pair in means_upper for m in pair)
+        return (
+            tuple(below) + tuple(m for pair in means_upper for m in pair) + tuple(face_bottom)
+        )
 
     zero = jnp.zeros((rows, cols), jnp.float32)
     first_wet = wet_at(jnp.int32(0))
@@ -218,7 +219,7 @@
         0,
         layer_total,
         level_step,
-        (zero, zero) + tuple(m for pair in first_means for m in pair),
+        (zero, zero) + tuple(m for pair in first_means for m in pair) + (zero,) * 5,
     )
 
 

time: 27.4 us -> 27.2 us (level)
  no operation moved by 1% of the time
where the time goes in v10:
time: 27.2 us; the launch traced here: 26.8 us
  Pallas kernels  12.3 us (45%)
  starting transfers between devices  10.8 us (40%)
  waiting for transfers between devices  1.84 us (7%)
  local copies, waits for them, and re-layouts  1.24 us (5%)
  between operations  0.66 us (2%)
    pallas_call x1, Pallas kernels, on_device(): pl.pallas_call(stencil_kernel, out_shape=(field, field), in_specs=[pl.Blo...  9.11 us
    ppermute x1, starting transfers between devices, on_device(): lax.ppermute(east_pack, 'lon', [((i + 1) % lon_count, i) for i in range(l...  4.22 us
    ppermute x1, starting transfers between devices, on_device(): second_got = lax.ppermute(second_lines, ('lon', 'lat'), second_pairs)  4.17 us
    pallas_call x1, Pallas kernels, on_device(): pl.pallas_call(edge_kernel, out_shape=(packed, packed, lines, lines), in_...  3.18 us
    ppermute x1, starting transfers between devices, on_device(): first_got = lax.ppermute(first_lines, ('lon', 'lat'), first_pairs)  1.91 us
    ppermute x1, waiting for transfers between devices, on_device(): lax.ppermute(west_pack, 'lon', [(i, (i + 1) % lon_count) for i in range(l...  1.83 us
    unnamed x8, local copies, waits for them, and re-layouts  1.24 us
  transfers between devices with their start and end apart: 4, of which 1 were waited for; matrix products, arithmetic and copies ran while one was open for 0% of the time, Pallas kernels for 0%

profile of v10, /device:TPU:2, one launch (start us, length us, event | category | flops | bytes accessed | tf_op | source)
XLA Modules:
  0.0 26.8 jit_solution(10839542957841207135)
XLA Ops:
  0.6 3.2 %shard_map.86 = (f32[16,128]{1,0:T(8,128)}, f32[16,128]{1,0:T(8,128)}, f32[76,256]{1,0:T(8,128)}, f32[76,256]{1,0:T(8,128)}) custom-call(f32[25,16,256]{2,1,0:T(8,128)} %t_ref.3, f32[25,16,256]{2,1,0:T(8,128)} %s_ref.3, f32[25,16,256]{2,1,0:T(8,128)} %u_ref.3, f32[25,16,256]{2,1,0:T(8,128)} %v_ref.3, s32[16,256]{1,0:T(8,128)} %wi_ref.3, s32[16,256]{1,0:T(8,128)} %sb_ref.3), custom_call_target="tpu_custom_call" | custom-call | tf_op jit(solution)/shard_map/pallas_call | solution.py:294
  3.8 1.9 %collective-permute-start.2 = (f32[76,256]{1,0:T(8,128)}, f32[76,256]{1,0:T(8,128)S(1)}, u32[]{:S(2)}, u32[]{:S(2)}) collective-permute-start(f32[76,256]{1,0:T(8,128)} %get-tuple-element.8), channel_id=1, source_target_pairs={{1,2},{2,1},{3,31},{5,6},{6,5},{7,27},{9,10},{10,9},{11,23},{13,14... | collective-permute-start | bytes 233480 | tf_op jit(solution)/shard_map/ppermute | solution.py:332
  5.7 4.2 %collective-permute-start.3 = (f32[76,256]{1,0:T(8,128)}, f32[76,256]{1,0:T(8,128)S(1)}, u32[]{:S(2)}, u32[]{:S(2)}) collective-permute-start(f32[76,256]{1,0:T(8,128)} %get-tuple-element.9), channel_id=1, source_target_pairs={{0,1},{1,0},{2,3},{3,2},{4,5},{5,4},{6,7},{7,6},{8,9},{9,8},{10,11... | collective-permute-start | bytes 233480 | tf_op jit(solution)/shard_map/ppermute | solution.py:333
  9.9 0.5 %collective-permute-start = (f32[16,128]{1,0:T(8,128)}, f32[16,128]{1,0:T(8,128)S(1)}, u32[]{:S(2)}, u32[]{:S(2)}) collective-permute-start(f32[16,128]{1,0:T(8,128)} %get-tuple-element.6), channel_id=1, source_target_pairs={{0,4},{4,8},{8,12},{12,16},{16,20},{20,24},{24,28},{28,0},{1,5},{5... | collective-permute-start | bytes 24584 | tf_op jit(solution)/shard_map/ppermute | solution.py:312
  10.4 4.2 %collective-permute-start.1 = (f32[16,128]{1,0:T(8,128)}, f32[16,128]{1,0:T(8,128)S(1)}, u32[]{:S(2)}, u32[]{:S(2)}) collective-permute-start(f32[16,128]{1,0:T(8,128)} %get-tuple-element.7), channel_id=1, source_target_pairs={{4,0},{8,4},{12,8},{16,12},{20,16},{24,20},{28,24},{0,28},{5,1},{9... | collective-permute-start | bytes 24584 | tf_op jit(solution)/shard_map/ppermute | solution.py:315
  14.6 1.8 %collective-permute-done.hw_ref = f32[16,128]{1,0:T(8,128)S(1)} collective-permute-done((f32[16,128]{1,0:T(8,128)}, f32[16,128]{1,0:T(8,128)S(1)}, u32[]{:S(2)}, u32[]{:S(2)}) %collective-permute-start) | collective-permute-done | bytes 8224 | tf_op jit(solution)/shard_map/ppermute | solution.py:312
  16.4 0.0 copy-start.2
  16.5 0.0 collective-permute-done.1.he_ref
  16.5 0.0 copy-start.3
  16.5 0.0 collective-permute-done.2.first_ref
  16.5 0.0 copy-start
  16.5 0.0 collective-permute-done.3.second_ref
  16.5 0.6 %copy-done.2 = f32[16,128]{1,0:T(8,128)} copy-done((f32[16,128]{1,0:T(8,128)}, f32[16,128]{1,0:T(8,128)S(1)}, u32[]{:S(2)}) %copy-start.2) | copy-done | bytes 8216
  17.0 0.0 copy-done.3
  17.1 0.0 copy-done
  17.1 0.0 copy-start.1
  17.1 0.6 %copy-done.1 = f32[76,256]{1,0:T(8,128)} copy-done((f32[76,256]{1,0:T(8,128)}, f32[76,256]{1,0:T(8,128)S(1)}, u32[]{:S(2)}) %copy-start.1) | copy-done | bytes 77848
  17.7 9.1 %shard_map.87 = (f32[25,16,256]{2,1,0:T(8,128)}, f32[25,16,256]{2,1,0:T(8,128)}) custom-call(f32[25,16,256]{2,1,0:T(8,128)} %t_ref.3, f32[25,16,256]{2,1,0:T(8,128)} %s_ref.3, f32[25,16,256]{2,1,0:T(8,128)} %u_ref.3, f32[25,16,256]{2,1,0:T(8,128)} %v_ref.3, f32[25,16,256]{2,1,0:T(8,128)} %w_ref.1, s32[16,256]{1,0:T(8,128)} %wi_ref.3, s32[16,256]{1,0:T(8,128)} %sb_ref.3, ...), custom_call_target="tpu_custom_call" | custom-call | tf_op jit(solution)/shard_map/pallas_call | solution.py:335
Async XLA Ops:
  3.8 12.7 %collective-permute-start.2 = (f32[76,256]{1,0:T(8,128)}, f32[76,256]{1,0:T(8,128)S(1)}, u32[]{:S(2)}, u32[]{:S(2)}) collective-permute-start(f32[76,256]{1,0:T(8,128)} %get-tuple-element.8), channel_id=1, source_target_pairs={{1,2},{2,1},{3,31},{5,6},{6,5},{7,27},{9,10},{10,9},{11,23},{13,14... | collective-permute-start | bytes 233480 | tf_op jit(solution)/shard_map/ppermute | solution.py:332
  5.7 10.8 %collective-permute-start.3 = (f32[76,256]{1,0:T(8,128)}, f32[76,256]{1,0:T(8,128)S(1)}, u32[]{:S(2)}, u32[]{:S(2)}) collective-permute-start(f32[76,256]{1,0:T(8,128)} %get-tuple-element.9), channel_id=1, source_target_pairs={{0,1},{1,0},{2,3},{3,2},{4,5},{5,4},{6,7},{7,6},{8,9},{9,8},{10,11... | collective-permute-start | bytes 233480 | tf_op jit(solution)/shard_map/ppermute | solution.py:333
  9.9 6.6 %collective-permute-start = (f32[16,128]{1,0:T(8,128)}, f32[16,128]{1,0:T(8,128)S(1)}, u32[]{:S(2)}, u32[]{:S(2)}) collective-permute-start(f32[16,128]{1,0:T(8,128)} %get-tuple-element.6), channel_id=1, source_target_pairs={{0,4},{4,8},{8,12},{12,16},{16,20},{20,24},{24,28},{28,0},{1,5},{5... | collective-permute-start | bytes 24584 | tf_op jit(solution)/shard_map/ppermute | solution.py:312
  10.4 6.1 %collective-permute-start.1 = (f32[16,128]{1,0:T(8,128)}, f32[16,128]{1,0:T(8,128)S(1)}, u32[]{:S(2)}, u32[]{:S(2)}) collective-permute-start(f32[16,128]{1,0:T(8,128)} %get-tuple-element.7), channel_id=1, source_target_pairs={{4,0},{8,4},{12,8},{16,12},{20,16},{24,20},{28,24},{0,28},{5,1},{9... | collective-permute-start | bytes 24584 | tf_op jit(solution)/shard_map/ppermute | solution.py:315
  16.4 0.6 %copy-start.2 = (f32[16,128]{1,0:T(8,128)}, f32[16,128]{1,0:T(8,128)S(1)}, u32[]{:S(2)}) copy-start(f32[16,128]{1,0:T(8,128)S(1)} %collective-permute-done.hw_ref) | copy-start | bytes 24580
  16.5 0.6 %copy-start.3 = (f32[16,128]{1,0:T(8,128)}, f32[16,128]{1,0:T(8,128)S(1)}, u32[]{:S(2)}) copy-start(f32[16,128]{1,0:T(8,128)S(1)} %collective-permute-done.1.he_ref) | copy-start | bytes 24580
  16.5 0.6 %copy-start = (f32[76,256]{1,0:T(8,128)}, f32[76,256]{1,0:T(8,128)S(1)}, u32[]{:S(2)}) copy-start(f32[76,256]{1,0:T(8,128)S(1)} %collective-permute-done.2.first_ref) | copy-start | bytes 233476
  17.1 0.6 %copy-start.1 = (f32[76,256]{1,0:T(8,128)}, f32[76,256]{1,0:T(8,128)S(1)}, u32[]{:S(2)}) copy-start(f32[76,256]{1,0:T(8,128)S(1)} %collective-permute-done.3.second_ref) | copy-start | bytes 233476

commit v11 on v10

--- a/solution.py
+++ b/solution.py
@@ -145,10 +145,10 @@
         down_temp, down_salt = carry[:2]
         means_here = [carry[2 + 2 * n : 4 + 2 * n] for n in range(3)]
         face_top = list(carry[8:13])
+        wet_here = list(carry[13:18])
         lower = planes(k - 1)
         here = planes(k)
         upper = planes(k + 1)
-        wet_here = wet_at(k)
         wet_upper = wet_at(k + 1)
         face_bottom = [wet_upper[i] * wet_here[i] for i in range(5)]
 
@@ -209,7 +209,10 @@
             divergence = divergence + (below[n] - top)
             dst[k] = here[n][0] - divergence
         return (
-            tuple(below) + tuple(m for pair in means_upper for m in pair) + tuple(face_bottom)
+            tuple(below)
+            + tuple(m for pair in means_upper for m in pair)
+            + tuple(face_bottom)
+            + tuple(wet_upper)
         )
 
     zero = jnp.zeros((rows, cols), jnp.float32)
@@ -219,7 +222,10 @@
         0,
         layer_total,
         level_step,
-        (zero, zero) + tuple(m for pair in first_means for m in pair) + (zero,) * 5,
+        (zero, zero)
+        + tuple(m for pair in first_means for m in pair)
+        + (zero,) * 5
+        + tuple(first_wet),
     )
 
 

time: 27.2 us -> 27.3 us (level)
  no operation moved by 1% of the time
where the time goes in v11:
time: 27.3 us; the launch traced here: 27 us
  Pallas kernels  12.5 us (46%)
  starting transfers between devices  10.8 us (40%)
  waiting for transfers between devices  1.84 us (7%)
  local copies, waits for them, and re-layouts  1.24 us (5%)
  between operations  0.66 us (2%)
    pallas_call x1, Pallas kernels, on_device(): pl.pallas_call(stencil_kernel, out_shape=(field, field), in_specs=[pl.Blo...  9.27 us
    ppermute x1, starting transfers between devices, on_device(): lax.ppermute(east_pack, 'lon', [((i + 1) % lon_count, i) for i in range(l...  4.22 us
    ppermute x1, starting transfers between devices, on_device(): second_got = lax.ppermute(second_lines, ('lon', 'lat'), second_pairs)  4.17 us
    pallas_call x1, Pallas kernels, on_device(): pl.pallas_call(edge_kernel, out_shape=(packed, packed, lines, lines), in_...  3.18 us
    ppermute x1, starting transfers between devices, on_device(): first_got = lax.ppermute(first_lines, ('lon', 'lat'), first_pairs)  1.91 us
    ppermute x1, waiting for transfers between devices, on_device(): lax.ppermute(west_pack, 'lon', [(i, (i + 1) % lon_count) for i in range(l...  1.83 us
    unnamed x8, local copies, waits for them, and re-layouts  1.24 us
  transfers between devices with their start and end apart: 4, of which 1 were waited for; matrix products, arithmetic and copies ran while one was open for 0% of the time, Pallas kernels for 0%

profile of v11, /device:TPU:2, one launch (start us, length us, event | category | flops | bytes accessed | tf_op | source)
XLA Modules:
  0.0 27.0 jit_solution(4812903262670714808)
XLA Ops:
  0.6 3.2 %shard_map.86 = (f32[16,128]{1,0:T(8,128)}, f32[16,128]{1,0:T(8,128)}, f32[76,256]{1,0:T(8,128)}, f32[76,256]{1,0:T(8,128)}) custom-call(f32[25,16,256]{2,1,0:T(8,128)} %t_ref.3, f32[25,16,256]{2,1,0:T(8,128)} %s_ref.3, f32[25,16,256]{2,1,0:T(8,128)} %u_ref.3, f32[25,16,256]{2,1,0:T(8,128)} %v_ref.3, s32[16,256]{1,0:T(8,128)} %wi_ref.3, s32[16,256]{1,0:T(8,128)} %sb_ref.3), custom_call_target="tpu_custom_call" | custom-call | tf_op jit(solution)/shard_map/pallas_call | solution.py:300
  3.8 1.9 %collective-permute-start.2 = (f32[76,256]{1,0:T(8,128)}, f32[76,256]{1,0:T(8,128)S(1)}, u32[]{:S(2)}, u32[]{:S(2)}) collective-permute-start(f32[76,256]{1,0:T(8,128)} %get-tuple-element.8), channel_id=1, source_target_pairs={{1,2},{2,1},{3,31},{5,6},{6,5},{7,27},{9,10},{10,9},{11,23},{13,14... | collective-permute-start | bytes 233480 | tf_op jit(solution)/shard_map/ppermute | solution.py:338
  5.7 4.2 %collective-permute-start.3 = (f32[76,256]{1,0:T(8,128)}, f32[76,256]{1,0:T(8,128)S(1)}, u32[]{:S(2)}, u32[]{:S(2)}) collective-permute-start(f32[76,256]{1,0:T(8,128)} %get-tuple-element.9), channel_id=1, source_target_pairs={{0,1},{1,0},{2,3},{3,2},{4,5},{5,4},{6,7},{7,6},{8,9},{9,8},{10,11... | collective-permute-start | bytes 233480 | tf_op jit(solution)/shard_map/ppermute | solution.py:339
  9.9 0.5 %collective-permute-start = (f32[16,128]{1,0:T(8,128)}, f32[16,128]{1,0:T(8,128)S(1)}, u32[]{:S(2)}, u32[]{:S(2)}) collective-permute-start(f32[16,128]{1,0:T(8,128)} %get-tuple-element.6), channel_id=1, source_target_pairs={{0,4},{4,8},{8,12},{12,16},{16,20},{20,24},{24,28},{28,0},{1,5},{5... | collective-permute-start | bytes 24584 | tf_op jit(solution)/shard_map/ppermute | solution.py:318
  10.4 4.2 %collective-permute-start.1 = (f32[16,128]{1,0:T(8,128)}, f32[16,128]{1,0:T(8,128)S(1)}, u32[]{:S(2)}, u32[]{:S(2)}) collective-permute-start(f32[16,128]{1,0:T(8,128)} %get-tuple-element.7), channel_id=1, source_target_pairs={{4,0},{8,4},{12,8},{16,12},{20,16},{24,20},{28,24},{0,28},{5,1},{9... | collective-permute-start | bytes 24584 | tf_op jit(solution)/shard_map/ppermute | solution.py:321
  14.6 1.8 %collective-permute-done.hw_ref = f32[16,128]{1,0:T(8,128)S(1)} collective-permute-done((f32[16,128]{1,0:T(8,128)}, f32[16,128]{1,0:T(8,128)S(1)}, u32[]{:S(2)}, u32[]{:S(2)}) %collective-permute-start) | collective-permute-done | bytes 8224 | tf_op jit(solution)/shard_map/ppermute | solution.py:318
  16.4 0.0 copy-start.2
  16.5 0.0 collective-permute-done.1.he_ref
  16.5 0.0 copy-start.3
  16.5 0.0 collective-permute-done.2.first_ref
  16.5 0.0 copy-start
  16.5 0.0 collective-permute-done.3.second_ref
  16.5 0.6 %copy-done.2 = f32[16,128]{1,0:T(8,128)} copy-done((f32[16,128]{1,0:T(8,128)}, f32[16,128]{1,0:T(8,128)S(1)}, u32[]{:S(2)}) %copy-start.2) | copy-done | bytes 8216
  17.0 0.0 copy-done.3
  17.1 0.0 copy-done
  17.1 0.0 copy-start.1
  17.1 0.6 %copy-done.1 = f32[76,256]{1,0:T(8,128)} copy-done((f32[76,256]{1,0:T(8,128)}, f32[76,256]{1,0:T(8,128)S(1)}, u32[]{:S(2)}) %copy-start.1) | copy-done | bytes 77848
  17.7 9.3 %shard_map.87 = (f32[25,16,256]{2,1,0:T(8,128)}, f32[25,16,256]{2,1,0:T(8,128)}) custom-call(f32[25,16,256]{2,1,0:T(8,128)} %t_ref.3, f32[25,16,256]{2,1,0:T(8,128)} %s_ref.3, f32[25,16,256]{2,1,0:T(8,128)} %u_ref.3, f32[25,16,256]{2,1,0:T(8,128)} %v_ref.3, f32[25,16,256]{2,1,0:T(8,128)} %w_ref.1, s32[16,256]{1,0:T(8,128)} %wi_ref.3, s32[16,256]{1,0:T(8,128)} %sb_ref.3, ...), custom_call_target="tpu_custom_call" | custom-call | tf_op jit(solution)/shard_map/pallas_call | solution.py:341
Async XLA Ops:
  3.8 12.7 %collective-permute-start.2 = (f32[76,256]{1,0:T(8,128)}, f32[76,256]{1,0:T(8,128)S(1)}, u32[]{:S(2)}, u32[]{:S(2)}) collective-permute-start(f32[76,256]{1,0:T(8,128)} %get-tuple-element.8), channel_id=1, source_target_pairs={{1,2},{2,1},{3,31},{5,6},{6,5},{7,27},{9,10},{10,9},{11,23},{13,14... | collective-permute-start | bytes 233480 | tf_op jit(solution)/shard_map/ppermute | solution.py:338
  5.7 10.8 %collective-permute-start.3 = (f32[76,256]{1,0:T(8,128)}, f32[76,256]{1,0:T(8,128)S(1)}, u32[]{:S(2)}, u32[]{:S(2)}) collective-permute-start(f32[76,256]{1,0:T(8,128)} %get-tuple-element.9), channel_id=1, source_target_pairs={{0,1},{1,0},{2,3},{3,2},{4,5},{5,4},{6,7},{7,6},{8,9},{9,8},{10,11... | collective-permute-start | bytes 233480 | tf_op jit(solution)/shard_map/ppermute | solution.py:339
  9.9 6.6 %collective-permute-start = (f32[16,128]{1,0:T(8,128)}, f32[16,128]{1,0:T(8,128)S(1)}, u32[]{:S(2)}, u32[]{:S(2)}) collective-permute-start(f32[16,128]{1,0:T(8,128)} %get-tuple-element.6), channel_id=1, source_target_pairs={{0,4},{4,8},{8,12},{12,16},{16,20},{20,24},{24,28},{28,0},{1,5},{5... | collective-permute-start | bytes 24584 | tf_op jit(solution)/shard_map/ppermute | solution.py:318
  10.4 6.1 %collective-permute-start.1 = (f32[16,128]{1,0:T(8,128)}, f32[16,128]{1,0:T(8,128)S(1)}, u32[]{:S(2)}, u32[]{:S(2)}) collective-permute-start(f32[16,128]{1,0:T(8,128)} %get-tuple-element.7), channel_id=1, source_target_pairs={{4,0},{8,4},{12,8},{16,12},{20,16},{24,20},{28,24},{0,28},{5,1},{9... | collective-permute-start | bytes 24584 | tf_op jit(solution)/shard_map/ppermute | solution.py:321
  16.4 0.6 %copy-start.2 = (f32[16,128]{1,0:T(8,128)}, f32[16,128]{1,0:T(8,128)S(1)}, u32[]{:S(2)}) copy-start(f32[16,128]{1,0:T(8,128)S(1)} %collective-permute-done.hw_ref) | copy-start | bytes 24580
  16.5 0.6 %copy-start.3 = (f32[16,128]{1,0:T(8,128)}, f32[16,128]{1,0:T(8,128)S(1)}, u32[]{:S(2)}) copy-start(f32[16,128]{1,0:T(8,128)S(1)} %collective-permute-done.1.he_ref) | copy-start | bytes 24580
  16.5 0.6 %copy-start = (f32[76,256]{1,0:T(8,128)}, f32[76,256]{1,0:T(8,128)S(1)}, u32[]{:S(2)}) copy-start(f32[76,256]{1,0:T(8,128)S(1)} %collective-permute-done.2.first_ref) | copy-start | bytes 233476
  17.1 0.6 %copy-start.1 = (f32[76,256]{1,0:T(8,128)}, f32[76,256]{1,0:T(8,128)S(1)}, u32[]{:S(2)}) copy-start(f32[76,256]{1,0:T(8,128)S(1)} %collective-permute-done.3.second_ref) | copy-start | bytes 233476

commit v12 on v10

--- a/solution.py
+++ b/solution.py
@@ -160,8 +160,14 @@
 
         kc_full = [kc_set(i, whole) for i in (0, 1, 3)]
         kcs = [[kc_full[0][n], kc_full[1][n], None, kc_full[2][n], None] for n in range(3)]
-        west_kcs = [[kc_set(0, west_part)[n], None, kc_set(2, west_part)[n], None, None] for n in range(3)]
-        south_kcs = [[kc_set(0, south_part)[n], None, None, None, kc_set(4, south_part)[n]] for n in range(3)]
+        west_kc = kc_set(2, west_part)
+        south_kc = kc_set(4, south_part)
+        west_kcs = [
+            [west_part(kc_full[0][n]), None, west_kc[n], None, None] for n in range(3)
+        ]
+        south_kcs = [
+            [south_part(kc_full[0][n]), None, None, None, south_kc[n]] for n in range(3)
+        ]
         zonal = u_ref[k]
         meridional = v_ref[k]
         east = horizontal(here, kcs, wet_here, 0, 1, zonal, ush[0, k], whole)

time: 27.2 us -> 27.2 us (level)
  no operation moved by 1% of the time
where the time goes in v12:
time: 27.2 us; the launch traced here: 26.8 us
  Pallas kernels  12.3 us (45%)
  starting transfers between devices  10.8 us (40%)
  waiting for transfers between devices  1.84 us (7%)
  local copies, waits for them, and re-layouts  1.24 us (5%)
  between operations  0.66 us (2%)
    pallas_call x1, Pallas kernels, on_device(): pl.pallas_call(stencil_kernel, out_shape=(field, field), in_specs=[pl.Blo...  9.11 us
    ppermute x1, starting transfers between devices, on_device(): lax.ppermute(east_pack, 'lon', [((i + 1) % lon_count, i) for i in range(l...  4.22 us
    ppermute x1, starting transfers between devices, on_device(): second_got = lax.ppermute(second_lines, ('lon', 'lat'), second_pairs)  4.17 us
    pallas_call x1, Pallas kernels, on_device(): pl.pallas_call(edge_kernel, out_shape=(packed, packed, lines, lines), in_...  3.18 us
    ppermute x1, starting transfers between devices, on_device(): first_got = lax.ppermute(first_lines, ('lon', 'lat'), first_pairs)  1.91 us
    ppermute x1, waiting for transfers between devices, on_device(): lax.ppermute(west_pack, 'lon', [(i, (i + 1) % lon_count) for i in range(l...  1.83 us
    unnamed x8, local copies, waits for them, and re-layouts  1.24 us
  transfers between devices with their start and end apart: 4, of which 1 were waited for; matrix products, arithmetic and copies ran while one was open for 0% of the time, Pallas kernels for 0%

profile of v12, /device:TPU:2, one launch (start us, length us, event | category | flops | bytes accessed | tf_op | source)
XLA Modules:
  0.0 26.8 jit_solution(10839542957841207135)
XLA Ops:
  0.6 3.2 %shard_map.86 = (f32[16,128]{1,0:T(8,128)}, f32[16,128]{1,0:T(8,128)}, f32[76,256]{1,0:T(8,128)}, f32[76,256]{1,0:T(8,128)}) custom-call(f32[25,16,256]{2,1,0:T(8,128)} %t_ref.3, f32[25,16,256]{2,1,0:T(8,128)} %s_ref.3, f32[25,16,256]{2,1,0:T(8,128)} %u_ref.3, f32[25,16,256]{2,1,0:T(8,128)} %v_ref.3, s32[16,256]{1,0:T(8,128)} %wi_ref.3, s32[16,256]{1,0:T(8,128)} %sb_ref.3), custom_call_target="tpu_custom_call" | custom-call | tf_op jit(solution)/shard_map/pallas_call | solution.py:300
  3.8 1.9 %collective-permute-start.2 = (f32[76,256]{1,0:T(8,128)}, f32[76,256]{1,0:T(8,128)S(1)}, u32[]{:S(2)}, u32[]{:S(2)}) collective-permute-start(f32[76,256]{1,0:T(8,128)} %get-tuple-element.8), channel_id=1, source_target_pairs={{1,2},{2,1},{3,31},{5,6},{6,5},{7,27},{9,10},{10,9},{11,23},{13,14... | collective-permute-start | bytes 233480 | tf_op jit(solution)/shard_map/ppermute | solution.py:338
  5.7 4.2 %collective-permute-start.3 = (f32[76,256]{1,0:T(8,128)}, f32[76,256]{1,0:T(8,128)S(1)}, u32[]{:S(2)}, u32[]{:S(2)}) collective-permute-start(f32[76,256]{1,0:T(8,128)} %get-tuple-element.9), channel_id=1, source_target_pairs={{0,1},{1,0},{2,3},{3,2},{4,5},{5,4},{6,7},{7,6},{8,9},{9,8},{10,11... | collective-permute-start | bytes 233480 | tf_op jit(solution)/shard_map/ppermute | solution.py:339
  9.9 0.5 %collective-permute-start = (f32[16,128]{1,0:T(8,128)}, f32[16,128]{1,0:T(8,128)S(1)}, u32[]{:S(2)}, u32[]{:S(2)}) collective-permute-start(f32[16,128]{1,0:T(8,128)} %get-tuple-element.6), channel_id=1, source_target_pairs={{0,4},{4,8},{8,12},{12,16},{16,20},{20,24},{24,28},{28,0},{1,5},{5... | collective-permute-start | bytes 24584 | tf_op jit(solution)/shard_map/ppermute | solution.py:318
  10.4 4.2 %collective-permute-start.1 = (f32[16,128]{1,0:T(8,128)}, f32[16,128]{1,0:T(8,128)S(1)}, u32[]{:S(2)}, u32[]{:S(2)}) collective-permute-start(f32[16,128]{1,0:T(8,128)} %get-tuple-element.7), channel_id=1, source_target_pairs={{4,0},{8,4},{12,8},{16,12},{20,16},{24,20},{28,24},{0,28},{5,1},{9... | collective-permute-start | bytes 24584 | tf_op jit(solution)/shard_map/ppermute | solution.py:321
  14.6 1.8 %collective-permute-done.hw_ref = f32[16,128]{1,0:T(8,128)S(1)} collective-permute-done((f32[16,128]{1,0:T(8,128)}, f32[16,128]{1,0:T(8,128)S(1)}, u32[]{:S(2)}, u32[]{:S(2)}) %collective-permute-start) | collective-permute-done | bytes 8224 | tf_op jit(solution)/shard_map/ppermute | solution.py:318
  16.4 0.0 copy-start.2
  16.5 0.0 collective-permute-done.1.he_ref
  16.5 0.0 copy-start.3
  16.5 0.0 collective-permute-done.2.first_ref
  16.5 0.0 copy-start
  16.5 0.0 collective-permute-done.3.second_ref
  16.5 0.6 %copy-done.2 = f32[16,128]{1,0:T(8,128)} copy-done((f32[16,128]{1,0:T(8,128)}, f32[16,128]{1,0:T(8,128)S(1)}, u32[]{:S(2)}) %copy-start.2) | copy-done | bytes 8216
  17.0 0.0 copy-done.3
  17.1 0.0 copy-done
  17.1 0.0 copy-start.1
  17.1 0.6 %copy-done.1 = f32[76,256]{1,0:T(8,128)} copy-done((f32[76,256]{1,0:T(8,128)}, f32[76,256]{1,0:T(8,128)S(1)}, u32[]{:S(2)}) %copy-start.1) | copy-done | bytes 77848
  17.7 9.1 %shard_map.87 = (f32[25,16,256]{2,1,0:T(8,128)}, f32[25,16,256]{2,1,0:T(8,128)}) custom-call(f32[25,16,256]{2,1,0:T(8,128)} %t_ref.3, f32[25,16,256]{2,1,0:T(8,128)} %s_ref.3, f32[25,16,256]{2,1,0:T(8,128)} %u_ref.3, f32[25,16,256]{2,1,0:T(8,128)} %v_ref.3, f32[25,16,256]{2,1,0:T(8,128)} %w_ref.1, s32[16,256]{1,0:T(8,128)} %wi_ref.3, s32[16,256]{1,0:T(8,128)} %sb_ref.3, ...), custom_call_target="tpu_custom_call" | custom-call | tf_op jit(solution)/shard_map/pallas_call | solution.py:341
Async XLA Ops:
  3.8 12.7 %collective-permute-start.2 = (f32[76,256]{1,0:T(8,128)}, f32[76,256]{1,0:T(8,128)S(1)}, u32[]{:S(2)}, u32[]{:S(2)}) collective-permute-start(f32[76,256]{1,0:T(8,128)} %get-tuple-element.8), channel_id=1, source_target_pairs={{1,2},{2,1},{3,31},{5,6},{6,5},{7,27},{9,10},{10,9},{11,23},{13,14... | collective-permute-start | bytes 233480 | tf_op jit(solution)/shard_map/ppermute | solution.py:338
  5.7 10.8 %collective-permute-start.3 = (f32[76,256]{1,0:T(8,128)}, f32[76,256]{1,0:T(8,128)S(1)}, u32[]{:S(2)}, u32[]{:S(2)}) collective-permute-start(f32[76,256]{1,0:T(8,128)} %get-tuple-element.9), channel_id=1, source_target_pairs={{0,1},{1,0},{2,3},{3,2},{4,5},{5,4},{6,7},{7,6},{8,9},{9,8},{10,11... | collective-permute-start | bytes 233480 | tf_op jit(solution)/shard_map/ppermute | solution.py:339
  9.9 6.6 %collective-permute-start = (f32[16,128]{1,0:T(8,128)}, f32[16,128]{1,0:T(8,128)S(1)}, u32[]{:S(2)}, u32[]{:S(2)}) collective-permute-start(f32[16,128]{1,0:T(8,128)} %get-tuple-element.6), channel_id=1, source_target_pairs={{0,4},{4,8},{8,12},{12,16},{16,20},{20,24},{24,28},{28,0},{1,5},{5... | collective-permute-start | bytes 24584 | tf_op jit(solution)/shard_map/ppermute | solution.py:318
  10.4 6.1 %collective-permute-start.1 = (f32[16,128]{1,0:T(8,128)}, f32[16,128]{1,0:T(8,128)S(1)}, u32[]{:S(2)}, u32[]{:S(2)}) collective-permute-start(f32[16,128]{1,0:T(8,128)} %get-tuple-element.7), channel_id=1, source_target_pairs={{4,0},{8,4},{12,8},{16,12},{20,16},{24,20},{28,24},{0,28},{5,1},{9... | collective-permute-start | bytes 24584 | tf_op jit(solution)/shard_map/ppermute | solution.py:321
  16.4 0.6 %copy-start.2 = (f32[16,128]{1,0:T(8,128)}, f32[16,128]{1,0:T(8,128)S(1)}, u32[]{:S(2)}) copy-start(f32[16,128]{1,0:T(8,128)S(1)} %collective-permute-done.hw_ref) | copy-start | bytes 24580
  16.5 0.6 %copy-start.3 = (f32[16,128]{1,0:T(8,128)}, f32[16,128]{1,0:T(8,128)S(1)}, u32[]{:S(2)}) copy-start(f32[16,128]{1,0:T(8,128)S(1)} %collective-permute-done.1.he_ref) | copy-start | bytes 24580
  16.5 0.6 %copy-start = (f32[76,256]{1,0:T(8,128)}, f32[76,256]{1,0:T(8,128)S(1)}, u32[]{:S(2)}) copy-start(f32[76,256]{1,0:T(8,128)S(1)} %collective-permute-done.2.first_ref) | copy-start | bytes 233476
  17.1 0.6 %copy-start.1 = (f32[76,256]{1,0:T(8,128)}, f32[76,256]{1,0:T(8,128)S(1)}, u32[]{:S(2)}) copy-start(f32[76,256]{1,0:T(8,128)S(1)} %collective-permute-done.3.second_ref) | copy-start | bytes 233476

commit v13 on v10

--- a/solution.py
+++ b/solution.py
@@ -243,8 +243,14 @@
     west = jnp.zeros((rows, lane_tile), jnp.float32)
     east = jnp.zeros((rows, lane_tile), jnp.float32)
     for p, x in enumerate(column_planes):
-        west = jnp.where(lane == p, x[:, cols - 1 :], west)
-        east = jnp.where(lane == p, x[:, :1], east)
+        last = x[:, cols - lane_tile :]
+        first = x[:, :lane_tile]
+        if (p + 1) % lane_tile:
+            last = pltpu.roll(last, (p + 1) % lane_tile, 1)
+        if p % lane_tile:
+            first = pltpu.roll(first, p % lane_tile, 1)
+        west = jnp.where(lane == p, last, west)
+        east = jnp.where(lane == p, first, east)
     west_ref[...] = west
     east_ref[...] = east
     base_planes = 2 * layer_total + 1

time: 27.2 us -> 27 us (level)
  no operation moved by 1% of the time
where the time goes in v13:
time: 27 us; the launch traced here: 26.7 us
  Pallas kernels  12.1 us (45%)
  starting transfers between devices  10.8 us (40%)
  waiting for transfers between devices  1.84 us (7%)
  local copies, waits for them, and re-layouts  1.24 us (5%)
  between operations  0.66 us (2%)
    pallas_call x1, Pallas kernels, on_device(): pl.pallas_call(stencil_kernel, out_shape=(field, field), in_specs=[pl.Blo...  9.11 us
    ppermute x1, starting transfers between devices, on_device(): lax.ppermute(east_pack, 'lon', [((i + 1) % lon_count, i) for i in range(l...  4.22 us
    ppermute x1, starting transfers between devices, on_device(): second_got = lax.ppermute(second_lines, ('lon', 'lat'), second_pairs)  4.17 us
    pallas_call x1, Pallas kernels, on_device(): pl.pallas_call(edge_kernel, out_shape=(packed, packed, lines, lines), in_...  3.03 us
    ppermute x1, starting transfers between devices, on_device(): first_got = lax.ppermute(first_lines, ('lon', 'lat'), first_pairs)  1.91 us
    ppermute x1, waiting for transfers between devices, on_device(): lax.ppermute(west_pack, 'lon', [(i, (i + 1) % lon_count) for i in range(l...  1.83 us
    unnamed x8, local copies, waits for them, and re-layouts  1.24 us
  transfers between devices with their start and end apart: 4, of which 1 were waited for; matrix products, arithmetic and copies ran while one was open for 0% of the time, Pallas kernels for 0%

profile of v13, /device:TPU:2, one launch (start us, length us, event | category | flops | bytes accessed | tf_op | source)
XLA Modules:
  0.0 26.7 jit_solution(11555185620464664279)
XLA Ops:
  0.6 3.0 %shard_map.86 = (f32[16,128]{1,0:T(8,128)}, f32[16,128]{1,0:T(8,128)}, f32[76,256]{1,0:T(8,128)}, f32[76,256]{1,0:T(8,128)}) custom-call(f32[25,16,256]{2,1,0:T(8,128)} %t_ref.3, f32[25,16,256]{2,1,0:T(8,128)} %s_ref.3, f32[25,16,256]{2,1,0:T(8,128)} %u_ref.3, f32[25,16,256]{2,1,0:T(8,128)} %v_ref.3, s32[16,256]{1,0:T(8,128)} %wi_ref.3, s32[16,256]{1,0:T(8,128)} %sb_ref.3), custom_call_target="tpu_custom_call" | custom-call | tf_op jit(solution)/shard_map/pallas_call | solution.py:300
  3.7 1.9 %collective-permute-start.2 = (f32[76,256]{1,0:T(8,128)}, f32[76,256]{1,0:T(8,128)S(1)}, u32[]{:S(2)}, u32[]{:S(2)}) collective-permute-start(f32[76,256]{1,0:T(8,128)} %get-tuple-element.8), channel_id=1, source_target_pairs={{1,2},{2,1},{3,31},{5,6},{6,5},{7,27},{9,10},{10,9},{11,23},{13,14... | collective-permute-start | bytes 233480 | tf_op jit(solution)/shard_map/ppermute | solution.py:338
  5.6 4.2 %collective-permute-start.3 = (f32[76,256]{1,0:T(8,128)}, f32[76,256]{1,0:T(8,128)S(1)}, u32[]{:S(2)}, u32[]{:S(2)}) collective-permute-start(f32[76,256]{1,0:T(8,128)} %get-tuple-element.9), channel_id=1, source_target_pairs={{0,1},{1,0},{2,3},{3,2},{4,5},{5,4},{6,7},{7,6},{8,9},{9,8},{10,11... | collective-permute-start | bytes 233480 | tf_op jit(solution)/shard_map/ppermute | solution.py:339
  9.7 0.5 %collective-permute-start = (f32[16,128]{1,0:T(8,128)}, f32[16,128]{1,0:T(8,128)S(1)}, u32[]{:S(2)}, u32[]{:S(2)}) collective-permute-start(f32[16,128]{1,0:T(8,128)} %get-tuple-element.6), channel_id=1, source_target_pairs={{0,4},{4,8},{8,12},{12,16},{16,20},{20,24},{24,28},{28,0},{1,5},{5... | collective-permute-start | bytes 24584 | tf_op jit(solution)/shard_map/ppermute | solution.py:318
  10.2 4.2 %collective-permute-start.1 = (f32[16,128]{1,0:T(8,128)}, f32[16,128]{1,0:T(8,128)S(1)}, u32[]{:S(2)}, u32[]{:S(2)}) collective-permute-start(f32[16,128]{1,0:T(8,128)} %get-tuple-element.7), channel_id=1, source_target_pairs={{4,0},{8,4},{12,8},{16,12},{20,16},{24,20},{28,24},{0,28},{5,1},{9... | collective-permute-start | bytes 24584 | tf_op jit(solution)/shard_map/ppermute | solution.py:321
  14.5 1.8 %collective-permute-done.hw_ref = f32[16,128]{1,0:T(8,128)S(1)} collective-permute-done((f32[16,128]{1,0:T(8,128)}, f32[16,128]{1,0:T(8,128)S(1)}, u32[]{:S(2)}, u32[]{:S(2)}) %collective-permute-start) | collective-permute-done | bytes 8224 | tf_op jit(solution)/shard_map/ppermute | solution.py:318
  16.3 0.0 copy-start.2
  16.3 0.0 collective-permute-done.1.he_ref
  16.3 0.0 copy-start.3
  16.3 0.0 collective-permute-done.2.first_ref
  16.3 0.0 copy-start
  16.3 0.0 collective-permute-done.3.second_ref
  16.3 0.6 %copy-done.2 = f32[16,128]{1,0:T(8,128)} copy-done((f32[16,128]{1,0:T(8,128)}, f32[16,128]{1,0:T(8,128)S(1)}, u32[]{:S(2)}) %copy-start.2) | copy-done | bytes 8216
  16.9 0.0 copy-done.3
  16.9 0.0 copy-done
  16.9 0.0 copy-start.1
  16.9 0.6 %copy-done.1 = f32[76,256]{1,0:T(8,128)} copy-done((f32[76,256]{1,0:T(8,128)}, f32[76,256]{1,0:T(8,128)S(1)}, u32[]{:S(2)}) %copy-start.1) | copy-done | bytes 77848
  17.6 9.1 %shard_map.87 = (f32[25,16,256]{2,1,0:T(8,128)}, f32[25,16,256]{2,1,0:T(8,128)}) custom-call(f32[25,16,256]{2,1,0:T(8,128)} %t_ref.3, f32[25,16,256]{2,1,0:T(8,128)} %s_ref.3, f32[25,16,256]{2,1,0:T(8,128)} %u_ref.3, f32[25,16,256]{2,1,0:T(8,128)} %v_ref.3, f32[25,16,256]{2,1,0:T(8,128)} %w_ref.1, s32[16,256]{1,0:T(8,128)} %wi_ref.3, s32[16,256]{1,0:T(8,128)} %sb_ref.3, ...), custom_call_target="tpu_custom_call" | custom-call | tf_op jit(solution)/shard_map/pallas_call | solution.py:341
Async XLA Ops:
  3.7 12.7 %collective-permute-start.2 = (f32[76,256]{1,0:T(8,128)}, f32[76,256]{1,0:T(8,128)S(1)}, u32[]{:S(2)}, u32[]{:S(2)}) collective-permute-start(f32[76,256]{1,0:T(8,128)} %get-tuple-element.8), channel_id=1, source_target_pairs={{1,2},{2,1},{3,31},{5,6},{6,5},{7,27},{9,10},{10,9},{11,23},{13,14... | collective-permute-start | bytes 233480 | tf_op jit(solution)/shard_map/ppermute | solution.py:338
  5.6 10.8 %collective-permute-start.3 = (f32[76,256]{1,0:T(8,128)}, f32[76,256]{1,0:T(8,128)S(1)}, u32[]{:S(2)}, u32[]{:S(2)}) collective-permute-start(f32[76,256]{1,0:T(8,128)} %get-tuple-element.9), channel_id=1, source_target_pairs={{0,1},{1,0},{2,3},{3,2},{4,5},{5,4},{6,7},{7,6},{8,9},{9,8},{10,11... | collective-permute-start | bytes 233480 | tf_op jit(solution)/shard_map/ppermute | solution.py:339
  9.7 6.6 %collective-permute-start = (f32[16,128]{1,0:T(8,128)}, f32[16,128]{1,0:T(8,128)S(1)}, u32[]{:S(2)}, u32[]{:S(2)}) collective-permute-start(f32[16,128]{1,0:T(8,128)} %get-tuple-element.6), channel_id=1, source_target_pairs={{0,4},{4,8},{8,12},{12,16},{16,20},{20,24},{24,28},{28,0},{1,5},{5... | collective-permute-start | bytes 24584 | tf_op jit(solution)/shard_map/ppermute | solution.py:318
  10.2 6.1 %collective-permute-start.1 = (f32[16,128]{1,0:T(8,128)}, f32[16,128]{1,0:T(8,128)S(1)}, u32[]{:S(2)}, u32[]{:S(2)}) collective-permute-start(f32[16,128]{1,0:T(8,128)} %get-tuple-element.7), channel_id=1, source_target_pairs={{4,0},{8,4},{12,8},{16,12},{20,16},{24,20},{28,24},{0,28},{5,1},{9... | collective-permute-start | bytes 24584 | tf_op jit(solution)/shard_map/ppermute | solution.py:321
  16.3 0.6 %copy-start.2 = (f32[16,128]{1,0:T(8,128)}, f32[16,128]{1,0:T(8,128)S(1)}, u32[]{:S(2)}) copy-start(f32[16,128]{1,0:T(8,128)S(1)} %collective-permute-done.hw_ref) | copy-start | bytes 24580
  16.3 0.6 %copy-start.3 = (f32[16,128]{1,0:T(8,128)}, f32[16,128]{1,0:T(8,128)S(1)}, u32[]{:S(2)}) copy-start(f32[16,128]{1,0:T(8,128)S(1)} %collective-permute-done.1.he_ref) | copy-start | bytes 24580
  16.3 0.6 %copy-start = (f32[76,256]{1,0:T(8,128)}, f32[76,256]{1,0:T(8,128)S(1)}, u32[]{:S(2)}) copy-start(f32[76,256]{1,0:T(8,128)S(1)} %collective-permute-done.2.first_ref) | copy-start | bytes 233476
  16.9 0.6 %copy-start.1 = (f32[76,256]{1,0:T(8,128)}, f32[76,256]{1,0:T(8,128)S(1)}, u32[]{:S(2)}) copy-start(f32[76,256]{1,0:T(8,128)S(1)} %collective-permute-done.3.second_ref) | copy-start | bytes 233476
